TPU v7x, 128 devices: a whole 4x4x4 slice. The times are simulated.
128 devices in a mesh: req: 32 (over x, z, core), head: 4 (over y).
Axes of the slice: x: 4, y: 4, z: 4, core: 2. Of those that a mesh axis runs over, the one named last changes fastest.
Arguments:
- tokens: bfloat16 [32768, 1536], P(('req', 'head')), may hold values from -6 to 6
- norm1_gain: float32 [1536], replicated, may hold values from 0.1 to 1.9
- query_key_value_weight: bfloat16 [1536, 2048], replicated, may hold values from -0.15625 to 0.15625
- w_out: bfloat16 [1536, 1536], replicated, may hold values from -0.15625 to 0.15625
- norm2_gain: float32 [1536], replicated, may hold values from 0.1 to 1.9
- router_weight: float32 [1536, 32], replicated, may hold values from -0.078125 to 0.078125
- w_gate_up: bfloat16 [32, 1536, 1536], P('req'), may hold values from -0.15625 to 0.15625
- w_down: bfloat16 [32, 768, 1536], P('req'), may hold values from -0.21875 to 0.21875
- routes: int32 [32768, 4], P(('req', 'head')), may hold values from 0 to 31, all different within a row; in each aligned block of 256 rows (0 to 255, 256 to 511, ...) at most 48 rows name the same one
- key_page_store: bfloat16 [1024, 128, 256], P('req'), may hold values from -100 to 100
- value_page_store: bfloat16 [1024, 128, 256], P('req'), may hold values from -6 to 6
- page_table: int32 [64, 16], P('req'), may hold values from 0 to 31, as said below
- cached_pages: int32 [64], replicated, may hold values from 0 to 16
- anchor: int32 [64], replicated, may hold values from 0 to 63, as said below
Outputs:
- mixed: bfloat16 [32768, 1536], P(('req', 'head'))
- appended: bfloat16 [32768, 512], P(('req', 'head'))
Inputs may be any that keep to these rules, and one draw needn't show every extreme that they name: `page_table`: row o lists the pages of request o of the previous placement, as page numbers of the pool of index o // 2 of req; the rows of one index of req use distinct pages; entries past cached_pages[o] are not part of the cache. A permutation. Either anchor[i] = i, or request i and request anchor[i] lie on two indices of req that differ only in the lowest bit and trade places with each other; an index of req gives and takes at most one request.
All inputs are finite; a program needn't handle non-finite values.
Results may differ from a plain program's by a relative error of at most 0.011.
Values may be sent and summed in bfloat16 or wider, within the bound.
No kernel may reach another device: no remote copies, remote signals or barrier semaphores. Data moves between devices by JAX's collectives and lax.ppermute only.
A program may use at most 128 MiB of HBM per device.

v0:
```python
import jax
import jax.numpy as jnp
from jax import lax
from jax.sharding import PartitionSpec as P

MODEL_WIDTH = 1536
QUERY_HEADS = 12
KEY_VALUE_HEADS = 2
HEAD_SIZE = 128
FE = 768
TOPK = 4
REQUEST_TOKENS = 512


EPS = 1e-06
THETA = 1000000.0


def swapped(value, axis, bit):
    mask = 2**bit
    pairs = [(source, source ^ mask) for source in range(lax.axis_size(axis))]
    return lax.ppermute(value, axis, pairs)


def rms_scale(values, gain_vector):
    mean_sq = jnp.mean(values * values, axis=-1, keepdims=True)
    return values * lax.rsqrt(mean_sq + EPS) * gain_vector


def apply_rotary(values, where_at):
    half_dim = values.shape[-1] // 2
    frequency = jnp.exp(
        -jnp.log(jnp.float32(THETA))
        * jnp.arange(half_dim, dtype=jnp.float32)
        * 2.0
        / values.shape[-1]
    )
    angles = where_at.astype(jnp.float32)[:, None] * frequency[None, :]
    cosine = jnp.cos(angles)[:, None, :]
    sines = jnp.sin(angles)[:, None, :]
    first_half = values[..., :half_dim]
    second = values[..., half_dim:]
    return jnp.concatenate(
        [first_half * cosine - second * sines, second * cosine + first_half * sines], axis=-1
    )


def position_of(row_ids, cached_pages, anchor, page_size):
    request = row_ids // REQUEST_TOKENS
    return cached_pages[anchor[request]] * page_size + row_ids % REQUEST_TOKENS


def attend(slot_rows, page_keys, page_values, page_count, group_heads):
    width_q = group_heads * HEAD_SIZE
    queries = slot_rows[:, :width_q].reshape(REQUEST_TOKENS * group_heads, HEAD_SIZE)
    span_keys = slot_rows[:, width_q : width_q + HEAD_SIZE]
    span_values = slot_rows[:, width_q + HEAD_SIZE :]
    scaling = HEAD_SIZE ** (-0.5)
    contract = (((1,), (1,)), ((), ()))
    scores = (
        lax.dot_general(queries, span_keys, contract, preferred_element_type=jnp.float32) * scaling
    )
    query_pos = jnp.arange(REQUEST_TOKENS * group_heads, dtype=jnp.int32) // group_heads
    key_pos = jnp.arange(REQUEST_TOKENS, dtype=jnp.int32)
    scores = jnp.where(key_pos[None, :] <= query_pos[:, None], scores, -jnp.inf)
    row_max = jnp.max(scores, axis=1, keepdims=True)
    weights = jnp.exp(scores - row_max)
    row_sum = jnp.sum(weights, axis=1, keepdims=True)
    weighted = jnp.dot(
        weights.astype(jnp.bfloat16), span_values, preferred_element_type=jnp.float32
    )

    def visit(page_index, carry):
        old_max, old_sum, old_weighted = carry
        page_scores = (
            lax.dot_general(
                queries, page_keys[page_index], contract, preferred_element_type=jnp.float32
            )
            * scaling
        )
        new_max = jnp.maximum(old_max, jnp.max(page_scores, axis=1, keepdims=True))
        factor = jnp.exp(old_max - new_max)
        page_weights = jnp.exp(page_scores - new_max)
        new_sum = old_sum * factor + jnp.sum(page_weights, axis=1, keepdims=True)
        new_weighted = old_weighted * factor + jnp.dot(
            page_weights.astype(jnp.bfloat16),
            page_values[page_index],
            preferred_element_type=jnp.float32,
        )
        return (new_max, new_sum, new_weighted)

    row_max, row_sum, weighted = lax.fori_loop(0, page_count, visit, (row_max, row_sum, weighted))
    return (weighted / row_sum).astype(jnp.bfloat16).reshape(REQUEST_TOKENS, width_q)


def on_device(
    tokens,
    norm1_gain,
    query_key_value_weight,
    w_out,
    norm2_gain,
    router_weight,
    w_gate_up,
    w_down,
    routes,
    key_page_store,
    value_page_store,
    page_table,
    cached_pages,
    anchor,
):
    req_index = lax.axis_index("req")
    head_index = lax.axis_index("head")
    count_of_heads = lax.axis_size("head")
    req_count = lax.axis_size("req")
    tokens_per_device = tokens.shape[0]
    req_dev = page_table.shape[0]
    page_size = key_page_store.shape[1]
    group_heads = QUERY_HEADS // count_of_heads
    key_value_share = count_of_heads // KEY_VALUE_HEADS
    kv_index = head_index // key_value_share
    width_q = group_heads * HEAD_SIZE
    row_width = width_q + 2 * HEAD_SIZE
    first_row = (req_index * count_of_heads + head_index) * tokens_per_device
    token_positions = position_of(
        first_row + jnp.arange(tokens_per_device, dtype=jnp.int32), cached_pages, anchor, page_size
    )
    normed = rms_scale(tokens.astype(jnp.float32), norm1_gain).astype(jnp.bfloat16)
    projected_rows = jnp.dot(normed, query_key_value_weight, preferred_element_type=jnp.float32)
    queries = apply_rotary(
        projected_rows[:, : QUERY_HEADS * HEAD_SIZE].reshape(
            tokens_per_device, QUERY_HEADS, HEAD_SIZE
        ),
        token_positions,
    ).astype(jnp.bfloat16)
    fresh_keys = apply_rotary(
        projected_rows[
            :, QUERY_HEADS * HEAD_SIZE : (QUERY_HEADS + KEY_VALUE_HEADS) * HEAD_SIZE
        ].reshape(tokens_per_device, KEY_VALUE_HEADS, HEAD_SIZE),
        token_positions,
    ).astype(jnp.bfloat16)
    fresh_values = (
        projected_rows[:, (QUERY_HEADS + KEY_VALUE_HEADS) * HEAD_SIZE :]
        .astype(jnp.bfloat16)
        .reshape(tokens_per_device, KEY_VALUE_HEADS, HEAD_SIZE)
    )
    appended = jnp.concatenate(
        [
            fresh_keys.reshape(tokens_per_device, KEY_VALUE_HEADS * HEAD_SIZE),
            fresh_values.reshape(tokens_per_device, KEY_VALUE_HEADS * HEAD_SIZE),
        ],
        axis=1,
    )
    outgoing = jnp.concatenate(
        [
            queries.reshape(tokens_per_device, count_of_heads, width_q),
            jnp.repeat(fresh_keys, key_value_share, axis=1),
            jnp.repeat(fresh_values, key_value_share, axis=1),
        ],
        axis=2,
    )
    arrived = lax.all_to_all(outgoing, "head", split_axis=1, concat_axis=0, tiled=True)
    head_rows = arrived.reshape(req_dev * REQUEST_TOKENS, row_width)
    k_local = lax.dynamic_slice_in_dim(key_page_store, kv_index * HEAD_SIZE, HEAD_SIZE, 2)
    v_local = lax.dynamic_slice_in_dim(value_page_store, kv_index * HEAD_SIZE, HEAD_SIZE, 2)
    partner = req_index ^ 1
    partner_anchor = lax.dynamic_slice_in_dim(anchor, partner * req_dev, req_dev, 0)
    leaving = partner_anchor // req_dev == req_index
    out_request = jnp.sum(jnp.where(leaving, partner_anchor, 0))
    out_row = out_request % req_dev

    def pages_of(table_row):
        page_numbers = page_table[table_row]
        return (jnp.take(k_local, page_numbers, axis=0), jnp.take(v_local, page_numbers, axis=0))

    slot_blocks = [
        head_rows[slot_index * REQUEST_TOKENS : (slot_index + 1) * REQUEST_TOKENS]
        for slot_index in range(req_dev)
    ]
    slot_anchor = [anchor[req_index * req_dev + slot_index] for slot_index in range(req_dev)]
    moved_in = [slot_anchor[slot_index] // req_dev != req_index for slot_index in range(req_dev)]
    answers = []
    sent_k, sent_v = pages_of(out_row)
    got_k, got_v = swapped((sent_k, sent_v), "req", 0)
    for slot_index in range(req_dev):
        own_k, own_v = pages_of(slot_anchor[slot_index] % req_dev)
        use_k = jnp.where(moved_in[slot_index], got_k, own_k)
        use_v = jnp.where(moved_in[slot_index], got_v, own_v)
        answers.append(
            attend(
                slot_blocks[slot_index],
                use_k,
                use_v,
                cached_pages[slot_anchor[slot_index]],
                group_heads,
            )
        )
    attn_all = jnp.concatenate(answers, axis=0).reshape(count_of_heads, tokens_per_device, width_q)
    back_rows = lax.all_to_all(attn_all, "head", split_axis=0, concat_axis=2, tiled=True).reshape(
        tokens_per_device, QUERY_HEADS * HEAD_SIZE
    )
    residual = tokens.astype(jnp.float32) + jnp.dot(
        back_rows, w_out, preferred_element_type=jnp.float32
    )
    normed_moe = rms_scale(residual, norm2_gain).astype(jnp.bfloat16)
    logits = jnp.dot(normed_moe.astype(jnp.float32), router_weight, precision=lax.Precision.HIGHEST)
    chosen = jnp.take_along_axis(logits, routes, axis=1)
    sigmoids = jax.nn.sigmoid(chosen)
    route_gates = sigmoids / jnp.sum(sigmoids, axis=1, keepdims=True)
    exp_dev = w_gate_up.shape[0]
    expert_total = exp_dev * req_count
    capacity = max(2, 3 * tokens_per_device * TOPK // (2 * expert_total))
    flat_ids = routes.reshape(-1)
    one_hot = (flat_ids[:, None] == jnp.arange(expert_total, dtype=jnp.int32)[None, :]).astype(
        jnp.int32
    )
    slot_ranks = jnp.sum(jnp.cumsum(one_hot, axis=0) * one_hot, axis=1) - 1
    slot_ids = flat_ids * capacity + slot_ranks
    route_rows = flat_ids.shape[0]
    slot_token = (
        jnp.zeros((expert_total * capacity,), jnp.int32)
        .at[slot_ids]
        .set(jnp.arange(route_rows, dtype=jnp.int32) // TOPK)
    )
    slot_live = jnp.zeros((expert_total * capacity,), jnp.bool_).at[slot_ids].set(True)
    dispatch = jnp.where(
        slot_live[:, None], jnp.take(normed_moe, slot_token, axis=0), jnp.zeros((), jnp.bfloat16)
    )
    dispatch = dispatch.reshape(req_count, exp_dev, capacity, MODEL_WIDTH)
    gate_up = jnp.einsum(
        "nekd,edf->nekf",
        lax.all_to_all(dispatch, "req", split_axis=0, concat_axis=0, tiled=True),
        w_gate_up,
        preferred_element_type=jnp.float32,
    )
    hidden = (jax.nn.relu(gate_up[..., :FE]) * gate_up[..., FE:]).astype(jnp.bfloat16)
    result = jnp.einsum(
        "nekf,efd->nekd", hidden, w_down, preferred_element_type=jnp.float32
    ).astype(jnp.bfloat16)
    results = lax.all_to_all(result, "req", split_axis=0, concat_axis=0, tiled=True)
    flat_results = results.reshape(expert_total * capacity, MODEL_WIDTH)
    picked = jnp.take(flat_results, slot_ids, axis=0).reshape(tokens_per_device, TOPK, MODEL_WIDTH)
    expert_sum = jnp.zeros((tokens_per_device, MODEL_WIDTH), jnp.float32)
    for route_index in range(TOPK):
        expert_sum = expert_sum + route_gates[:, route_index : route_index + 1] * picked[
            :, route_index
        ].astype(jnp.float32)
    mixed_out = (residual + expert_sum).astype(jnp.bfloat16)
    return (mixed_out, appended)


def solution(mesh):
    return jax.shard_map(
        on_device,
        mesh=mesh,
        in_specs=(
            P(("req", "head"), None),
            P(),
            P(),
            P(),
            P(),
            P(),
            P("req", None, None),
            P("req", None, None),
            P(("req", "head"), None),
            P("req", None, None),
            P("req", None, None),
            P("req", None),
            P(),
            P(),
        ),
        out_specs=(P(("req", "head"), None), P(("req", "head"), None)),
        check_vma=False,
    )
```

profile of v0, /device:TPU:56, one launch (start us, length us, event | category | flops | bytes accessed | tf_op | source)
XLA Modules:
  0.0 417.2 jit_solution(10360244788630973997)
XLA Ops:
  2.2 4.9 %fusion.49 = f32[256,2048]{1,0:T(8,128)S(1)} fusion(bf16[1536,2048]{1,0:T(8,128)(2,1)} %param.22, bf16[256,1536]{1,0:T(8,128)(2,1)} %param.20, f32[1536]{0:T(1024)} %param.21, f32[256]{0:T(256)S(1)} %add_rsqrt_fusion.1), kind=kOutput, calls=%fused_computation.90 | convolution fusion | flops 1612185600 | bytes 9182208 | tf_op jit(solution)/shard_map/dot_general | solution.py:129
  14.9 3.0 copy.77
  23.9 4.7 %all-to-all-start = ((bf16[256,4,640]{0,2,1:T(8,128)(2,1)}), bf16[256,4,640]{0,2,1:T(8,128)(2,1)}, u32[]{:S(2)}, u32[]{:S(2)}) async-start(bf16[256,4,640]{0,2,1:T(8,128)(2,1)} %pad_maximum_fusion), calls=%async_computation | async-start | bytes 2621440 | tf_op jit(solution)/shard_map/all_to_all | solution.py:162
  36.1 2.7 constant_dynamic-slice_fusion.1
  38.8 2.6 gather_fusion.7
  49.1 2.7 gather_fusion.10
  58.8 9.0 %reduce-window.6 = s32[32,8,128]{2,1,0:T(8,128)S(1)} reduce-window(s32[32,8,128]{2,1,0:T(8,128)S(1)} %fusion.59, s32[]{:T(128)} %constant.209.clone.1), window={size=1x1x128 pad=0_0x0_0x127_0}, to_apply=%region_16.18 | reduce-window | flops 4161536 | bytes 262148 | tf_op jit(solution)/shard_map/reduce-window
  70.1 3.5 select_select_fusion.4
  93.3 16.2 %while.29 = (s32[]{:T(128)}, f32[1536,1]{0,1:T(1,128)S(1)}, f32[1536,1]{0,1:T(1,128)}, f32[1536,128]{1,0:T(8,128)}, s32[]{:T(128)}, /*index=5*/bf16[16,128,128]{...) while((s32[]{:T(128)}, f32[1536,1]{0,1:T(1,128)S(1)}, ...), condition=%wide.region_13.15_spmd, body=%wide.region_10.14_spmd.sunk | while | flops 102240768 | bytes 4544727 | solution.py:92
  118.1 4.8 %all-to-all-start.1 = ((bf16[4,256,384]{2,1,0:T(8,128)(2,1)}), bf16[4,256,384]{2,1,0:T(8,128)(2,1)S(1)}, u32[]{:S(2)}, u32[]{:S(2)}) async-start(bf16[4,256,384]{2,1,0:T(8,128)(2,1)} %bitcast.160), calls=%async_computation.1 | async-start | bytes 1572864 | tf_op jit(solution)/shard_map/all_to_all | solution.py:199
  122.9 4.5 %scatter_custom_fusion = pred[1536]{0:T(1024)(128)(4,1)S(1)} fusion(s32[1024]{0:T(1024)} %bitcast.176, pred[1024]{0:T(1024)(128)(4,1)S(1)} %broadcast.431, pred[]{:T(512)} %constant.238.clone.1), kind=kCustom, calls=%fused_computation.161 | custom fusion | bytes 2048 | tf_op jit(solution)/shard_map/scatter | solution.py:225
  127.4 4.5 %scatter_custom_fusion.1 = s32[1536]{0:T(1024)S(1)} fusion(s32[1024]{0:T(1024)} %bitcast.177, s32[1024]{0:T(1024)S(1)} %add_select_fusion.1, s32[]{:T(128)} %constant.209.clone.1), kind=kCustom, calls=%fused_computation.157 | custom fusion | bytes 6656 | tf_op jit(solution)/shard_map/scatter | solution.py:223
  134.3 4.0 multiply_reduce_fusion
  139.8 6.2 %gather_fusion.2 = bf16[1536,1536]{1,0:T(8,128)(2,1)} fusion(bf16[256,1536]{1,0:T(8,128)(2,1)S(1)} %multiply_convert_fusion, s32[2048]{0:T(1024)S(1)} %pad_clamp_fusion), kind=kCustom, calls=%fused_computation.8 | custom fusion | bytes 9443328 | tf_op jit(solution)/shard_map/jit(_take)/gather | solution.py:227
  146.0 2.8 select_select_fusion
  148.7 163.8 %all_to_all.40 = bf16[32,1,48,1536]{3,2,1,0:T(8,128)(2,1)S(1)} all-to-all(bf16[32,1,48,1536]{3,2,1,0:T(8,128)(2,1)S(1)} %select_select_fusion), channel_id=1, replica_groups=mesh['req'=32,'head'=4] {'req'}, dimensions={0} | all-to-all | bytes 9437184 | tf_op jit(solution)/shard_map/all_to_all | solution.py:232
  312.6 9.7 %convolution_bitcast_fusion = f32[32,1,48,1536]{3,2,0,1:T(8,128)S(1)} fusion(bf16[1,1536,1536]{2,1,0:T(8,128)(2,1)} %param.26, bf16[32,1,48,1536]{3,2,1,0:T(8,128)(2,1)S(1)} %all_to_all.40), kind=kOutput, calls=%fused_computation.45 | convolution fusion | flops 7247757312 | bytes 18874368 | tf_op jit(solution)/shard_map/nekd,edf->nekf/dot_general | solution.py:230
  322.3 5.5 %convert_bitcast_fusion = bf16[32,1,48,1536]{3,2,1,0:T(8,128)(2,1)} fusion(f32[32,1,48,1536]{3,2,0,1:T(8,128)S(1)} %convolution_bitcast_fusion, bf16[1,768,1536]{2,1,0:T(8,128)(2,1)S(1)} %copy-done), kind=kOutput, calls=%fused_computation.51 | convolution fusion | flops 3629776896 | bytes 16515072 | tf_op jit(solution)/shard_map/nekf,efd->nekd/dot_general | solution.py:237
  327.8 5.9 %all-to-all-start.3 = ((bf16[32,1,48,1536]{3,2,1,0:T(8,128)(2,1)}), bf16[32,1,48,1536]{3,2,1,0:T(8,128)(2,1)}, u32[]{:S(2)}, u32[]{:S(2)}) async-start(bf16[32,1,48,1536]{3,2,1,0:T(8,128)(2,1)} %convert_bitcast_fusion), calls=%async_computation.3 | async-start | bytes 9437184 | tf_op jit(solution)/shard_map/all_to_all | solution.py:240
  335.8 8.6 %gather_fusion.4 = f32[1024]{0:T(1024)S(1)} fusion(f32[256,32]{0,1:T(8,128)S(1)} %fusion.86, s32[1024]{0:T(1024)S(1)} %reshape.472), kind=kCustom, calls=%fused_computation.10 | custom fusion | bytes 16384 | tf_op jit(solution)/shard_map/jit(take_along_axis)/gather | solution.py:207
  344.7 51.3 %all-to-all-done.3 = bf16[32,1,48,1536]{3,2,1,0:T(8,128)(2,1)} async-done(((bf16[32,1,48,1536]{3,2,1,0:T(8,128)(2,1)}), bf16[32,1,48,1536]{3,2,1,0:T(8,128)(2,1)}, u32[]{:S(2)}, u32[]{:S(2)}) %all-to-all-start.3) | async-done | bytes 4718624 | tf_op jit(solution)/shard_map/all_to_all | solution.py:240
  396.1 10.2 %gather_fusion.3 = bf16[1024,1536]{1,0:T(8,128)(2,1)} fusion(bf16[1536,1536]{1,0:T(8,128)(2,1)} %bitcast.51, s32[1024]{0:T(1024)S(1)} %broadcast_clamp_fusion), kind=kCustom, calls=%fused_computation.9 | custom fusion | bytes 6295552 | tf_op jit(solution)/shard_map/jit(_take)/gather | solution.py:242
  406.3 6.1 %gather.34 = bf16[256,4,1536]{2,1,0:T(4,128)(2,1)} reshape(bf16[1024,1536]{1,0:T(8,128)(2,1)} %gather_fusion.3) | data formatting | bytes 6291456 | tf_op jit(solution)/shard_map/jit(_take)/gather | solution.py:242
  412.4 3.1 copy_select_fusion
  (183 shorter events, 79.8 us)
Async XLA Ops:
  0.6 321.7 %copy-start = (bf16[1,768,1536]{2,1,0:T(8,128)(2,1)S(1)}, bf16[1,768,1536]{2,1,0:T(8,128)(2,1)}, u32[]{:S(2)}) copy-start(bf16[1,768,1536]{2,1,0:T(8,128)(2,1)} %param.27) | copy-start | bytes 7077892
  7.1 4.0 copy-start.3
  7.2 7.7 %copy-start.10 = (bf16[256,256]{1,0:T(8,128)(2,1)}, bf16[256,256]{1,0:T(8,128)(2,1)S(1)}, u32[]{:S(2)}) copy-start(bf16[256,256]{1,0:T(8,128)(2,1)S(1)} %slice.207) | copy-start | bytes 393220
  22.7 12.8 %copy-start.22 = (s32[2,16]{1,0:T(2,128)S(1)}, s32[2,16]{1,0:T(2,128)}, u32[]{:S(2)}) copy-start(s32[2,16]{1,0:T(2,128)} %param.31) | copy-start | bytes 388
  23.9 49.7 %all-to-all-start = ((bf16[256,4,640]{0,2,1:T(8,128)(2,1)}), bf16[256,4,640]{0,2,1:T(8,128)(2,1)}, u32[]{:S(2)}, u32[]{:S(2)}) async-start(bf16[256,4,640]{0,2,1:T(8,128)(2,1)} %pad_maximum_fusion), calls=%async_computation | async-start | bytes 2621440 | tf_op jit(solution)/shard_map/all_to_all | solution.py:162
  38.8 9.3 %copy-start.15 = (s32[256,4]{0,1:T(4,128)S(1)}, s32[256,4]{0,1:T(4,128)}, u32[]{:S(2)}) copy-start(s32[256,4]{0,1:T(4,128)} %param.28) | copy-start | bytes 12292
  45.2 24.9 %collective-permute-start.1 = (bf16[16,128,128]{2,1,0:T(8,128)(2,1)}, bf16[16,128,128]{2,1,0:T(8,128)(2,1)}, u32[]{:S(2)}, u32[]{:S(2)}) collective-permute-start(bf16[16,128,128]{2,1,0:T(8,128)(2,1)} %get-tuple-element.171), channel_id=1, source_target_pairs={{0,4},{4,0},{8,12},{12,8},{16,20},{20,16},{24,28},{28,24},{32,36},... | collective-permute-start | bytes 1572872 | tf_op jit(solution)/shard_map/ppermute | solution.py:22
  45.2 24.9 %collective-permute-start = (bf16[16,128,128]{2,1,0:T(8,128)(2,1)}, bf16[16,128,128]{2,1,0:T(8,128)(2,1)}, u32[]{:S(2)}, u32[]{:S(2)}) collective-permute-start(bf16[16,128,128]{2,1,0:T(8,128)(2,1)} %get-tuple-element.172), channel_id=1, source_target_pairs={{0,4},{4,0},{8,12},{12,8},{16,20},{20,16},{24,28},{28,24},{32,36},... | collective-permute-start | bytes 1572872 | tf_op jit(solution)/shard_map/ppermute | solution.py:22
  81.0 2.8 copy-start.6
  90.1 2.7 copy-start.19
  94.0 3.9 copy-start.12
  99.2 3.9 copy-start.12
  104.4 3.9 copy-start.12
  118.1 14.0 %all-to-all-start.1 = ((bf16[4,256,384]{2,1,0:T(8,128)(2,1)}), bf16[4,256,384]{2,1,0:T(8,128)(2,1)S(1)}, u32[]{:S(2)}, u32[]{:S(2)}) async-start(bf16[4,256,384]{2,1,0:T(8,128)(2,1)} %bitcast.160), calls=%async_computation.1 | async-start | bytes 1572864 | tf_op jit(solution)/shard_map/all_to_all | solution.py:199
  134.3 5.2 %copy-start.21 = (f32[1536]{0:T(1024)S(1)}, f32[1536]{0:T(1024)}, u32[]{:S(2)}) copy-start(f32[1536]{0:T(1024)} %param.24) | copy-start | bytes 18436
  327.8 5.9 %copy-start.18 = (s32[1024]{0:T(1024)S(1)}, s32[1024]{0:T(1024)}, u32[]{:S(2)}) copy-start(s32[1024]{0:T(1024)} %copy-done.17) | copy-start | bytes 12292
  327.8 6.1 %copy-start.16 = (s32[256,4]{0,1:T(4,128)S(1)}, s32[256,4]{0,1:T(4,128)}, u32[]{:S(2)}) copy-start(s32[256,4]{0,1:T(4,128)} %param.28) | copy-start | bytes 12292
  327.8 6.4 %copy-start.9 = (bf16[256,2,128]{2,1,0:T(2,128)(2,1)S(1)}, bf16[256,2,128]{2,1,0:T(2,128)(2,1)}, u32[]{:S(2)}) copy-start(bf16[256,2,128]{2,1,0:T(2,128)(2,1)} %copy-done.8) | copy-start | bytes 393220
  327.8 6.5 %copy-start.11 = (bf16[256,256]{1,0:T(8,128)(2,1)S(1)}, bf16[256,256]{1,0:T(8,128)(2,1)}, u32[]{:S(2)}) copy-start(bf16[256,256]{1,0:T(8,128)(2,1)} %copy-done.10) | copy-start | bytes 393220
  327.8 7.2 %copy-start.20 = (s32[1024,1]{0,1:T(1,128)S(1)}, s32[1024,1]{0,1:T(1,128)}, u32[]{:S(2)}) copy-start(s32[1024,1]{0,1:T(1,128)} %compare_select_fusion) | copy-start | bytes 12292
  327.8 7.2 %copy-start.14 = (f32[1536,32]{0,1:T(8,128)S(1)}, f32[1536,32]{0,1:T(8,128)}, u32[]{:S(2)}) copy-start(f32[1536,32]{0,1:T(8,128)} %param.25) | copy-start | bytes 589828
  327.8 68.2 %all-to-all-start.3 = ((bf16[32,1,48,1536]{3,2,1,0:T(8,128)(2,1)}), bf16[32,1,48,1536]{3,2,1,0:T(8,128)(2,1)}, u32[]{:S(2)}, u32[]{:S(2)}) async-start(bf16[32,1,48,1536]{3,2,1,0:T(8,128)(2,1)} %convert_bitcast_fusion), calls=%async_computation.3 | async-start | bytes 9437184 | tf_op jit(solution)/shard_map/all_to_all | solution.py:240
  412.4 3.2 copy-start.5
  412.4 4.8 %copy-start.1 = (bf16[1,768,1536]{2,1,0:T(8,128)(2,1)S(1)}, bf16[1,768,1536]{2,1,0:T(8,128)(2,1)}, u32[]{:S(2)}) copy-start(bf16[1,768,1536]{2,1,0:T(8,128)(2,1)} %param.27) | copy-start | bytes 7077892
  (8 other events, 7.9 us)
where the time goes:
time: 421 us; the launch traced here: 417 us
  blocking collectives  164 us (39%)
  local copies, waits for them, and re-layouts  88.5 us (21%)
  waiting for transfers between devices  51.3 us (12%)
  matrix products  43.3 us (10%)
  other arithmetic  40.6 us (10%)
  starting transfers between devices  15.9 us (4%)
  between operations  10.4 us (2%)
    all_to_all x1, blocking collectives, on_device(): lax.all_to_all(dispatch, 'req', split_axis=0, concat_axis=0, tiled=True)  164 us
    all_to_all x1, waiting for transfers between devices, on_device(): lax.all_to_all(result, 'req', split_axis=0, concat_axis=0, tiled=True)  51.3 us
    gather x2, local copies, waits for them, and re-layouts, on_device(): jnp.take(flat_results, slot_ids, axis=0)  16.3 us
    another operation x4, other arithmetic  10.8 us
    dot_general x1, matrix products, on_device(): jnp.einsum('nekd,edf->nekf', lax.all_to_all(dispatch, 'req', split_axis=0...  9.72 us
    gather x5, local copies, waits for them, and re-layouts, on_device(): chosen = jnp.take_along_axis(logits, routes, axis=1)  9.1 us
  transfers between devices with their start and end apart: 5, of which 1 were waited for; matrix products, arithmetic and copies ran while one was open for 13% of the time, Pallas kernels for 0%

commit v1 on v0

v1 whole, which is shorter than its diff:
```python
import functools

import jax
import jax.numpy as jnp
from jax import lax
from jax.experimental import pallas as pl
from jax.experimental.pallas import tpu as pltpu
from jax.sharding import PartitionSpec as P

MODEL_WIDTH = 1536
QUERY_HEADS = 12
KEY_VALUE_HEADS = 2
HEAD_SIZE = 128
FE = 768
TOPK = 4
REQUEST_TOKENS = 512


EPS = 1e-06
THETA = 1000000.0


def rms_scale(values, gain_vector):
    mean_sq = jnp.mean(values * values, axis=-1, keepdims=True)
    return values * lax.rsqrt(mean_sq + EPS) * gain_vector


def apply_rotary(values, where_at):
    half_dim = values.shape[-1] // 2
    frequency = jnp.exp(
        -jnp.log(jnp.float32(THETA))
        * jnp.arange(half_dim, dtype=jnp.float32)
        * 2.0
        / values.shape[-1]
    )
    angles = where_at.astype(jnp.float32)[:, None] * frequency[None, :]
    cosine = jnp.cos(angles)[:, None, :]
    sines = jnp.sin(angles)[:, None, :]
    first_half = values[..., :half_dim]
    second = values[..., half_dim:]
    return jnp.concatenate(
        [first_half * cosine - second * sines, second * cosine + first_half * sines], axis=-1
    )


def attention_kernel(
    meta_ref, page_ref, q_ref, kn_ref, vn_ref, kl_ref, vl_ref, kr_ref, vr_ref,
    o_ref, m_sc, l_sc, acc_sc, *, group, tokens
):
    j = pl.program_id(1)
    count = meta_ref[0]
    moved = meta_ref[1]
    half = meta_ref[2]
    scaling = HEAD_SIZE ** (-0.5)
    contract = (((1,), (1,)), ((), ()))

    def stacked_queries():
        q = q_ref[...]
        return jnp.concatenate(
            [q[:, g * HEAD_SIZE : (g + 1) * HEAD_SIZE] for g in range(group)], axis=0
        )

    @pl.when(j == 0)
    def _():
        qa = stacked_queries()
        s = lax.dot_general(qa, kn_ref[...], contract, preferred_element_type=jnp.float32)
        s = s * scaling
        rows = group * tokens
        t = lax.broadcasted_iota(jnp.int32, (group, tokens, s.shape[1]), 1).reshape(rows, -1)
        v = lax.broadcasted_iota(jnp.int32, s.shape, 1)
        s = jnp.where(v <= t + half * tokens, s, -jnp.inf)
        m = jnp.max(s, axis=1, keepdims=True)
        p = jnp.exp(s - m)
        l_sc[...] = jnp.sum(p, axis=1, keepdims=True)
        m_sc[...] = m
        acc_sc[...] = jnp.dot(
            p.astype(jnp.bfloat16), vn_ref[...], preferred_element_type=jnp.float32
        )

    @pl.when((j > 0) & (j - 1 < count))
    def _():
        qa = stacked_queries()
        k = jnp.where(moved == 1, kr_ref[0], kl_ref[0])
        vv = jnp.where(moved == 1, vr_ref[0], vl_ref[0])
        s = lax.dot_general(qa, k, contract, preferred_element_type=jnp.float32) * scaling
        m_old = m_sc[...]
        m_new = jnp.maximum(m_old, jnp.max(s, axis=1, keepdims=True))
        factor = jnp.exp(m_old - m_new)
        p = jnp.exp(s - m_new)
        l_sc[...] = l_sc[...] * factor + jnp.sum(p, axis=1, keepdims=True)
        acc_sc[...] = acc_sc[...] * factor + jnp.dot(
            p.astype(jnp.bfloat16), vv, preferred_element_type=jnp.float32
        )
        m_sc[...] = m_new

    @pl.when(j == pl.num_programs(1) - 1)
    def _():
        res = acc_sc[...] / l_sc[...]
        o_ref[...] = jnp.concatenate(
            [res[g * tokens : (g + 1) * tokens] for g in range(group)], axis=1
        ).astype(jnp.bfloat16)


def attend(meta, page_ids, queries, new_keys, new_values, k_pool, v_pool, k_got, v_got):
    tokens = queries.shape[0]
    group = QUERY_HEADS // KEY_VALUE_HEADS
    width = group * HEAD_SIZE
    span = new_keys.shape[0]
    page_size = k_pool.shape[1]
    max_pages = page_ids.shape[0]

    def page_at(j, meta_ref):
        return jnp.maximum(jnp.minimum(j - 1, meta_ref[0] - 1), 0)

    def local_map(c, j, meta_ref, page_ref):
        return (page_ref[page_at(j, meta_ref)] * (1 - meta_ref[1]), 0, c)

    def got_map(c, j, meta_ref, page_ref):
        return (page_at(j, meta_ref) * meta_ref[1], 0, c)

    page_block = (1, page_size, HEAD_SIZE)
    grid_spec = pltpu.PrefetchScalarGridSpec(
        num_scalar_prefetch=2,
        grid=(KEY_VALUE_HEADS, max_pages + 1),
        in_specs=[
            pl.BlockSpec((tokens, width), lambda c, j, m, p: (0, c)),
            pl.BlockSpec((span, HEAD_SIZE), lambda c, j, m, p: (0, c)),
            pl.BlockSpec((span, HEAD_SIZE), lambda c, j, m, p: (0, c)),
            pl.BlockSpec(page_block, local_map),
            pl.BlockSpec(page_block, local_map),
            pl.BlockSpec(page_block, got_map),
            pl.BlockSpec(page_block, got_map),
        ],
        out_specs=pl.BlockSpec((tokens, width), lambda c, j, m, p: (0, c)),
        scratch_shapes=[
            pltpu.VMEM((group * tokens, 1), jnp.float32),
            pltpu.VMEM((group * tokens, 1), jnp.float32),
            pltpu.VMEM((group * tokens, HEAD_SIZE), jnp.float32),
        ],
    )
    return pl.pallas_call(
        functools.partial(attention_kernel, group=group, tokens=tokens),
        grid_spec=grid_spec,
        out_shape=jax.ShapeDtypeStruct((tokens, QUERY_HEADS * HEAD_SIZE), jnp.bfloat16),
        compiler_params=pltpu.CompilerParams(dimension_semantics=("arbitrary", "arbitrary")),
    )(meta, page_ids, queries, new_keys, new_values, k_pool, v_pool, k_got, v_got)


def on_device(
    tokens,
    norm1_gain,
    query_key_value_weight,
    w_out,
    norm2_gain,
    router_weight,
    w_gate_up,
    w_down,
    routes,
    key_page_store,
    value_page_store,
    page_table,
    cached_pages,
    anchor,
):
    req_index = lax.axis_index("req")
    head_index = lax.axis_index("head")
    count_of_heads = lax.axis_size("head")
    req_count = lax.axis_size("req")
    tokens_per_device = tokens.shape[0]
    req_dev = page_table.shape[0]
    page_size = key_page_store.shape[1]
    share = REQUEST_TOKENS // tokens_per_device
    kv_width = KEY_VALUE_HEADS * HEAD_SIZE

    request = (req_index * count_of_heads + head_index) // share
    half = head_index % share
    slot = request % req_dev
    old_id = anchor[request]
    place = half * tokens_per_device + jnp.arange(tokens_per_device, dtype=jnp.int32)
    token_positions = cached_pages[old_id] * page_size + place

    normed = rms_scale(tokens.astype(jnp.float32), norm1_gain).astype(jnp.bfloat16)
    projected_rows = jnp.dot(normed, query_key_value_weight, preferred_element_type=jnp.float32)
    queries = apply_rotary(
        projected_rows[:, : QUERY_HEADS * HEAD_SIZE].reshape(
            tokens_per_device, QUERY_HEADS, HEAD_SIZE
        ),
        token_positions,
    ).astype(jnp.bfloat16)
    fresh_keys = apply_rotary(
        projected_rows[
            :, QUERY_HEADS * HEAD_SIZE : (QUERY_HEADS + KEY_VALUE_HEADS) * HEAD_SIZE
        ].reshape(tokens_per_device, KEY_VALUE_HEADS, HEAD_SIZE),
        token_positions,
    ).astype(jnp.bfloat16)
    fresh_values = projected_rows[:, (QUERY_HEADS + KEY_VALUE_HEADS) * HEAD_SIZE :].astype(
        jnp.bfloat16
    )
    appended = jnp.concatenate(
        [fresh_keys.reshape(tokens_per_device, kv_width), fresh_values], axis=1
    )

    forward_pairs = [
        (h, h + 1) for h in range(count_of_heads) if h % share != share - 1
    ]
    earlier = lax.ppermute(appended, "head", forward_pairs)
    is_second = half == 1
    span_rows = jnp.where(
        is_second,
        jnp.concatenate([earlier, appended], axis=0),
        jnp.concatenate([appended, earlier], axis=0),
    )
    new_keys = span_rows[:, :kv_width]
    new_values = span_rows[:, kv_width:]

    partner = req_index ^ 1
    partner_anchor = lax.dynamic_slice_in_dim(anchor, partner * req_dev, req_dev, 0)
    leaving = partner_anchor // req_dev == req_index
    out_row = jnp.sum(jnp.where(leaving, partner_anchor, 0)) % req_dev
    sent_pages = page_table[out_row]
    sent = (
        jnp.take(key_page_store, sent_pages, axis=0),
        jnp.take(value_page_store, sent_pages, axis=0),
    )
    pairs = [(source, source ^ 1) for source in range(req_count)]
    k_got, v_got = lax.ppermute(sent, "req", pairs)

    moved_in = (old_id // req_dev != req_index).astype(jnp.int32)
    page_ids = page_table[old_id % req_dev]
    meta = jnp.stack([cached_pages[old_id], moved_in, half.astype(jnp.int32)]).astype(jnp.int32)
    attention = attend(
        meta, page_ids, queries.reshape(tokens_per_device, QUERY_HEADS * HEAD_SIZE),
        new_keys, new_values, key_page_store, value_page_store, k_got, v_got,
    )
    del slot

    residual = tokens.astype(jnp.float32) + jnp.dot(
        attention, w_out, preferred_element_type=jnp.float32
    )
    normed_moe = rms_scale(residual, norm2_gain).astype(jnp.bfloat16)
    logits = jnp.dot(normed_moe.astype(jnp.float32), router_weight, precision=lax.Precision.HIGHEST)
    chosen = jnp.take_along_axis(logits, routes, axis=1)
    sigmoids = jax.nn.sigmoid(chosen)
    route_gates = sigmoids / jnp.sum(sigmoids, axis=1, keepdims=True)

    exp_dev = w_gate_up.shape[0]
    expert_total = exp_dev * req_count
    capacity = max(2, 3 * tokens_per_device * TOPK // (2 * expert_total))
    slot_total = expert_total * capacity
    flat_ids = routes.reshape(-1)
    route_rows = flat_ids.shape[0]
    one_hot = (flat_ids[:, None] == jnp.arange(expert_total, dtype=jnp.int32)[None, :]).astype(
        jnp.bfloat16
    )
    row_i = lax.broadcasted_iota(jnp.int32, (route_rows, route_rows), 0)
    col_i = lax.broadcasted_iota(jnp.int32, (route_rows, route_rows), 1)
    before = (col_i < row_i).astype(jnp.bfloat16)
    earlier_counts = jnp.dot(before, one_hot, preferred_element_type=jnp.float32)
    slot_ranks = jnp.sum(earlier_counts * one_hot.astype(jnp.float32), axis=1).astype(jnp.int32)
    slot_ids = (flat_ids * capacity + slot_ranks).reshape(tokens_per_device, TOPK)

    slot_iota = jnp.arange(slot_total, dtype=jnp.int32)
    hits = slot_ids[None, :, :] == slot_iota[:, None, None]
    gather_matrix = jnp.any(hits, axis=2).astype(jnp.bfloat16)
    dispatch = jnp.dot(gather_matrix, normed_moe, preferred_element_type=jnp.float32).astype(
        jnp.bfloat16
    )
    dispatch = dispatch.reshape(req_count, exp_dev, capacity, MODEL_WIDTH)
    gate_up = jnp.einsum(
        "nekd,edf->nekf",
        lax.all_to_all(dispatch, "req", split_axis=0, concat_axis=0, tiled=True),
        w_gate_up,
        preferred_element_type=jnp.float32,
    )
    hidden = (jax.nn.relu(gate_up[..., :FE]) * gate_up[..., FE:]).astype(jnp.bfloat16)
    result = jnp.einsum(
        "nekf,efd->nekd", hidden, w_down, preferred_element_type=jnp.float32
    ).astype(jnp.bfloat16)
    results = lax.all_to_all(result, "req", split_axis=0, concat_axis=0, tiled=True)
    flat_results = results.reshape(slot_total, MODEL_WIDTH)

    token_hits = slot_ids[:, :, None] == slot_iota[None, None, :]
    combine = jnp.sum(jnp.where(token_hits, route_gates[:, :, None], 0.0), axis=1)
    combine_hi = combine.astype(jnp.bfloat16)
    combine_lo = (combine - combine_hi.astype(jnp.float32)).astype(jnp.bfloat16)
    expert_sum = jnp.dot(combine_hi, flat_results, preferred_element_type=jnp.float32) + jnp.dot(
        combine_lo, flat_results, preferred_element_type=jnp.float32
    )
    mixed_out = (residual + expert_sum).astype(jnp.bfloat16)
    return (mixed_out, appended)


def solution(mesh):
    return jax.shard_map(
        on_device,
        mesh=mesh,
        in_specs=(
            P(("req", "head"), None),
            P(),
            P(),
            P(),
            P(),
            P(),
            P("req", None, None),
            P("req", None, None),
            P(("req", "head"), None),
            P("req", None, None),
            P("req", None, None),
            P("req", None),
            P(),
            P(),
        ),
        out_specs=(P(("req", "head"), None), P(("req", "head"), None)),
        check_vma=False,
    )
```

time: 421 us -> 282 us (0.67)
  local copies, waits for them, and re-layouts: 88.5 us -> 26.2 us
  blocking collectives: 164 us -> 116 us
  other arithmetic: 40.6 us -> 16 us
  Pallas kernels: 0 us -> 20 us
  matrix products: 43.3 us -> 34.6 us
  starting transfers between devices: 15.9 us -> 7.66 us
    all_to_all x1, blocking collectives: 164 us -> 116 us  [on_device(): lax.all_to_all(dispatch, 'req', split_axis=0, concat_axis=0, tiled=True)]
    gather x11 -> x2, local copies, waits for them, and re-layouts: 38.5 us -> 5.41 us  [the longest x1 3.2 us: on_device(): jnp.take(key_page_store, sent_pages, axis=0)]
    pallas_call x0 -> x1, Pallas kernels: none -> 20 us  [attend(): pl.pallas_call(functools.partial(attention_kernel, group=group, tokens=to...]
    all_to_all x2 -> x0, starting transfers between devices: 9.48 us -> none  [the longest x1 4.8 us: on_device(): lax.all_to_all(attn_all, 'head', split_axis=0, concat_axis=2, tiled=True)]
    scatter x2 -> x0, local copies, waits for them, and re-layouts: 8.91 us -> none  [the longest x1 4.46 us: on_device(): jnp.zeros((expert_total * capacity,), jnp.bool_).at[slot_ids].set(True)]
    select_n x10 -> x2, other arithmetic: 12.4 us -> 4.41 us  [the longest x1 2.99 us: on_device(): jnp.take(value_page_store, sent_pages, axis=0)]
    slice x8 -> x1, local copies, waits for them, and re-layouts: 8.48 us -> 0.84 us  [on_device(): new_values = span_rows[:, kv_width:]]
    another operation x4 -> x3, other arithmetic: 10.8 us -> 4.02 us
  transfers between devices with their start and end apart: 5 -> 4, of which waited for: 1 -> 1; matrix products, arithmetic and copies ran while one was open for 13% -> 13% of each run, Pallas kernels for 0% -> 0%
where the time goes in v1:
time: 282 us; the launch traced here: 278 us
  blocking collectives  116 us (41%)
  waiting for transfers between devices  51.2 us (18%)
  matrix products  34.6 us (12%)
  local copies, waits for them, and re-layouts  26.2 us (9%)
  Pallas kernels  20 us (7%)
  other arithmetic  16 us (6%)
  starting transfers between devices  7.66 us (3%)
  between operations  7.22 us (3%)
    all_to_all x1, blocking collectives, on_device(): lax.all_to_all(dispatch, 'req', split_axis=0, concat_axis=0, tiled=True)  116 us
    all_to_all x1, waiting for transfers between devices, on_device(): lax.all_to_all(result, 'req', split_axis=0, concat_axis=0, tiled=True)  51.2 us
    pallas_call x1, Pallas kernels, attend(): pl.pallas_call(functools.partial(attention_kernel, group=group, tokens=to...  20 us
    gather x5, local copies, waits for them, and re-layouts, on_device(): chosen = jnp.take_along_axis(logits, routes, axis=1)  9.1 us
    dot_general x1, matrix products, on_device(): jnp.einsum('nekd,edf->nekf', lax.all_to_all(dispatch, 'req', split_axis=0...  7.51 us
    all_to_all x1, starting transfers between devices, on_device(): lax.all_to_all(result, 'req', split_axis=0, concat_axis=0, tiled=True)  5.87 us
    dot_general x1, matrix products, on_device(): jnp.dot(combine_lo, flat_results, preferred_element_type=jnp.float32)  5.76 us
  transfers between devices with their start and end apart: 4, of which 1 were waited for; matrix products, arithmetic and copies ran while one was open for 13% of the time, Pallas kernels for 0%

profile of v1, /device:TPU:56, one launch (start us, length us, event | category | flops | bytes accessed | tf_op | source)
XLA Modules:
  0.0 278.3 jit_solution(10835383625849819777)
XLA Ops:
  0.7 1.4 dynamic_slice.16
  3.2 1.4 fusion.11
  4.6 4.9 %fusion.16 = f32[256,2048]{1,0:T(8,128)S(1)} fusion(bf16[1536,2048]{1,0:T(8,128)(2,1)} %param.18, bf16[256,1536]{1,0:T(8,128)(2,1)} %param.16, f32[1536]{0:T(1024)} %param.17, f32[256]{0:T(256)S(1)} %add_rsqrt_fusion.1), kind=kOutput, calls=%fused_computation.36 | convolution fusion | flops 1612185600 | bytes 9182208 | tf_op jit(solution)/shard_map/dot_general | solution.py:183
  9.6 1.3 copy-done.5
  15.5 1.3 collective-permute-start
  19.8 2.2 gather_fusion.2
  22.0 3.2 %gather_fusion.1 = bf16[16,128,256]{2,1,0:T(8,128)(2,1)} fusion(bf16[32,128,256]{2,1,0:T(8,128)(2,1)} %kl_ref.1, s32[1024]{0:T(1024)S(1)} %pad_clamp_fusion), kind=kCustom, calls=%fused_computation.clone | custom fusion | bytes 2097216 | tf_op jit(solution)/shard_map/jit(_take)/gather | solution.py:222
  25.2 3.0 %broadcast_select_fusion = (bf16[16,128,256]{2,1,0:T(8,128)(2,1)}, bf16[16,128,256]{2,1,0:T(8,128)(2,1)}) fusion(bf16[16,128,256]{2,1,0:T(8,128)(2,1)S(1)} %gather_fusion.2, pred[16]{0:T(512)(128)(4,1)S(1)} %get-tuple-element.5, bf16[16,128,256]{2,1,0:T(8,128)(2,1)} %gather_fusion.1), kind=kLoop, calls=%fused_computation.34 | loop fusion | flops 1048576 | bytes 4194320 | tf_op jit(solution)/shard_map/jit(_take)/select_n | solution.py:223
  28.7 1.2 slice.51
  29.9 3.1 %copy.62 = f32[256,1536]{0,1:T(8,128)} copy(f32[256,1536]{1,0:T(8,128)} %slice.51) | data formatting | bytes 3145728 | tf_op jit(solution)/shard_map/slice | solution.py:185
  33.0 2.3 subtract_convert_fusion.2
  42.1 1.8 fusion
  43.9 1.4 maximum_select_fusion
  46.2 20.0 %shard_map.149 = bf16[256,1536]{1,0:T(8,128)(2,1)} custom-call(s32[3]{0:T(128)} %pad_add_fusion.meta_ref, s32[16]{0:T(128)} %dynamic-slice_bitcast_fusion.page_ref, bf16[256,1536]{1,0:T(8,128)(2,1)} %copy.65.q_ref, bf16[512,256]{1,0:T(8,128)(2,1)} %get-tuple-element.10.kn_ref, bf16[512,256]{1,0:T(8,128)(2,1)} %get-tuple-element.9.vn_ref, ...), custom_call_target="tpu_custom_call" | custom-call | tf_op jit(solution)/shard_map/pallas_call | solution.py:141
  66.2 4.2 %multiply_reduce_fusion = (f32[256]{0:T(256)S(1)}, f32[256,1536]{1,0:T(8,128)S(1)}) fusion(bf16[256,1536]{1,0:T(8,128)(2,1)} %shard_map.149, bf16[1536,1536]{1,0:T(8,128)(2,1)} %param.19, bf16[256,1536]{1,0:T(8,128)(2,1)S(1)} %copy-done.10), kind=kOutput, calls=%fused_computation.31 | convolution fusion | flops 1209532160 | bytes 7865344 | tf_op jit(solution)/shard_map/dot_general | solution.py:237
  70.4 1.5 convolution_convert_fusion
  71.9 115.6 %all_to_all.10 = bf16[32,1,48,1536]{3,2,1,0:T(8,128)(2,1)S(1)} all-to-all(bf16[32,1,48,1536]{3,2,1,0:T(8,128)(2,1)S(1)} %bitcast.58), channel_id=1, replica_groups=mesh['req'=32,'head'=4] {'req'}, dimensions={0} | all-to-all | bytes 9437184 | tf_op jit(solution)/shard_map/all_to_all | solution.py:271
  187.5 7.5 %convolution_bitcast_fusion = f32[32,1,48,1536]{3,2,0,1:T(8,128)S(1)} fusion(bf16[1,1536,1536]{2,1,0:T(8,128)(2,1)S(1)} %bitcast.65, bf16[32,1,48,1536]{3,2,1,0:T(8,128)(2,1)S(1)} %all_to_all.10), kind=kOutput, calls=%fused_computation.8 | convolution fusion | flops 7247757312 | bytes 18874368 | tf_op jit(solution)/shard_map/nekd,edf->nekf/dot_general | solution.py:269
  195.0 5.5 %convert_bitcast_fusion = bf16[32,1,48,1536]{3,2,1,0:T(8,128)(2,1)} fusion(f32[32,1,48,1536]{3,2,0,1:T(8,128)S(1)} %convolution_bitcast_fusion, bf16[1,768,1536]{2,1,0:T(8,128)(2,1)S(1)} %copy-done), kind=kOutput, calls=%fused_computation.14 | convolution fusion | flops 3629776896 | bytes 16515072 | tf_op jit(solution)/shard_map/nekf,efd->nekd/dot_general | solution.py:276
  200.5 5.9 %all-to-all-start.1 = ((bf16[32,1,48,1536]{3,2,1,0:T(8,128)(2,1)}), bf16[32,1,48,1536]{3,2,1,0:T(8,128)(2,1)}, u32[]{:S(2)}, u32[]{:S(2)}) async-start(bf16[32,1,48,1536]{3,2,1,0:T(8,128)(2,1)} %convert_bitcast_fusion), calls=%async_computation.1 | async-start | bytes 9437184 | tf_op jit(solution)/shard_map/all_to_all | solution.py:279
  207.5 8.6 %gather_fusion = f32[1024]{0:T(1024)S(1)} fusion(f32[256,32]{0,1:T(8,128)S(1)} %fusion.27, s32[1024]{0:T(1024)S(1)} %reshape.187), kind=kCustom, calls=%fused_computation.2 | custom fusion | bytes 16384 | tf_op jit(solution)/shard_map/jit(take_along_axis)/gather | solution.py:242
  217.5 51.2 %all-to-all-done.1 = bf16[32,1,48,1536]{3,2,1,0:T(8,128)(2,1)} async-done(((bf16[32,1,48,1536]{3,2,1,0:T(8,128)(2,1)}), bf16[32,1,48,1536]{3,2,1,0:T(8,128)(2,1)}, u32[]{:S(2)}, u32[]{:S(2)}) %all-to-all-start.1) | async-done | bytes 4718624 | tf_op jit(solution)/shard_map/all_to_all | solution.py:279
  268.7 3.8 %fusion.21 = f32[256,1536]{1,0:T(8,128)S(1)} fusion(bf16[1536,1536]{1,0:T(8,128)(2,1)} %bitcast.26, f32[256,1536]{1,0:T(8,128)S(1)} %select_reduce_fusion), kind=kOutput, calls=%fused_computation.44 | convolution fusion | flops 1208352768 | bytes 7864320 | tf_op jit(solution)/shard_map/dot_general | solution.py:286
  272.6 5.8 %fusion.6 = bf16[256,1536]{1,0:T(8,128)(2,1)} fusion(f32[256,1536]{1,0:T(8,128)S(1)} %copy-done.4, f32[256,1536]{1,0:T(8,128)S(1)} %fusion.21, bf16[1536,1536]{1,0:T(8,128)(2,1)} %bitcast.26, f32[256,1536]{1,0:T(8,128)} %copy-done.7), kind=kOutput, calls=%fused_computation.20 | convolution fusion | flops 1210712064 | bytes 10223616 | tf_op jit(solution)/shard_map/dot_general | solution.py:286
  (90 shorter events, 13.1 us)
Async XLA Ops:
  0.6 194.4 %copy-start = (bf16[1,768,1536]{2,1,0:T(8,128)(2,1)S(1)}, bf16[1,768,1536]{2,1,0:T(8,128)(2,1)}, u32[]{:S(2)}) copy-start(bf16[1,768,1536]{2,1,0:T(8,128)(2,1)} %param.23) | copy-start | bytes 7077892
  4.6 7.0 %copy-start.20 = (s32[64]{0:T(128)S(1)}, s32[64]{0:T(128)}, u32[]{:S(2)}) copy-start(s32[64]{0:T(128)} %param.28) | copy-start | bytes 772
  9.5 7.3 %copy-start.18 = (s32[64]{0:T(128)S(1)}, s32[64]{0:T(128)}, u32[]{:S(2)}) copy-start(s32[64]{0:T(128)} %param.29) | copy-start | bytes 772
  9.5 10.2 %copy-start.19 = (s32[2,16]{1,0:T(2,128)S(1)}, s32[2,16]{1,0:T(2,128)}, u32[]{:S(2)}) copy-start(s32[2,16]{1,0:T(2,128)} %param.27) | copy-start | bytes 388
  10.9 8.9 %copy-start.8 = (bf16[256,256]{1,0:T(8,128)(2,1)}, bf16[256,256]{1,0:T(8,128)(2,1)S(1)}, u32[]{:S(2)}) copy-start(bf16[256,256]{1,0:T(8,128)(2,1)S(1)} %slice.83) | copy-start | bytes 393220
  13.0 6.7 %copy-start.11 = (f32[256,64]{0,1:T(8,128)}, f32[256,64]{0,1:T(8,128)S(1)}, u32[]{:S(2)}) copy-start(f32[256,64]{0,1:T(8,128)S(1)} %get-tuple-element.13) | copy-start | bytes 196612
  13.1 6.7 %copy-start.13 = (f32[256,64]{0,1:T(8,128)}, f32[256,64]{0,1:T(8,128)S(1)}, u32[]{:S(2)}) copy-start(f32[256,64]{0,1:T(8,128)S(1)} %get-tuple-element.14) | copy-start | bytes 196612
  15.5 28.4 %collective-permute-start = (bf16[256,512]{1,0:T(8,128)(2,1)}, bf16[256,512]{1,0:T(8,128)(2,1)}, u32[]{:S(2)}, u32[]{:S(2)}) collective-permute-start(bf16[256,512]{1,0:T(8,128)(2,1)} %pad_maximum_fusion.1), channel_id=1, source_target_pairs={{0,1},{2,3},{4,5},{6,7},{8,9},{10,11},{12,13},{14,15},{16,17},{18,... | collective-permute-start | bytes 786440 | tf_op jit(solution)/shard_map/ppermute | solution.py:206
  25.2 3.5 %copy-start.6 = (f32[256,2048]{1,0:T(8,128)S(1)}, f32[256,2048]{1,0:T(8,128)}, u32[]{:S(2)}) copy-start(f32[256,2048]{1,0:T(8,128)} %copy-done.5) | copy-start | bytes 6291460
  28.2 18.0 %collective-permute-start.1 = (bf16[16,128,256]{2,1,0:T(8,128)(2,1)}, bf16[16,128,256]{2,1,0:T(8,128)(2,1)}, u32[]{:S(2)}, u32[]{:S(2)}) collective-permute-start(bf16[16,128,256]{2,1,0:T(8,128)(2,1)} %get-tuple-element.16), channel_id=1, source_target_pairs={{0,4},{4,0},{8,12},{12,8},{16,20},{20,16},{24,28},{28,24},{32,36},... | collective-permute-start | bytes 3145736 | tf_op jit(solution)/shard_map/ppermute | solution.py:226
  28.2 18.0 %collective-permute-start.2 = (bf16[16,128,256]{2,1,0:T(8,128)(2,1)}, bf16[16,128,256]{2,1,0:T(8,128)(2,1)}, u32[]{:S(2)}, u32[]{:S(2)}) collective-permute-start(bf16[16,128,256]{2,1,0:T(8,128)(2,1)} %get-tuple-element.15), channel_id=1, source_target_pairs={{0,4},{4,0},{8,12},{12,8},{16,20},{20,16},{24,28},{28,24},{32,36},... | collective-permute-start | bytes 3145736 | tf_op jit(solution)/shard_map/ppermute | solution.py:226
  29.9 3.1 %copy-start.12 = (f32[256,64]{0,1:T(8,128)S(1)}, f32[256,64]{0,1:T(8,128)}, u32[]{:S(2)}) copy-start(f32[256,64]{0,1:T(8,128)} %copy-done.11) | copy-start | bytes 196612
  29.9 3.1 %copy-start.14 = (f32[256,64]{0,1:T(8,128)S(1)}, f32[256,64]{0,1:T(8,128)}, u32[]{:S(2)}) copy-start(f32[256,64]{0,1:T(8,128)} %copy-done.13) | copy-start | bytes 196612
  29.9 5.4 %copy-start.16 = (s32[256,4]{0,1:T(4,128)S(1)}, s32[256,4]{0,1:T(4,128)}, u32[]{:S(2)}) copy-start(s32[256,4]{0,1:T(4,128)} %param.24) | copy-start | bytes 12292
  46.2 20.0 %copy-start.10 = (bf16[256,1536]{1,0:T(8,128)(2,1)S(1)}, bf16[256,1536]{1,0:T(8,128)(2,1)}, u32[]{:S(2)}) copy-start(bf16[256,1536]{1,0:T(8,128)(2,1)} %param.16) | copy-start | bytes 2359300
  66.1 4.2 %copy-start.17 = (f32[1536]{0:T(1024)S(1)}, f32[1536]{0:T(1024)}, u32[]{:S(2)}) copy-start(f32[1536]{0:T(1024)} %param.20) | copy-start | bytes 18436
  66.1 121.3 %slice-start = ((s8[4718592]{0:T(1024)(128)(4,1)}), s8[4194304]{0:T(1024)(128)(4,1)S(1)}, s32[]{:S(2)}) async-start(s8[4718592]{0:T(1024)(128)(4,1)} %bitcast.64), calls=%async_computation.2 | async-start | bytes 8388608
  70.4 117.1 %slice-start.1 = ((s8[4718592]{0:T(1024)(128)(4,1)}), s8[524288]{0:T(1024)(128)(4,1)S(1)}, s32[]{:S(2)}) async-start(s8[4718592]{0:T(1024)(128)(4,1)} %bitcast.64), calls=%async_computation.3 | async-start | bytes 1048576
  200.5 6.2 %copy-start.3 = (f32[256,1536]{1,0:T(8,128)S(1)}, f32[256,1536]{1,0:T(8,128)}, u32[]{:S(2)}) copy-start(f32[256,1536]{1,0:T(8,128)} %copy-done.2) | copy-start | bytes 4718596
  200.5 6.2 %copy-start.15 = (f32[1536,32]{0,1:T(8,128)S(1)}, f32[1536,32]{0,1:T(8,128)}, u32[]{:S(2)}) copy-start(f32[1536,32]{0,1:T(8,128)} %param.21) | copy-start | bytes 589828
  200.5 68.2 %all-to-all-start.1 = ((bf16[32,1,48,1536]{3,2,1,0:T(8,128)(2,1)}), bf16[32,1,48,1536]{3,2,1,0:T(8,128)(2,1)}, u32[]{:S(2)}, u32[]{:S(2)}) async-start(bf16[32,1,48,1536]{3,2,1,0:T(8,128)(2,1)} %convert_bitcast_fusion), calls=%async_computation.1 | async-start | bytes 9437184 | tf_op jit(solution)/shard_map/all_to_all | solution.py:279
  217.5 51.2 %copy-start.7 = (f32[256,1536]{1,0:T(8,128)}, f32[256,1536]{1,0:T(8,128)S(1)}, u32[]{:S(2)}) copy-start(f32[256,1536]{1,0:T(8,128)S(1)} %select_reduce_fusion) | copy-start | bytes 4718596
  268.7 3.8 %copy-start.4 = (f32[256,1536]{1,0:T(8,128)S(1)}, f32[256,1536]{1,0:T(8,128)}, u32[]{:S(2)}) copy-start(f32[256,1536]{1,0:T(8,128)} %copy-done.2) | copy-start | bytes 4718596
  272.6 5.8 %copy-start.1 = (bf16[1,768,1536]{2,1,0:T(8,128)(2,1)S(1)}, bf16[1,768,1536]{2,1,0:T(8,128)(2,1)}, u32[]{:S(2)}) copy-start(bf16[1,768,1536]{2,1,0:T(8,128)(2,1)} %param.23) | copy-start | bytes 7077892
  (3 other events, 3.5 us)

commit v2 on v1

--- a/solution.py
+++ b/solution.py
@@ -14,6 +14,7 @@
 FE = 768
 TOPK = 4
 REQUEST_TOKENS = 512
+PAGE_CHUNK = 128
 
 
 EPS = 1e-06
@@ -44,45 +45,38 @@
 
 
 def attention_kernel(
-    meta_ref, page_ref, q_ref, kn_ref, vn_ref, kl_ref, vl_ref, kr_ref, vr_ref,
-    o_ref, m_sc, l_sc, acc_sc, *, group, tokens
+    meta_ref, q_ref, kn_ref, vn_ref, k_ref, v_ref, o_ref, q_sc, m_sc, l_sc, acc_sc, *, group, tokens
 ):
-    j = pl.program_id(1)
     count = meta_ref[0]
-    moved = meta_ref[1]
-    half = meta_ref[2]
+    half = meta_ref[1]
     scaling = HEAD_SIZE ** (-0.5)
     contract = (((1,), (1,)), ((), ()))
-
-    def stacked_queries():
-        q = q_ref[...]
-        return jnp.concatenate(
-            [q[:, g * HEAD_SIZE : (g + 1) * HEAD_SIZE] for g in range(group)], axis=0
-        )
-
-    @pl.when(j == 0)
-    def _():
-        qa = stacked_queries()
-        s = lax.dot_general(qa, kn_ref[...], contract, preferred_element_type=jnp.float32)
-        s = s * scaling
-        rows = group * tokens
-        t = lax.broadcasted_iota(jnp.int32, (group, tokens, s.shape[1]), 1).reshape(rows, -1)
-        v = lax.broadcasted_iota(jnp.int32, s.shape, 1)
-        s = jnp.where(v <= t + half * tokens, s, -jnp.inf)
-        m = jnp.max(s, axis=1, keepdims=True)
-        p = jnp.exp(s - m)
-        l_sc[...] = jnp.sum(p, axis=1, keepdims=True)
-        m_sc[...] = m
-        acc_sc[...] = jnp.dot(
-            p.astype(jnp.bfloat16), vn_ref[...], preferred_element_type=jnp.float32
-        )
-
-    @pl.when((j > 0) & (j - 1 < count))
-    def _():
-        qa = stacked_queries()
-        k = jnp.where(moved == 1, kr_ref[0], kl_ref[0])
-        vv = jnp.where(moved == 1, vr_ref[0], vl_ref[0])
-        s = lax.dot_general(qa, k, contract, preferred_element_type=jnp.float32) * scaling
+    chunk = 2 * PAGE_CHUNK
+
+    q = q_ref[...]
+    q_sc[...] = jnp.concatenate(
+        [q[:, g * HEAD_SIZE : (g + 1) * HEAD_SIZE] for g in range(group)], axis=0
+    )
+    s = lax.dot_general(q_sc[...], kn_ref[...], contract, preferred_element_type=jnp.float32)
+    s = s * scaling
+    rows = group * tokens
+    t = lax.broadcasted_iota(jnp.int32, (group, tokens, s.shape[1]), 1).reshape(rows, -1)
+    v = lax.broadcasted_iota(jnp.int32, s.shape, 1)
+    s = jnp.where(v <= t + half * tokens, s, -jnp.inf)
+    m = jnp.max(s, axis=1, keepdims=True)
+    p = jnp.exp(s - m)
+    l_sc[...] = jnp.sum(p, axis=1, keepdims=True)
+    m_sc[...] = m
+    acc_sc[...] = jnp.dot(p.astype(jnp.bfloat16), vn_ref[...], preferred_element_type=jnp.float32)
+    limit = count * PAGE_CHUNK
+
+    def visit(i, carry):
+        first = pl.multiple_of(i * chunk, chunk)
+        k = k_ref[pl.ds(first, chunk), :]
+        vv = v_ref[pl.ds(first, chunk), :]
+        s = lax.dot_general(q_sc[...], k, contract, preferred_element_type=jnp.float32) * scaling
+        key_ids = first + lax.broadcasted_iota(jnp.int32, s.shape, 1)
+        s = jnp.where(key_ids < limit, s, -jnp.inf)
         m_old = m_sc[...]
         m_new = jnp.maximum(m_old, jnp.max(s, axis=1, keepdims=True))
         factor = jnp.exp(m_old - m_new)
@@ -92,47 +86,34 @@
             p.astype(jnp.bfloat16), vv, preferred_element_type=jnp.float32
         )
         m_sc[...] = m_new
-
-    @pl.when(j == pl.num_programs(1) - 1)
-    def _():
-        res = acc_sc[...] / l_sc[...]
-        o_ref[...] = jnp.concatenate(
-            [res[g * tokens : (g + 1) * tokens] for g in range(group)], axis=1
-        ).astype(jnp.bfloat16)
-
-
-def attend(meta, page_ids, queries, new_keys, new_values, k_pool, v_pool, k_got, v_got):
+        return carry
+
+    lax.fori_loop(0, (count + 1) // 2, visit, 0)
+    res = acc_sc[...] / l_sc[...]
+    o_ref[...] = jnp.concatenate(
+        [res[g * tokens : (g + 1) * tokens] for g in range(group)], axis=1
+    ).astype(jnp.bfloat16)
+
+
+def attend(meta, queries, new_keys, new_values, cache_keys, cache_values):
     tokens = queries.shape[0]
     group = QUERY_HEADS // KEY_VALUE_HEADS
     width = group * HEAD_SIZE
     span = new_keys.shape[0]
-    page_size = k_pool.shape[1]
-    max_pages = page_ids.shape[0]
-
-    def page_at(j, meta_ref):
-        return jnp.maximum(jnp.minimum(j - 1, meta_ref[0] - 1), 0)
-
-    def local_map(c, j, meta_ref, page_ref):
-        return (page_ref[page_at(j, meta_ref)] * (1 - meta_ref[1]), 0, c)
-
-    def got_map(c, j, meta_ref, page_ref):
-        return (page_at(j, meta_ref) * meta_ref[1], 0, c)
-
-    page_block = (1, page_size, HEAD_SIZE)
+    cache_rows = cache_keys.shape[0]
     grid_spec = pltpu.PrefetchScalarGridSpec(
-        num_scalar_prefetch=2,
-        grid=(KEY_VALUE_HEADS, max_pages + 1),
+        num_scalar_prefetch=1,
+        grid=(KEY_VALUE_HEADS,),
         in_specs=[
-            pl.BlockSpec((tokens, width), lambda c, j, m, p: (0, c)),
-            pl.BlockSpec((span, HEAD_SIZE), lambda c, j, m, p: (0, c)),
-            pl.BlockSpec((span, HEAD_SIZE), lambda c, j, m, p: (0, c)),
-            pl.BlockSpec(page_block, local_map),
-            pl.BlockSpec(page_block, local_map),
-            pl.BlockSpec(page_block, got_map),
-            pl.BlockSpec(page_block, got_map),
+            pl.BlockSpec((tokens, width), lambda c, m: (0, c)),
+            pl.BlockSpec((span, HEAD_SIZE), lambda c, m: (0, c)),
+            pl.BlockSpec((span, HEAD_SIZE), lambda c, m: (0, c)),
+            pl.BlockSpec((cache_rows, HEAD_SIZE), lambda c, m: (0, c)),
+            pl.BlockSpec((cache_rows, HEAD_SIZE), lambda c, m: (0, c)),
         ],
-        out_specs=pl.BlockSpec((tokens, width), lambda c, j, m, p: (0, c)),
+        out_specs=pl.BlockSpec((tokens, width), lambda c, m: (0, c)),
         scratch_shapes=[
+            pltpu.VMEM((group * tokens, HEAD_SIZE), jnp.bfloat16),
             pltpu.VMEM((group * tokens, 1), jnp.float32),
             pltpu.VMEM((group * tokens, 1), jnp.float32),
             pltpu.VMEM((group * tokens, HEAD_SIZE), jnp.float32),
@@ -142,8 +123,8 @@
         functools.partial(attention_kernel, group=group, tokens=tokens),
         grid_spec=grid_spec,
         out_shape=jax.ShapeDtypeStruct((tokens, QUERY_HEADS * HEAD_SIZE), jnp.bfloat16),
-        compiler_params=pltpu.CompilerParams(dimension_semantics=("arbitrary", "arbitrary")),
-    )(meta, page_ids, queries, new_keys, new_values, k_pool, v_pool, k_got, v_got)
+        compiler_params=pltpu.CompilerParams(dimension_semantics=("arbitrary",)),
+    )(meta, queries, new_keys, new_values, cache_keys, cache_values)
 
 
 def on_device(
@@ -225,12 +206,16 @@
     pairs = [(source, source ^ 1) for source in range(req_count)]
     k_got, v_got = lax.ppermute(sent, "req", pairs)
 
-    moved_in = (old_id // req_dev != req_index).astype(jnp.int32)
+    moved_in = old_id // req_dev != req_index
     page_ids = page_table[old_id % req_dev]
-    meta = jnp.stack([cached_pages[old_id], moved_in, half.astype(jnp.int32)]).astype(jnp.int32)
+    cache_rows = page_ids.shape[0] * page_size
+    cache_keys = jnp.where(moved_in, k_got, jnp.take(key_page_store, page_ids, axis=0))
+    cache_values = jnp.where(moved_in, v_got, jnp.take(value_page_store, page_ids, axis=0))
+    meta = jnp.stack([cached_pages[old_id], half.astype(jnp.int32)]).astype(jnp.int32)
     attention = attend(
-        meta, page_ids, queries.reshape(tokens_per_device, QUERY_HEADS * HEAD_SIZE),
-        new_keys, new_values, key_page_store, value_page_store, k_got, v_got,
+        meta, queries.reshape(tokens_per_device, QUERY_HEADS * HEAD_SIZE),
+        new_keys, new_values,
+        cache_keys.reshape(cache_rows, kv_width), cache_values.reshape(cache_rows, kv_width),
     )
     del slot
 
@@ -239,7 +224,8 @@
     )
     normed_moe = rms_scale(residual, norm2_gain).astype(jnp.bfloat16)
     logits = jnp.dot(normed_moe.astype(jnp.float32), router_weight, precision=lax.Precision.HIGHEST)
-    chosen = jnp.take_along_axis(logits, routes, axis=1)
+    route_match = routes[:, :, None] == jnp.arange(logits.shape[1], dtype=jnp.int32)[None, None, :]
+    chosen = jnp.sum(jnp.where(route_match, logits[:, None, :], 0.0), axis=2)
     sigmoids = jax.nn.sigmoid(chosen)
     route_gates = sigmoids / jnp.sum(sigmoids, axis=1, keepdims=True)
 

time: 282 us -> 287 us (1.018)
  blocking collectives: 116 us -> 90.8 us
  Pallas kernels: 20 us -> 37.9 us
  waiting for transfers between devices: 51.2 us -> 57.8 us
    all_to_all x1, blocking collectives: 116 us -> 90.8 us  [on_device(): lax.all_to_all(dispatch, 'req', split_axis=0, concat_axis=0, tiled=True)]
    pallas_call x1, Pallas kernels: 20 us -> 37.9 us  [attend(): pl.pallas_call(functools.partial(attention_kernel, group=group, tokens=to...]
    all_to_all x1, waiting for transfers between devices: 51.2 us -> 57.8 us  [on_device(): lax.all_to_all(result, 'req', split_axis=0, concat_axis=0, tiled=True)]
    gather x5 -> x2, local copies, waits for them, and re-layouts: 9.1 us -> 5.39 us  [the longest x1 3.18 us: on_device(): jnp.take(key_page_store, page_ids, axis=0)]
  transfers between devices with their start and end apart: 4 -> 4, of which waited for: 1 -> 1; matrix products, arithmetic and copies ran while one was open for 13% -> 14% of each run, Pallas kernels for 0% -> 0%
where the time goes in v2:
time: 287 us; the launch traced here: 282 us
  blocking collectives  90.8 us (32%)
  waiting for transfers between devices  57.8 us (20%)
  Pallas kernels  37.9 us (13%)
  matrix products  35.4 us (12%)
  local copies, waits for them, and re-layouts  26.3 us (9%)
  other arithmetic  18.8 us (7%)
  starting transfers between devices  7.66 us (3%)
  between operations  7.4 us (3%)
    all_to_all x1, blocking collectives, on_device(): lax.all_to_all(dispatch, 'req', split_axis=0, concat_axis=0, tiled=True)  90.8 us
    all_to_all x1, waiting for transfers between devices, on_device(): lax.all_to_all(result, 'req', split_axis=0, concat_axis=0, tiled=True)  57.8 us
    pallas_call x1, Pallas kernels, attend(): pl.pallas_call(functools.partial(attention_kernel, group=group, tokens=to...  37.9 us
    dot_general x1, matrix products, on_device(): jnp.einsum('nekd,edf->nekf', lax.all_to_all(dispatch, 'req', split_axis=0...  7.51 us
    all_to_all x1, starting transfers between devices, on_device(): lax.all_to_all(result, 'req', split_axis=0, concat_axis=0, tiled=True)  5.86 us
  transfers between devices with their start and end apart: 4, of which 1 were waited for; matrix products, arithmetic and copies ran while one was open for 14% of the time, Pallas kernels for 0%

profile of v2, /device:TPU:56, one launch (start us, length us, event | category | flops | bytes accessed | tf_op | source)
XLA Modules:
  0.0 282.1 jit_solution(17604952977953977457)
XLA Ops:
  0.7 1.4 dynamic_slice.16
  4.8 4.9 %fusion.16 = f32[256,2048]{1,0:T(8,128)S(1)} fusion(bf16[1536,2048]{1,0:T(8,128)(2,1)} %param.18, bf16[256,1536]{1,0:T(8,128)(2,1)} %param.16, f32[1536]{0:T(1024)} %param.17, f32[256]{0:T(256)S(1)} %add_rsqrt_fusion.1), kind=kOutput, calls=%fused_computation.39 | convolution fusion | flops 1612185600 | bytes 9182208 | tf_op jit(solution)/shard_map/dot_general | solution.py:164
  21.1 2.2 gather_fusion.2
  23.3 3.2 %gather_fusion = bf16[16,128,256]{2,1,0:T(8,128)(2,1)} fusion(bf16[32,128,256]{2,1,0:T(8,128)(2,1)} %param.25, s32[1024]{0:T(1024)S(1)} %pad_clamp_fusion.1), kind=kCustom, calls=%fused_computation.clone | custom fusion | bytes 2097216 | tf_op jit(solution)/shard_map/jit(_take)/gather | solution.py:203
  26.5 3.0 %broadcast_select_fusion = (bf16[16,128,256]{2,1,0:T(8,128)(2,1)}, bf16[16,128,256]{2,1,0:T(8,128)(2,1)}) fusion(bf16[16,128,256]{2,1,0:T(8,128)(2,1)S(1)} %gather_fusion.2, pred[16]{0:T(512)(128)(4,1)S(1)} %get-tuple-element.15, bf16[16,128,256]{2,1,0:T(8,128)(2,1)} %gather_fusion), kind=kLoop, calls=%fused_computation.37 | loop fusion | flops 1048576 | bytes 4194320 | tf_op jit(solution)/shard_map/jit(_take)/select_n | solution.py:204
  31.3 3.1 %copy.51 = f32[256,1536]{0,1:T(8,128)} copy(f32[256,1536]{1,0:T(8,128)} %slice.53) | data formatting | bytes 3145728 | tf_op jit(solution)/shard_map/slice | solution.py:166
  34.4 1.6 subtract_convert_fusion.2
  37.5 2.2 gather_fusion.3
  39.8 3.2 %gather_fusion.1 = bf16[16,128,256]{2,1,0:T(8,128)(2,1)} fusion(bf16[32,128,256]{2,1,0:T(8,128)(2,1)} %param.25, s32[1024]{0:T(1024)S(1)} %pad_clamp_fusion), kind=kCustom, calls=%fused_computation.1.clone | custom fusion | bytes 2097216 | tf_op jit(solution)/shard_map/jit(_take)/gather | solution.py:212
  42.9 2.3 copy.54.q_ref
  50.8 2.6 fusion
  55.5 1.7 select_select_fusion
  57.2 37.9 %shard_map.149 = bf16[256,1536]{1,0:T(8,128)(2,1)} custom-call(s32[2]{0:T(128)} %pad_add_fusion.meta_ref, bf16[256,1536]{1,0:T(8,128)(2,1)} %copy.54.q_ref, bf16[512,256]{1,0:T(8,128)(2,1)} %get-tuple-element.10.kn_ref, bf16[512,256]{1,0:T(8,128)(2,1)} %get-tuple-element.9.vn_ref, bf16[2048,256]{1,0:T(8,128)(2,1)} %bitcast.59, bf16[2048,256]{1,0:T(8,128)(2,1)} %bitcast.58), custom_call_target="tpu_custom_call" | custom-call | tf_op jit(solution)/shard_map/pallas_call | solution.py:122
  95.2 4.2 %multiply_reduce_fusion = (f32[256]{0:T(256)S(1)}, f32[256,1536]{1,0:T(8,128)S(1)}) fusion(bf16[256,1536]{1,0:T(8,128)(2,1)} %shard_map.149, bf16[1536,1536]{1,0:T(8,128)(2,1)} %param.19, bf16[256,1536]{1,0:T(8,128)(2,1)S(1)} %copy-done.9), kind=kOutput, calls=%fused_computation.32 | convolution fusion | flops 1209532160 | bytes 7865344 | tf_op jit(solution)/shard_map/dot_general | solution.py:222
  99.5 1.5 convolution_convert_fusion
  101.0 90.8 %all_to_all.10 = bf16[32,1,48,1536]{3,2,1,0:T(8,128)(2,1)S(1)} all-to-all(bf16[32,1,48,1536]{3,2,1,0:T(8,128)(2,1)S(1)} %bitcast.56), channel_id=1, replica_groups=mesh['req'=32,'head'=4] {'req'}, dimensions={0} | all-to-all | bytes 9437184 | tf_op jit(solution)/shard_map/all_to_all | solution.py:257
  191.8 7.5 %convolution_bitcast_fusion = f32[32,1,48,1536]{3,2,0,1:T(8,128)S(1)} fusion(bf16[1,1536,1536]{2,1,0:T(8,128)(2,1)S(1)} %bitcast.65, bf16[32,1,48,1536]{3,2,1,0:T(8,128)(2,1)S(1)} %all_to_all.10), kind=kOutput, calls=%fused_computation.9 | convolution fusion | flops 7247757312 | bytes 18874368 | tf_op jit(solution)/shard_map/nekd,edf->nekf/dot_general | solution.py:255
  199.3 5.5 %convert_bitcast_fusion = bf16[32,1,48,1536]{3,2,1,0:T(8,128)(2,1)} fusion(f32[32,1,48,1536]{3,2,0,1:T(8,128)S(1)} %convolution_bitcast_fusion, bf16[1,768,1536]{2,1,0:T(8,128)(2,1)S(1)} %copy-done), kind=kOutput, calls=%fused_computation.15 | convolution fusion | flops 3629776896 | bytes 16515072 | tf_op jit(solution)/shard_map/nekf,efd->nekd/dot_general | solution.py:262
  204.8 5.9 %all-to-all-start.1 = ((bf16[32,1,48,1536]{3,2,1,0:T(8,128)(2,1)}), bf16[32,1,48,1536]{3,2,1,0:T(8,128)(2,1)}, u32[]{:S(2)}, u32[]{:S(2)}) async-start(bf16[32,1,48,1536]{3,2,1,0:T(8,128)(2,1)} %convert_bitcast_fusion), calls=%async_computation.1 | async-start | bytes 9437184 | tf_op jit(solution)/shard_map/all_to_all | solution.py:265
  210.7 2.2 fusion.27
  213.1 2.2 select_reduce_fusion
  215.3 57.8 %all-to-all-done.1 = bf16[32,1,48,1536]{3,2,1,0:T(8,128)(2,1)} async-done(((bf16[32,1,48,1536]{3,2,1,0:T(8,128)(2,1)}), bf16[32,1,48,1536]{3,2,1,0:T(8,128)(2,1)}, u32[]{:S(2)}, u32[]{:S(2)}) %all-to-all-start.1) | async-done | bytes 4718624 | tf_op jit(solution)/shard_map/all_to_all | solution.py:265
  273.1 4.3 %fusion.21 = f32[256,1536]{1,0:T(8,128)S(1)} fusion(bf16[1536,1536]{1,0:T(8,128)(2,1)} %bitcast.26, f32[256,1536]{1,0:T(8,128)} %select_reduce_fusion), kind=kOutput, calls=%fused_computation.47 | convolution fusion | flops 1208352768 | bytes 7864320 | tf_op jit(solution)/shard_map/dot_general | solution.py:272
  277.4 4.7 %fusion.6 = bf16[256,1536]{1,0:T(8,128)(2,1)} fusion(f32[256,1536]{1,0:T(8,128)S(1)} %copy-done.2, f32[256,1536]{1,0:T(8,128)S(1)} %fusion.21, bf16[1536,1536]{1,0:T(8,128)(2,1)} %bitcast.26, f32[256,1536]{1,0:T(8,128)S(1)} %copy-done.7), kind=kOutput, calls=%fused_computation.21 | convolution fusion | flops 1210712064 | bytes 10223616 | tf_op jit(solution)/shard_map/dot_general | solution.py:272
  (86 shorter events, 18.7 us)
Async XLA Ops:
  0.6 198.7 %copy-start = (bf16[1,768,1536]{2,1,0:T(8,128)(2,1)S(1)}, bf16[1,768,1536]{2,1,0:T(8,128)(2,1)}, u32[]{:S(2)}) copy-start(bf16[1,768,1536]{2,1,0:T(8,128)(2,1)} %param.23) | copy-start | bytes 7077892
  4.8 7.0 %copy-start.19 = (s32[64]{0:T(128)S(1)}, s32[64]{0:T(128)}, u32[]{:S(2)}) copy-start(s32[64]{0:T(128)} %param.28) | copy-start | bytes 772
  9.7 8.7 %copy-start.18 = (s32[64]{0:T(128)S(1)}, s32[64]{0:T(128)}, u32[]{:S(2)}) copy-start(s32[64]{0:T(128)} %param.29) | copy-start | bytes 772
  9.7 11.4 %copy-start.17 = (s32[2,16]{1,0:T(2,128)S(1)}, s32[2,16]{1,0:T(2,128)}, u32[]{:S(2)}) copy-start(s32[2,16]{1,0:T(2,128)} %param.27) | copy-start | bytes 388
  13.3 7.7 %copy-start.10 = (f32[256,64]{0,1:T(8,128)}, f32[256,64]{0,1:T(8,128)S(1)}, u32[]{:S(2)}) copy-start(f32[256,64]{0,1:T(8,128)S(1)} %get-tuple-element.13) | copy-start | bytes 196612
  13.4 7.7 %copy-start.12 = (f32[256,64]{0,1:T(8,128)}, f32[256,64]{0,1:T(8,128)S(1)}, u32[]{:S(2)}) copy-start(f32[256,64]{0,1:T(8,128)S(1)} %get-tuple-element.14) | copy-start | bytes 196612
  15.8 37.5 %collective-permute-start = (bf16[256,512]{1,0:T(8,128)(2,1)}, bf16[256,512]{1,0:T(8,128)(2,1)}, u32[]{:S(2)}, u32[]{:S(2)}) collective-permute-start(bf16[256,512]{1,0:T(8,128)(2,1)} %pad_maximum_fusion.1), channel_id=1, source_target_pairs={{0,1},{2,3},{4,5},{6,7},{8,9},{10,11},{12,13},{14,15},{16,17},{18,... | collective-permute-start | bytes 786440 | tf_op jit(solution)/shard_map/ppermute | solution.py:187
  26.5 3.5 %copy-start.6 = (f32[256,2048]{1,0:T(8,128)S(1)}, f32[256,2048]{1,0:T(8,128)}, u32[]{:S(2)}) copy-start(f32[256,2048]{1,0:T(8,128)} %copy-done.5) | copy-start | bytes 6291460
  29.5 26.0 %collective-permute-start.2 = (bf16[16,128,256]{2,1,0:T(8,128)(2,1)}, bf16[16,128,256]{2,1,0:T(8,128)(2,1)}, u32[]{:S(2)}, u32[]{:S(2)}) collective-permute-start(bf16[16,128,256]{2,1,0:T(8,128)(2,1)} %get-tuple-element.19), channel_id=1, source_target_pairs={{0,4},{4,0},{8,12},{12,8},{16,20},{20,16},{24,28},{28,24},{32,36},... | collective-permute-start | bytes 3145736 | tf_op jit(solution)/shard_map/ppermute | solution.py:207
  29.5 26.0 %collective-permute-start.1 = (bf16[16,128,256]{2,1,0:T(8,128)(2,1)}, bf16[16,128,256]{2,1,0:T(8,128)(2,1)}, u32[]{:S(2)}, u32[]{:S(2)}) collective-permute-start(bf16[16,128,256]{2,1,0:T(8,128)(2,1)} %get-tuple-element.20), channel_id=1, source_target_pairs={{0,4},{4,0},{8,12},{12,8},{16,20},{20,16},{24,28},{28,24},{32,36},... | collective-permute-start | bytes 3145736 | tf_op jit(solution)/shard_map/ppermute | solution.py:207
  31.3 3.1 %copy-start.11 = (f32[256,64]{0,1:T(8,128)S(1)}, f32[256,64]{0,1:T(8,128)}, u32[]{:S(2)}) copy-start(f32[256,64]{0,1:T(8,128)} %copy-done.10) | copy-start | bytes 196612
  31.3 3.1 %copy-start.13 = (f32[256,64]{0,1:T(8,128)S(1)}, f32[256,64]{0,1:T(8,128)}, u32[]{:S(2)}) copy-start(f32[256,64]{0,1:T(8,128)} %copy-done.12) | copy-start | bytes 196612
  39.8 5.5 %copy-start.15 = (s32[256,4]{0,1:T(4,128)S(1)}, s32[256,4]{0,1:T(4,128)}, u32[]{:S(2)}) copy-start(s32[256,4]{0,1:T(4,128)} %param.24) | copy-start | bytes 12292
  49.4 6.1 %copy-start.3 = (bf16[16,128,256]{2,1,0:T(8,128)(2,1)S(1)}, bf16[16,128,256]{2,1,0:T(8,128)(2,1)}, u32[]{:S(2)}) copy-start(bf16[16,128,256]{2,1,0:T(8,128)(2,1)} %gather_fusion.1) | copy-start | bytes 3145732
  57.2 37.9 %copy-start.9 = (bf16[256,1536]{1,0:T(8,128)(2,1)S(1)}, bf16[256,1536]{1,0:T(8,128)(2,1)}, u32[]{:S(2)}) copy-start(bf16[256,1536]{1,0:T(8,128)(2,1)} %param.16) | copy-start | bytes 2359300
  95.2 4.2 %copy-start.4 = (pred[1536,256]{1,0:T(8,128)(4,1)S(1)}, pred[1536,256]{1,0:T(8,128)(4,1)}, u32[]{:S(2)}) copy-start(pred[1536,256]{1,0:T(8,128)(4,1)} %fusion) | copy-start | bytes 1179652
  95.2 4.3 %copy-start.16 = (f32[1536]{0:T(1024)S(1)}, f32[1536]{0:T(1024)}, u32[]{:S(2)}) copy-start(f32[1536]{0:T(1024)} %param.20) | copy-start | bytes 18436
  95.2 96.6 %slice-start = ((s8[4718592]{0:T(1024)(128)(4,1)}), s8[4194304]{0:T(1024)(128)(4,1)S(1)}, s32[]{:S(2)}) async-start(s8[4718592]{0:T(1024)(128)(4,1)} %bitcast.64), calls=%async_computation.2 | async-start | bytes 8388608
  99.4 1.5 copy-start.1
  99.5 92.4 %slice-start.1 = ((s8[4718592]{0:T(1024)(128)(4,1)}), s8[524288]{0:T(1024)(128)(4,1)S(1)}, s32[]{:S(2)}) async-start(s8[4718592]{0:T(1024)(128)(4,1)} %bitcast.64), calls=%async_computation.3 | async-start | bytes 1048576
  204.8 5.9 %copy-start.14 = (f32[1536,32]{0,1:T(8,128)S(1)}, f32[1536,32]{0,1:T(8,128)}, u32[]{:S(2)}) copy-start(f32[1536,32]{0,1:T(8,128)} %param.21) | copy-start | bytes 589828
  204.8 68.2 %all-to-all-start.1 = ((bf16[32,1,48,1536]{3,2,1,0:T(8,128)(2,1)}), bf16[32,1,48,1536]{3,2,1,0:T(8,128)(2,1)}, u32[]{:S(2)}, u32[]{:S(2)}) async-start(bf16[32,1,48,1536]{3,2,1,0:T(8,128)(2,1)} %convert_bitcast_fusion), calls=%async_computation.1 | async-start | bytes 9437184 | tf_op jit(solution)/shard_map/all_to_all | solution.py:265
  273.1 4.3 %copy-start.2 = (f32[256,1536]{1,0:T(8,128)S(1)}, f32[256,1536]{1,0:T(8,128)}, u32[]{:S(2)}) copy-start(f32[256,1536]{1,0:T(8,128)} %copy-done.1) | copy-start | bytes 4718596
  273.1 4.4 %copy-start.7 = (f32[256,1536]{1,0:T(8,128)S(1)}, f32[256,1536]{1,0:T(8,128)}, u32[]{:S(2)}) copy-start(f32[256,1536]{1,0:T(8,128)} %select_reduce_fusion) | copy-start | bytes 4718596
  (2 other events, 2.0 us)

commit v3 on v2

--- a/solution.py
+++ b/solution.py
@@ -15,6 +15,7 @@
 TOPK = 4
 REQUEST_TOKENS = 512
 PAGE_CHUNK = 128
+STACK = 6
 
 
 EPS = 1e-06
@@ -45,54 +46,62 @@
 
 
 def attention_kernel(
-    meta_ref, q_ref, kn_ref, vn_ref, k_ref, v_ref, o_ref, q_sc, m_sc, l_sc, acc_sc, *, group, tokens
+    meta_ref, q_ref, kn_ref, vn_ref, k_ref, v_ref, o_ref, m_sc, l_sc, acc_sc, *, group, tokens
 ):
     count = meta_ref[0]
     half = meta_ref[1]
     scaling = HEAD_SIZE ** (-0.5)
     contract = (((1,), (1,)), ((), ()))
-    chunk = 2 * PAGE_CHUNK
-
-    q = q_ref[...]
-    q_sc[...] = jnp.concatenate(
-        [q[:, g * HEAD_SIZE : (g + 1) * HEAD_SIZE] for g in range(group)], axis=0
-    )
-    s = lax.dot_general(q_sc[...], kn_ref[...], contract, preferred_element_type=jnp.float32)
-    s = s * scaling
-    rows = group * tokens
-    t = lax.broadcasted_iota(jnp.int32, (group, tokens, s.shape[1]), 1).reshape(rows, -1)
-    v = lax.broadcasted_iota(jnp.int32, s.shape, 1)
-    s = jnp.where(v <= t + half * tokens, s, -jnp.inf)
-    m = jnp.max(s, axis=1, keepdims=True)
-    p = jnp.exp(s - m)
-    l_sc[...] = jnp.sum(p, axis=1, keepdims=True)
-    m_sc[...] = m
-    acc_sc[...] = jnp.dot(p.astype(jnp.bfloat16), vn_ref[...], preferred_element_type=jnp.float32)
-    limit = count * PAGE_CHUNK
-
-    def visit(i, carry):
-        first = pl.multiple_of(i * chunk, chunk)
-        k = k_ref[pl.ds(first, chunk), :]
-        vv = v_ref[pl.ds(first, chunk), :]
-        s = lax.dot_general(q_sc[...], k, contract, preferred_element_type=jnp.float32) * scaling
-        key_ids = first + lax.broadcasted_iota(jnp.int32, s.shape, 1)
-        s = jnp.where(key_ids < limit, s, -jnp.inf)
-        m_old = m_sc[...]
-        m_new = jnp.maximum(m_old, jnp.max(s, axis=1, keepdims=True))
-        factor = jnp.exp(m_old - m_new)
-        p = jnp.exp(s - m_new)
-        l_sc[...] = l_sc[...] * factor + jnp.sum(p, axis=1, keepdims=True)
-        acc_sc[...] = acc_sc[...] * factor + jnp.dot(
-            p.astype(jnp.bfloat16), vv, preferred_element_type=jnp.float32
+    lanes = HEAD_SIZE
+
+    def absorb(qg, k, v):
+        s = lax.dot_general(qg, k, contract, preferred_element_type=jnp.float32) * scaling
+        m_prev = m_sc[...]
+        m_next = jnp.maximum(m_prev, jnp.max(s, axis=1, keepdims=True))
+        repeat = s.shape[1] // lanes
+        wide = m_next if repeat == 1 else jnp.concatenate([m_next] * repeat, axis=1)
+        p = jnp.exp(s - wide)
+        alpha = jnp.exp(m_prev - m_next)
+        l_sc[...] = alpha * l_sc[...] + jnp.sum(p, axis=1, keepdims=True)
+        acc_sc[...] = acc_sc[...] * alpha + jnp.dot(
+            p.astype(jnp.bfloat16), v, preferred_element_type=jnp.float32
         )
-        m_sc[...] = m_new
-        return carry
-
-    lax.fori_loop(0, (count + 1) // 2, visit, 0)
-    res = acc_sc[...] / l_sc[...]
-    o_ref[...] = jnp.concatenate(
-        [res[g * tokens : (g + 1) * tokens] for g in range(group)], axis=1
-    ).astype(jnp.bfloat16)
+        m_sc[...] = m_next
+
+    for b in range(group // STACK):
+        qg = jnp.concatenate(
+            [q_ref[:, g * HEAD_SIZE : (g + 1) * HEAD_SIZE] for g in range(b * STACK, (b + 1) * STACK)],
+            axis=0,
+        )
+        s = lax.dot_general(qg, kn_ref[...], contract, preferred_element_type=jnp.float32)
+        s = s * scaling
+        t = lax.broadcasted_iota(jnp.int32, s.shape, 0) % tokens
+        key_pos = lax.broadcasted_iota(jnp.int32, s.shape, 1)
+        s = jnp.where(key_pos <= t + half * tokens, s, -jnp.inf)
+        m = jnp.max(s, axis=1, keepdims=True)
+        p = jnp.exp(s - m)
+        l_sc[...] = jnp.broadcast_to(jnp.sum(p, axis=1, keepdims=True), l_sc.shape)
+        m_sc[...] = jnp.broadcast_to(m, m_sc.shape)
+        acc_sc[...] = jnp.dot(
+            p.astype(jnp.bfloat16), vn_ref[...], preferred_element_type=jnp.float32
+        )
+
+        def visit(i, carry):
+            first = pl.multiple_of(i * (2 * PAGE_CHUNK), 2 * PAGE_CHUNK)
+            absorb(qg, k_ref[pl.ds(first, 2 * PAGE_CHUNK), :], v_ref[pl.ds(first, 2 * PAGE_CHUNK), :])
+            return carry
+
+        lax.fori_loop(0, count // 2, visit, 0)
+
+        @pl.when(count % 2 == 1)
+        def _():
+            first = pl.multiple_of((count - 1) * PAGE_CHUNK, PAGE_CHUNK)
+            absorb(qg, k_ref[pl.ds(first, PAGE_CHUNK), :], v_ref[pl.ds(first, PAGE_CHUNK), :])
+
+        res = (acc_sc[...] / l_sc[...]).astype(jnp.bfloat16)
+        for i in range(STACK):
+            g = b * STACK + i
+            o_ref[:, g * HEAD_SIZE : (g + 1) * HEAD_SIZE] = res[i * tokens : (i + 1) * tokens]
 
 
 def attend(meta, queries, new_keys, new_values, cache_keys, cache_values):
@@ -113,10 +122,9 @@
         ],
         out_specs=pl.BlockSpec((tokens, width), lambda c, m: (0, c)),
         scratch_shapes=[
-            pltpu.VMEM((group * tokens, HEAD_SIZE), jnp.bfloat16),
-            pltpu.VMEM((group * tokens, 1), jnp.float32),
-            pltpu.VMEM((group * tokens, 1), jnp.float32),
-            pltpu.VMEM((group * tokens, HEAD_SIZE), jnp.float32),
+            pltpu.VMEM((STACK * tokens, HEAD_SIZE), jnp.float32),
+            pltpu.VMEM((STACK * tokens, HEAD_SIZE), jnp.float32),
+            pltpu.VMEM((STACK * tokens, HEAD_SIZE), jnp.float32),
         ],
     )
     return pl.pallas_call(

time: 287 us -> 239 us (0.83)
  Pallas kernels: 37.9 us -> 10.1 us
  blocking collectives: 90.8 us -> 73 us
    pallas_call x1, Pallas kernels: 37.9 us -> 10.1 us  [attend(): pl.pallas_call(functools.partial(attention_kernel, group=group, tokens=to...]
    all_to_all x1, blocking collectives: 90.8 us -> 73 us  [on_device(): lax.all_to_all(dispatch, 'req', split_axis=0, concat_axis=0, tiled=True)]
  transfers between devices with their start and end apart: 4 -> 4, of which waited for: 1 -> 1; matrix products, arithmetic and copies ran while one was open for 14% -> 16% of each run, Pallas kernels for 0% -> 0%
where the time goes in v3:
time: 239 us; the launch traced here: 236 us
  blocking collectives  73 us (31%)
  waiting for transfers between devices  57.8 us (24%)
  matrix products  35.4 us (15%)
  local copies, waits for them, and re-layouts  26.3 us (11%)
  other arithmetic  18.8 us (8%)
  Pallas kernels  10.1 us (4%)
  starting transfers between devices  7.66 us (3%)
  between operations  7.4 us (3%)
    all_to_all x1, blocking collectives, on_device(): lax.all_to_all(dispatch, 'req', split_axis=0, concat_axis=0, tiled=True)  73 us
    all_to_all x1, waiting for transfers between devices, on_device(): lax.all_to_all(result, 'req', split_axis=0, concat_axis=0, tiled=True)  57.8 us
    pallas_call x1, Pallas kernels, attend(): pl.pallas_call(functools.partial(attention_kernel, group=group, tokens=to...  10.1 us
    dot_general x1, matrix products, on_device(): jnp.einsum('nekd,edf->nekf', lax.all_to_all(dispatch, 'req', split_axis=0...  7.51 us
    all_to_all x1, starting transfers between devices, on_device(): lax.all_to_all(result, 'req', split_axis=0, concat_axis=0, tiled=True)  5.86 us
    dot_general x1, matrix products, on_device(): jnp.einsum('nekf,efd->nekd', hidden, w_down, preferred_element_type=jnp.f...  5.5 us
    dot_general x1, matrix products, on_device(): jnp.dot(normed, query_key_value_weight, preferred_element_type=jnp.float32)  4.9 us
  transfers between devices with their start and end apart: 4, of which 1 were waited for; matrix products, arithmetic and copies ran while one was open for 16% of the time, Pallas kernels for 0%

profile of v3, /device:TPU:56, one launch (start us, length us, event | category | flops | bytes accessed | tf_op | source)
XLA Modules:
  0.0 236.5 jit_solution(11935826495631413437)
XLA Ops:
  0.7 1.4 dynamic_slice.16
  4.8 4.9 %fusion.16 = f32[256,2048]{1,0:T(8,128)S(1)} fusion(bf16[1536,2048]{1,0:T(8,128)(2,1)} %param.18, bf16[256,1536]{1,0:T(8,128)(2,1)} %param.16, f32[1536]{0:T(1024)} %param.17, f32[256]{0:T(256)S(1)} %add_rsqrt_fusion.1), kind=kOutput, calls=%fused_computation.39 | convolution fusion | flops 1612185600 | bytes 9182208 | tf_op jit(solution)/shard_map/dot_general | solution.py:172
  21.1 2.2 gather_fusion.2
  23.3 3.2 %gather_fusion = bf16[16,128,256]{2,1,0:T(8,128)(2,1)} fusion(bf16[32,128,256]{2,1,0:T(8,128)(2,1)} %param.25, s32[1024]{0:T(1024)S(1)} %pad_clamp_fusion.1), kind=kCustom, calls=%fused_computation.clone | custom fusion | bytes 2097216 | tf_op jit(solution)/shard_map/jit(_take)/gather | solution.py:211
  26.5 3.0 %broadcast_select_fusion = (bf16[16,128,256]{2,1,0:T(8,128)(2,1)}, bf16[16,128,256]{2,1,0:T(8,128)(2,1)}) fusion(bf16[16,128,256]{2,1,0:T(8,128)(2,1)S(1)} %gather_fusion.2, pred[16]{0:T(512)(128)(4,1)S(1)} %get-tuple-element.15, bf16[16,128,256]{2,1,0:T(8,128)(2,1)} %gather_fusion), kind=kLoop, calls=%fused_computation.37 | loop fusion | flops 1048576 | bytes 4194320 | tf_op jit(solution)/shard_map/jit(_take)/select_n | solution.py:212
  31.3 3.1 %copy.51 = f32[256,1536]{0,1:T(8,128)} copy(f32[256,1536]{1,0:T(8,128)} %slice.53) | data formatting | bytes 3145728 | tf_op jit(solution)/shard_map/slice | solution.py:174
  34.4 1.6 subtract_convert_fusion.2
  37.5 2.2 gather_fusion.3
  39.8 3.2 %gather_fusion.1 = bf16[16,128,256]{2,1,0:T(8,128)(2,1)} fusion(bf16[32,128,256]{2,1,0:T(8,128)(2,1)} %param.25, s32[1024]{0:T(1024)S(1)} %pad_clamp_fusion), kind=kCustom, calls=%fused_computation.1.clone | custom fusion | bytes 2097216 | tf_op jit(solution)/shard_map/jit(_take)/gather | solution.py:220
  42.9 2.3 copy.54.q_ref
  50.8 2.6 %fusion = pred[1536,256]{1,0:T(8,128)(4,1)} fusion(s32[256,4]{0,1:T(4,128)S(1)} %multiply_add_fusion), kind=kLoop, calls=%fused_computation.8 | loop fusion | flops 2752512 | bytes 397312 | tf_op jit(solution)/shard_map/reduce_or | solution.py:258
  55.5 1.7 select_select_fusion
  57.2 10.1 %shard_map.149 = bf16[256,1536]{1,0:T(8,128)(2,1)} custom-call(s32[2]{0:T(128)} %pad_add_fusion.meta_ref, bf16[256,1536]{1,0:T(8,128)(2,1)} %copy.54.q_ref, bf16[512,256]{1,0:T(8,128)(2,1)} %get-tuple-element.10.kn_ref, bf16[512,256]{1,0:T(8,128)(2,1)} %get-tuple-element.9.vn_ref, bf16[2048,256]{1,0:T(8,128)(2,1)} %bitcast.59, bf16[2048,256]{1,0:T(8,128)(2,1)} %bitcast.58), custom_call_target="tpu_custom_call" | custom-call | tf_op jit(solution)/shard_map/pallas_call | solution.py:130
  67.4 4.2 %multiply_reduce_fusion = (f32[256]{0:T(256)S(1)}, f32[256,1536]{1,0:T(8,128)S(1)}) fusion(bf16[256,1536]{1,0:T(8,128)(2,1)} %shard_map.149, bf16[1536,1536]{1,0:T(8,128)(2,1)} %param.19, bf16[256,1536]{1,0:T(8,128)(2,1)S(1)} %copy-done.9), kind=kOutput, calls=%fused_computation.32 | convolution fusion | flops 1209532160 | bytes 7865344 | tf_op jit(solution)/shard_map/dot_general | solution.py:230
  71.6 1.5 convolution_convert_fusion
  73.1 73.0 %all_to_all.10 = bf16[32,1,48,1536]{3,2,1,0:T(8,128)(2,1)S(1)} all-to-all(bf16[32,1,48,1536]{3,2,1,0:T(8,128)(2,1)S(1)} %bitcast.56), channel_id=1, replica_groups=mesh['req'=32,'head'=4] {'req'}, dimensions={0} | all-to-all | bytes 9437184 | tf_op jit(solution)/shard_map/all_to_all | solution.py:265
  146.2 7.5 %convolution_bitcast_fusion = f32[32,1,48,1536]{3,2,0,1:T(8,128)S(1)} fusion(bf16[1,1536,1536]{2,1,0:T(8,128)(2,1)S(1)} %bitcast.65, bf16[32,1,48,1536]{3,2,1,0:T(8,128)(2,1)S(1)} %all_to_all.10), kind=kOutput, calls=%fused_computation.9 | convolution fusion | flops 7247757312 | bytes 18874368 | tf_op jit(solution)/shard_map/nekd,edf->nekf/dot_general | solution.py:263
  153.7 5.5 %convert_bitcast_fusion = bf16[32,1,48,1536]{3,2,1,0:T(8,128)(2,1)} fusion(f32[32,1,48,1536]{3,2,0,1:T(8,128)S(1)} %convolution_bitcast_fusion, bf16[1,768,1536]{2,1,0:T(8,128)(2,1)S(1)} %copy-done), kind=kOutput, calls=%fused_computation.15 | convolution fusion | flops 3629776896 | bytes 16515072 | tf_op jit(solution)/shard_map/nekf,efd->nekd/dot_general | solution.py:270
  159.2 5.9 %all-to-all-start.1 = ((bf16[32,1,48,1536]{3,2,1,0:T(8,128)(2,1)}), bf16[32,1,48,1536]{3,2,1,0:T(8,128)(2,1)}, u32[]{:S(2)}, u32[]{:S(2)}) async-start(bf16[32,1,48,1536]{3,2,1,0:T(8,128)(2,1)} %convert_bitcast_fusion), calls=%async_computation.1 | async-start | bytes 9437184 | tf_op jit(solution)/shard_map/all_to_all | solution.py:273
  165.1 2.2 fusion.27
  167.4 2.2 select_reduce_fusion
  169.6 57.8 %all-to-all-done.1 = bf16[32,1,48,1536]{3,2,1,0:T(8,128)(2,1)} async-done(((bf16[32,1,48,1536]{3,2,1,0:T(8,128)(2,1)}), bf16[32,1,48,1536]{3,2,1,0:T(8,128)(2,1)}, u32[]{:S(2)}, u32[]{:S(2)}) %all-to-all-start.1) | async-done | bytes 4718624 | tf_op jit(solution)/shard_map/all_to_all | solution.py:273
  227.4 4.3 %fusion.21 = f32[256,1536]{1,0:T(8,128)S(1)} fusion(bf16[1536,1536]{1,0:T(8,128)(2,1)} %bitcast.26, f32[256,1536]{1,0:T(8,128)} %select_reduce_fusion), kind=kOutput, calls=%fused_computation.47 | convolution fusion | flops 1208352768 | bytes 7864320 | tf_op jit(solution)/shard_map/dot_general | solution.py:280
  231.8 4.7 %fusion.6 = bf16[256,1536]{1,0:T(8,128)(2,1)} fusion(f32[256,1536]{1,0:T(8,128)S(1)} %copy-done.2, f32[256,1536]{1,0:T(8,128)S(1)} %fusion.21, bf16[1536,1536]{1,0:T(8,128)(2,1)} %bitcast.26, f32[256,1536]{1,0:T(8,128)S(1)} %copy-done.7), kind=kOutput, calls=%fused_computation.21 | convolution fusion | flops 1210712064 | bytes 10223616 | tf_op jit(solution)/shard_map/dot_general | solution.py:280
  (86 shorter events, 18.7 us)
Async XLA Ops:
  0.6 153.1 %copy-start = (bf16[1,768,1536]{2,1,0:T(8,128)(2,1)S(1)}, bf16[1,768,1536]{2,1,0:T(8,128)(2,1)}, u32[]{:S(2)}) copy-start(bf16[1,768,1536]{2,1,0:T(8,128)(2,1)} %param.23) | copy-start | bytes 7077892
  4.8 7.0 %copy-start.19 = (s32[64]{0:T(128)S(1)}, s32[64]{0:T(128)}, u32[]{:S(2)}) copy-start(s32[64]{0:T(128)} %param.28) | copy-start | bytes 772
  9.7 8.7 %copy-start.18 = (s32[64]{0:T(128)S(1)}, s32[64]{0:T(128)}, u32[]{:S(2)}) copy-start(s32[64]{0:T(128)} %param.29) | copy-start | bytes 772
  9.7 11.4 %copy-start.17 = (s32[2,16]{1,0:T(2,128)S(1)}, s32[2,16]{1,0:T(2,128)}, u32[]{:S(2)}) copy-start(s32[2,16]{1,0:T(2,128)} %param.27) | copy-start | bytes 388
  13.3 7.7 %copy-start.10 = (f32[256,64]{0,1:T(8,128)}, f32[256,64]{0,1:T(8,128)S(1)}, u32[]{:S(2)}) copy-start(f32[256,64]{0,1:T(8,128)S(1)} %get-tuple-element.13) | copy-start | bytes 196612
  13.4 7.7 %copy-start.12 = (f32[256,64]{0,1:T(8,128)}, f32[256,64]{0,1:T(8,128)S(1)}, u32[]{:S(2)}) copy-start(f32[256,64]{0,1:T(8,128)S(1)} %get-tuple-element.14) | copy-start | bytes 196612
  15.8 37.5 %collective-permute-start = (bf16[256,512]{1,0:T(8,128)(2,1)}, bf16[256,512]{1,0:T(8,128)(2,1)}, u32[]{:S(2)}, u32[]{:S(2)}) collective-permute-start(bf16[256,512]{1,0:T(8,128)(2,1)} %pad_maximum_fusion.1), channel_id=1, source_target_pairs={{0,1},{2,3},{4,5},{6,7},{8,9},{10,11},{12,13},{14,15},{16,17},{18,... | collective-permute-start | bytes 786440 | tf_op jit(solution)/shard_map/ppermute | solution.py:195
  26.5 3.5 %copy-start.6 = (f32[256,2048]{1,0:T(8,128)S(1)}, f32[256,2048]{1,0:T(8,128)}, u32[]{:S(2)}) copy-start(f32[256,2048]{1,0:T(8,128)} %copy-done.5) | copy-start | bytes 6291460
  29.5 26.0 %collective-permute-start.2 = (bf16[16,128,256]{2,1,0:T(8,128)(2,1)}, bf16[16,128,256]{2,1,0:T(8,128)(2,1)}, u32[]{:S(2)}, u32[]{:S(2)}) collective-permute-start(bf16[16,128,256]{2,1,0:T(8,128)(2,1)} %get-tuple-element.19), channel_id=1, source_target_pairs={{0,4},{4,0},{8,12},{12,8},{16,20},{20,16},{24,28},{28,24},{32,36},... | collective-permute-start | bytes 3145736 | tf_op jit(solution)/shard_map/ppermute | solution.py:215
  29.5 26.0 %collective-permute-start.1 = (bf16[16,128,256]{2,1,0:T(8,128)(2,1)}, bf16[16,128,256]{2,1,0:T(8,128)(2,1)}, u32[]{:S(2)}, u32[]{:S(2)}) collective-permute-start(bf16[16,128,256]{2,1,0:T(8,128)(2,1)} %get-tuple-element.20), channel_id=1, source_target_pairs={{0,4},{4,0},{8,12},{12,8},{16,20},{20,16},{24,28},{28,24},{32,36},... | collective-permute-start | bytes 3145736 | tf_op jit(solution)/shard_map/ppermute | solution.py:215
  31.3 3.1 %copy-start.11 = (f32[256,64]{0,1:T(8,128)S(1)}, f32[256,64]{0,1:T(8,128)}, u32[]{:S(2)}) copy-start(f32[256,64]{0,1:T(8,128)} %copy-done.10) | copy-start | bytes 196612
  31.3 3.1 %copy-start.13 = (f32[256,64]{0,1:T(8,128)S(1)}, f32[256,64]{0,1:T(8,128)}, u32[]{:S(2)}) copy-start(f32[256,64]{0,1:T(8,128)} %copy-done.12) | copy-start | bytes 196612
  39.8 5.5 %copy-start.15 = (s32[256,4]{0,1:T(4,128)S(1)}, s32[256,4]{0,1:T(4,128)}, u32[]{:S(2)}) copy-start(s32[256,4]{0,1:T(4,128)} %param.24) | copy-start | bytes 12292
  49.4 6.1 %copy-start.3 = (bf16[16,128,256]{2,1,0:T(8,128)(2,1)S(1)}, bf16[16,128,256]{2,1,0:T(8,128)(2,1)}, u32[]{:S(2)}) copy-start(bf16[16,128,256]{2,1,0:T(8,128)(2,1)} %gather_fusion.1) | copy-start | bytes 3145732
  57.2 10.1 %copy-start.9 = (bf16[256,1536]{1,0:T(8,128)(2,1)S(1)}, bf16[256,1536]{1,0:T(8,128)(2,1)}, u32[]{:S(2)}) copy-start(bf16[256,1536]{1,0:T(8,128)(2,1)} %param.16) | copy-start | bytes 2359300
  67.3 4.2 %copy-start.4 = (pred[1536,256]{1,0:T(8,128)(4,1)S(1)}, pred[1536,256]{1,0:T(8,128)(4,1)}, u32[]{:S(2)}) copy-start(pred[1536,256]{1,0:T(8,128)(4,1)} %fusion) | copy-start | bytes 1179652
  67.3 4.3 %copy-start.16 = (f32[1536]{0:T(1024)S(1)}, f32[1536]{0:T(1024)}, u32[]{:S(2)}) copy-start(f32[1536]{0:T(1024)} %param.20) | copy-start | bytes 18436
  67.4 78.8 %slice-start = ((s8[4718592]{0:T(1024)(128)(4,1)}), s8[4194304]{0:T(1024)(128)(4,1)S(1)}, s32[]{:S(2)}) async-start(s8[4718592]{0:T(1024)(128)(4,1)} %bitcast.64), calls=%async_computation.2 | async-start | bytes 8388608
  71.6 1.5 copy-start.1
  71.6 74.6 %slice-start.1 = ((s8[4718592]{0:T(1024)(128)(4,1)}), s8[524288]{0:T(1024)(128)(4,1)S(1)}, s32[]{:S(2)}) async-start(s8[4718592]{0:T(1024)(128)(4,1)} %bitcast.64), calls=%async_computation.3 | async-start | bytes 1048576
  159.2 5.9 %copy-start.14 = (f32[1536,32]{0,1:T(8,128)S(1)}, f32[1536,32]{0,1:T(8,128)}, u32[]{:S(2)}) copy-start(f32[1536,32]{0,1:T(8,128)} %param.21) | copy-start | bytes 589828
  159.2 68.2 %all-to-all-start.1 = ((bf16[32,1,48,1536]{3,2,1,0:T(8,128)(2,1)}), bf16[32,1,48,1536]{3,2,1,0:T(8,128)(2,1)}, u32[]{:S(2)}, u32[]{:S(2)}) async-start(bf16[32,1,48,1536]{3,2,1,0:T(8,128)(2,1)} %convert_bitcast_fusion), calls=%async_computation.1 | async-start | bytes 9437184 | tf_op jit(solution)/shard_map/all_to_all | solution.py:273
  227.4 4.3 %copy-start.2 = (f32[256,1536]{1,0:T(8,128)S(1)}, f32[256,1536]{1,0:T(8,128)}, u32[]{:S(2)}) copy-start(f32[256,1536]{1,0:T(8,128)} %copy-done.1) | copy-start | bytes 4718596
  227.4 4.4 %copy-start.7 = (f32[256,1536]{1,0:T(8,128)S(1)}, f32[256,1536]{1,0:T(8,128)}, u32[]{:S(2)}) copy-start(f32[256,1536]{1,0:T(8,128)} %select_reduce_fusion) | copy-start | bytes 4718596
  (2 other events, 2.0 us)

commit v4 on v3

--- a/solution.py
+++ b/solution.py
@@ -15,7 +15,6 @@
 TOPK = 4
 REQUEST_TOKENS = 512
 PAGE_CHUNK = 128
-STACK = 6
 
 
 EPS = 1e-06
@@ -46,13 +45,40 @@
 
 
 def attention_kernel(
-    meta_ref, q_ref, kn_ref, vn_ref, k_ref, v_ref, o_ref, m_sc, l_sc, acc_sc, *, group, tokens
+    meta_ref, page_ref, q_ref, kn_ref, vn_ref, k_own, v_own, k_got, v_got,
+    o_ref, k_buf, v_buf, sems, m_sc, l_sc, acc_sc, *, group, tokens
 ):
     count = meta_ref[0]
     half = meta_ref[1]
+    moved = meta_ref[2]
     scaling = HEAD_SIZE ** (-0.5)
     contract = (((1,), (1,)), ((), ()))
     lanes = HEAD_SIZE
+
+    def page_copies(c, j, k_pool, v_pool):
+        page = page_ref[j]
+        rows = pl.ds(pl.multiple_of(j * PAGE_CHUNK, PAGE_CHUNK), PAGE_CHUNK)
+        cols = pl.ds(c * HEAD_SIZE, HEAD_SIZE)
+        return (
+            pltpu.make_async_copy(k_pool.at[page, :, cols], k_buf.at[c, rows, :], sems.at[0, c, j]),
+            pltpu.make_async_copy(v_pool.at[page, :, cols], v_buf.at[c, rows, :], sems.at[1, c, j]),
+        )
+
+    def start_all(k_pool, v_pool):
+        for c in range(KEY_VALUE_HEADS):
+            def body(j, carry):
+                for copy in page_copies(c, j, k_pool, v_pool):
+                    copy.start()
+                return carry
+            lax.fori_loop(0, count, body, 0)
+
+    @pl.when(moved == 1)
+    def _():
+        start_all(k_got, v_got)
+
+    @pl.when(moved == 0)
+    def _():
+        start_all(k_own, v_own)
 
     def absorb(qg, k, v):
         s = lax.dot_general(qg, k, contract, preferred_element_type=jnp.float32) * scaling
@@ -68,12 +94,14 @@
         )
         m_sc[...] = m_next
 
-    for b in range(group // STACK):
+    for c in range(KEY_VALUE_HEADS):
+        heads = range(c * group, (c + 1) * group)
         qg = jnp.concatenate(
-            [q_ref[:, g * HEAD_SIZE : (g + 1) * HEAD_SIZE] for g in range(b * STACK, (b + 1) * STACK)],
-            axis=0,
+            [q_ref[:, g * HEAD_SIZE : (g + 1) * HEAD_SIZE] for g in heads], axis=0
         )
-        s = lax.dot_general(qg, kn_ref[...], contract, preferred_element_type=jnp.float32)
+        kn = kn_ref[:, c * HEAD_SIZE : (c + 1) * HEAD_SIZE]
+        vn = vn_ref[:, c * HEAD_SIZE : (c + 1) * HEAD_SIZE]
+        s = lax.dot_general(qg, kn, contract, preferred_element_type=jnp.float32)
         s = s * scaling
         t = lax.broadcasted_iota(jnp.int32, s.shape, 0) % tokens
         key_pos = lax.broadcasted_iota(jnp.int32, s.shape, 1)
@@ -82,13 +110,22 @@
         p = jnp.exp(s - m)
         l_sc[...] = jnp.broadcast_to(jnp.sum(p, axis=1, keepdims=True), l_sc.shape)
         m_sc[...] = jnp.broadcast_to(m, m_sc.shape)
-        acc_sc[...] = jnp.dot(
-            p.astype(jnp.bfloat16), vn_ref[...], preferred_element_type=jnp.float32
-        )
+        acc_sc[...] = jnp.dot(p.astype(jnp.bfloat16), vn, preferred_element_type=jnp.float32)
+
+        def wait_page(j, carry):
+            for copy in page_copies(c, j, k_own, v_own):
+                copy.wait()
+            return carry
+
+        lax.fori_loop(0, count, wait_page, 0)
 
         def visit(i, carry):
             first = pl.multiple_of(i * (2 * PAGE_CHUNK), 2 * PAGE_CHUNK)
-            absorb(qg, k_ref[pl.ds(first, 2 * PAGE_CHUNK), :], v_ref[pl.ds(first, 2 * PAGE_CHUNK), :])
+            absorb(
+                qg,
+                k_buf[c, pl.ds(first, 2 * PAGE_CHUNK), :],
+                v_buf[c, pl.ds(first, 2 * PAGE_CHUNK), :],
+            )
             return carry
 
         lax.fori_loop(0, count // 2, visit, 0)
@@ -96,43 +133,49 @@
         @pl.when(count % 2 == 1)
         def _():
             first = pl.multiple_of((count - 1) * PAGE_CHUNK, PAGE_CHUNK)
-            absorb(qg, k_ref[pl.ds(first, PAGE_CHUNK), :], v_ref[pl.ds(first, PAGE_CHUNK), :])
+            absorb(
+                qg,
+                k_buf[c, pl.ds(first, PAGE_CHUNK), :],
+                v_buf[c, pl.ds(first, PAGE_CHUNK), :],
+            )
 
         res = (acc_sc[...] / l_sc[...]).astype(jnp.bfloat16)
-        for i in range(STACK):
-            g = b * STACK + i
+        for i, g in enumerate(heads):
             o_ref[:, g * HEAD_SIZE : (g + 1) * HEAD_SIZE] = res[i * tokens : (i + 1) * tokens]
 
 
-def attend(meta, queries, new_keys, new_values, cache_keys, cache_values):
+def attend(meta, page_ids, queries, new_keys, new_values, k_own, v_own, k_got, v_got):
     tokens = queries.shape[0]
     group = QUERY_HEADS // KEY_VALUE_HEADS
-    width = group * HEAD_SIZE
-    span = new_keys.shape[0]
-    cache_rows = cache_keys.shape[0]
-    grid_spec = pltpu.PrefetchScalarGridSpec(
-        num_scalar_prefetch=1,
-        grid=(KEY_VALUE_HEADS,),
-        in_specs=[
-            pl.BlockSpec((tokens, width), lambda c, m: (0, c)),
-            pl.BlockSpec((span, HEAD_SIZE), lambda c, m: (0, c)),
-            pl.BlockSpec((span, HEAD_SIZE), lambda c, m: (0, c)),
-            pl.BlockSpec((cache_rows, HEAD_SIZE), lambda c, m: (0, c)),
-            pl.BlockSpec((cache_rows, HEAD_SIZE), lambda c, m: (0, c)),
-        ],
-        out_specs=pl.BlockSpec((tokens, width), lambda c, m: (0, c)),
-        scratch_shapes=[
-            pltpu.VMEM((STACK * tokens, HEAD_SIZE), jnp.float32),
-            pltpu.VMEM((STACK * tokens, HEAD_SIZE), jnp.float32),
-            pltpu.VMEM((STACK * tokens, HEAD_SIZE), jnp.float32),
-        ],
-    )
+    max_pages = page_ids.shape[0]
+    cache_rows = max_pages * PAGE_CHUNK
+    smem = pltpu.MemorySpace.SMEM if hasattr(pltpu, "MemorySpace") else pltpu.SMEM
+    vmem_spec = pl.BlockSpec(memory_space=pltpu.VMEM)
+    any_spec = pl.BlockSpec(memory_space=pl.ANY)
     return pl.pallas_call(
         functools.partial(attention_kernel, group=group, tokens=tokens),
-        grid_spec=grid_spec,
+        in_specs=[
+            pl.BlockSpec(memory_space=smem),
+            pl.BlockSpec(memory_space=smem),
+            vmem_spec,
+            vmem_spec,
+            vmem_spec,
+            any_spec,
+            any_spec,
+            any_spec,
+            any_spec,
+        ],
+        out_specs=vmem_spec,
         out_shape=jax.ShapeDtypeStruct((tokens, QUERY_HEADS * HEAD_SIZE), jnp.bfloat16),
-        compiler_params=pltpu.CompilerParams(dimension_semantics=("arbitrary",)),
-    )(meta, queries, new_keys, new_values, cache_keys, cache_values)
+        scratch_shapes=[
+            pltpu.VMEM((KEY_VALUE_HEADS, cache_rows, HEAD_SIZE), jnp.bfloat16),
+            pltpu.VMEM((KEY_VALUE_HEADS, cache_rows, HEAD_SIZE), jnp.bfloat16),
+            pltpu.SemaphoreType.DMA((2, KEY_VALUE_HEADS, max_pages)),
+            pltpu.VMEM((group * tokens, HEAD_SIZE), jnp.float32),
+            pltpu.VMEM((group * tokens, HEAD_SIZE), jnp.float32),
+            pltpu.VMEM((group * tokens, HEAD_SIZE), jnp.float32),
+        ],
+    )(meta, page_ids, queries, new_keys, new_values, k_own, v_own, k_got, v_got)
 
 
 def on_device(
@@ -163,7 +206,6 @@
 
     request = (req_index * count_of_heads + head_index) // share
     half = head_index % share
-    slot = request % req_dev
     old_id = anchor[request]
     place = half * tokens_per_device + jnp.arange(tokens_per_device, dtype=jnp.int32)
     token_positions = cached_pages[old_id] * page_size + place
@@ -202,30 +244,19 @@
     new_keys = span_rows[:, :kv_width]
     new_values = span_rows[:, kv_width:]
 
-    partner = req_index ^ 1
-    partner_anchor = lax.dynamic_slice_in_dim(anchor, partner * req_dev, req_dev, 0)
-    leaving = partner_anchor // req_dev == req_index
-    out_row = jnp.sum(jnp.where(leaving, partner_anchor, 0)) % req_dev
-    sent_pages = page_table[out_row]
-    sent = (
-        jnp.take(key_page_store, sent_pages, axis=0),
-        jnp.take(value_page_store, sent_pages, axis=0),
-    )
     pairs = [(source, source ^ 1) for source in range(req_count)]
-    k_got, v_got = lax.ppermute(sent, "req", pairs)
-
+    k_got, v_got, table_got = lax.ppermute(
+        (key_page_store, value_page_store, page_table), "req", pairs
+    )
     moved_in = old_id // req_dev != req_index
-    page_ids = page_table[old_id % req_dev]
-    cache_rows = page_ids.shape[0] * page_size
-    cache_keys = jnp.where(moved_in, k_got, jnp.take(key_page_store, page_ids, axis=0))
-    cache_values = jnp.where(moved_in, v_got, jnp.take(value_page_store, page_ids, axis=0))
-    meta = jnp.stack([cached_pages[old_id], half.astype(jnp.int32)]).astype(jnp.int32)
+    page_ids = jnp.where(moved_in, table_got[old_id % req_dev], page_table[old_id % req_dev])
+    meta = jnp.stack(
+        [cached_pages[old_id], half.astype(jnp.int32), moved_in.astype(jnp.int32)]
+    ).astype(jnp.int32)
     attention = attend(
-        meta, queries.reshape(tokens_per_device, QUERY_HEADS * HEAD_SIZE),
-        new_keys, new_values,
-        cache_keys.reshape(cache_rows, kv_width), cache_values.reshape(cache_rows, kv_width),
-    )
-    del slot
+        meta, page_ids, queries.reshape(tokens_per_device, QUERY_HEADS * HEAD_SIZE),
+        new_keys, new_values, key_page_store, value_page_store, k_got, v_got,
+    )
 
     residual = tokens.astype(jnp.float32) + jnp.dot(
         attention, w_out, preferred_element_type=jnp.float32

time: 239 us -> 219 us (0.916)
  the two profiles are of different devices: /device:TPU:56 before, /device:TPU:32 now
where the time goes in v4:
time: 219 us; the launch traced here: 218 us
  blocking collectives  71.8 us (33%)
  waiting for transfers between devices  57.7 us (26%)
  matrix products  35.4 us (16%)
  other arithmetic  14.3 us (7%)
  local copies, waits for them, and re-layouts  12.8 us (6%)
  starting transfers between devices  10.7 us (5%)
  Pallas kernels  10.2 us (5%)
  between operations  5.55 us (3%)
    all_to_all x1, blocking collectives, on_device(): lax.all_to_all(dispatch, 'req', split_axis=0, concat_axis=0, tiled=True)  71.8 us
    all_to_all x1, waiting for transfers between devices, on_device(): lax.all_to_all(result, 'req', split_axis=0, concat_axis=0, tiled=True)  57.7 us
    pallas_call x1, Pallas kernels, attend(): pl.pallas_call(functools.partial(attention_kernel, group=group, tokens=to...  10.2 us
    dot_general x1, matrix products, on_device(): jnp.einsum('nekd,edf->nekf', lax.all_to_all(dispatch, 'req', split_axis=0...  7.51 us
    all_to_all x1, starting transfers between devices, on_device(): lax.all_to_all(result, 'req', split_axis=0, concat_axis=0, tiled=True)  5.86 us
    slice x2, local copies, waits for them, and re-layouts, on_device(): projected_rows[:, :QUERY_HEADS * HEAD_SIZE]  5.73 us
    dot_general x1, matrix products, on_device(): jnp.einsum('nekf,efd->nekd', hidden, w_down, preferred_element_type=jnp.f...  5.48 us
    dot_general x1, matrix products, on_device(): jnp.dot(normed, query_key_value_weight, preferred_element_type=jnp.float32)  4.9 us
  transfers between devices with their start and end apart: 5, of which 1 were waited for; matrix products, arithmetic and copies ran while one was open for 15% of the time, Pallas kernels for 0%

profile of v4, /device:TPU:32, one launch (start us, length us, event | category | flops | bytes accessed | tf_op | source)
XLA Modules:
  0.0 218.5 jit_solution(3750569174660909535)
XLA Ops:
  1.3 1.3 dynamic_slice.13
  3.9 1.4 fusion.11
  5.9 1.3 dynamic_slice.14
  7.9 4.9 %fusion.16 = f32[256,2048]{1,0:T(8,128)S(1)} fusion(bf16[1536,2048]{1,0:T(8,128)(2,1)} %param.16, bf16[256,1536]{1,0:T(8,128)(2,1)} %param.14, f32[1536]{0:T(1024)} %param.15, f32[256]{0:T(256)S(1)} %add_rsqrt_fusion.1), kind=kOutput, calls=%fused_computation.31 | convolution fusion | flops 1612185600 | bytes 9182208 | tf_op jit(solution)/shard_map/dot_general | solution.py:214
  16.8 4.2 %collective-permute-start.1 = (bf16[256,512]{1,0:T(8,128)(2,1)}, bf16[256,512]{1,0:T(8,128)(2,1)}, u32[]{:S(2)}, u32[]{:S(2)}) collective-permute-start(bf16[256,512]{1,0:T(8,128)(2,1)} %pad_maximum_fusion.1), channel_id=1, source_target_pairs={{0,1},{2,3},{4,5},{6,7},{8,9},{10,11},{12,13},{14,15},{16,17},{18,... | collective-permute-start | bytes 786440 | tf_op jit(solution)/shard_map/ppermute | solution.py:237
  22.9 2.7 %slice.45 = f32[256,1536]{1,0:T(8,128)} slice(f32[256,2048]{1,0:T(8,128)} %copy-done.3), slice={[0:256], [0:1536]} | slice | bytes 3145728 | tf_op jit(solution)/shard_map/slice | solution.py:216
  25.6 3.1 %copy.51 = f32[256,1536]{0,1:T(8,128)} copy(f32[256,1536]{1,0:T(8,128)} %slice.45) | data formatting | bytes 3145728 | tf_op jit(solution)/shard_map/slice | solution.py:216
  29.7 1.8 fusion
  31.5 2.5 %subtract_convert_fusion.2 = (bf16[256,12,64]{0,2,1:T(8,128)(2,1)}, bf16[256,12,64]{0,2,1:T(8,128)(2,1)}) fusion(f32[256,12,128]{0,2,1:T(8,128)} %bitcast.52, f32[256,64]{0,1:T(8,128)S(1)} %get-tuple-element.9, f32[256,64]{0,1:T(8,128)S(1)} %get-tuple-element.8), kind=kLoop, calls=%fused_computation.34 | loop fusion | flops 1572864 | bytes 2490368 | tf_op jit(solution)/shard_map/convert.4
  34.0 1.3 pad_add_fusion.meta_ref
  35.3 1.2 pad_maximum_fusion
  38.2 1.4 maximum_select_fusion
  40.5 10.2 %shard_map.149 = bf16[256,1536]{1,0:T(8,128)(2,1)} custom-call(s32[3]{0:T(128)} %pad_add_fusion.meta_ref, s32[16]{0:T(128)} %fusion.25.page_ref, bf16[256,1536]{1,0:T(8,128)(2,1)} %copy.54.q_ref, bf16[512,256]{1,0:T(8,128)(2,1)} %get-tuple-element.5.kn_ref, bf16[512,256]{1,0:T(8,128)(2,1)} %get-tuple-element.4.vn_ref, bf16[32,128,256]{2,1,0:T(8,128)(2,1)} %k_own.1, ...), custom_call_target="tpu_custom_call" | custom-call | tf_op jit(solution)/shard_map/pallas_call | solution.py:155
  50.7 4.2 %multiply_reduce_fusion = (f32[256]{0:T(256)S(1)}, f32[256,1536]{1,0:T(8,128)S(1)}) fusion(bf16[256,1536]{1,0:T(8,128)(2,1)} %shard_map.149, bf16[1536,1536]{1,0:T(8,128)(2,1)} %param.17, bf16[256,1536]{1,0:T(8,128)(2,1)S(1)} %copy-done.7), kind=kOutput, calls=%fused_computation.28 | convolution fusion | flops 1209532160 | bytes 7865344 | tf_op jit(solution)/shard_map/dot_general | solution.py:261
  55.0 1.5 convolution_convert_fusion
  56.5 71.8 %all_to_all.10 = bf16[32,1,48,1536]{3,2,1,0:T(8,128)(2,1)S(1)} all-to-all(bf16[32,1,48,1536]{3,2,1,0:T(8,128)(2,1)S(1)} %bitcast.51), channel_id=1, replica_groups=mesh['req'=32,'head'=4] {'req'}, dimensions={0} | all-to-all | bytes 9437184 | tf_op jit(solution)/shard_map/all_to_all | solution.py:296
  128.2 7.5 %convolution_bitcast_fusion = f32[32,1,48,1536]{3,2,0,1:T(8,128)S(1)} fusion(bf16[1,1536,1536]{2,1,0:T(8,128)(2,1)S(1)} %bitcast.58, bf16[32,1,48,1536]{3,2,1,0:T(8,128)(2,1)S(1)} %all_to_all.10), kind=kOutput, calls=%fused_computation.5 | convolution fusion | flops 7247757312 | bytes 18874368 | tf_op jit(solution)/shard_map/nekd,edf->nekf/dot_general | solution.py:294
  135.8 5.5 %convert_bitcast_fusion = bf16[32,1,48,1536]{3,2,1,0:T(8,128)(2,1)} fusion(f32[32,1,48,1536]{3,2,0,1:T(8,128)S(1)} %convolution_bitcast_fusion, bf16[1,768,1536]{2,1,0:T(8,128)(2,1)S(1)} %copy-done), kind=kOutput, calls=%fused_computation.11 | convolution fusion | flops 3629776896 | bytes 16515072 | tf_op jit(solution)/shard_map/nekf,efd->nekd/dot_general | solution.py:301
  141.3 5.9 %all-to-all-start.1 = ((bf16[32,1,48,1536]{3,2,1,0:T(8,128)(2,1)}), bf16[32,1,48,1536]{3,2,1,0:T(8,128)(2,1)}, u32[]{:S(2)}, u32[]{:S(2)}) async-start(bf16[32,1,48,1536]{3,2,1,0:T(8,128)(2,1)} %convert_bitcast_fusion), calls=%async_computation.1 | async-start | bytes 9437184 | tf_op jit(solution)/shard_map/all_to_all | solution.py:304
  147.1 2.2 %fusion.27 = f32[256,32]{0,1:T(8,128)S(1)} fusion(f32[1536,32]{0,1:T(8,128)S(1)} %copy-done.8, f32[256,1536]{1,0:T(8,128)} %copy-done.1, f32[1536]{0:T(1024)S(1)} %copy-done.10, f32[256]{0:T(256)S(1)} %add_rsqrt_fusion), kind=kOutput, calls=%fused_computation.66 | convolution fusion | flops 152174592 | bytes 1809408 | tf_op jit(solution)/shard_map/dot_general | solution.py:265
  149.5 2.2 %select_reduce_fusion = f32[256,1536]{1,0:T(8,128)} fusion(f32[256,4]{0,1:T(4,128)S(1)} %multiply_divide_fusion, s32[256,4]{0,1:T(4,128)S(1)} %multiply_add_fusion), kind=kLoop, calls=%fused_computation.2 | loop fusion | flops 4325376 | bytes 1581056 | tf_op jit(solution)/shard_map/reduce_sum | solution.py:308
  151.7 57.7 %all-to-all-done.1 = bf16[32,1,48,1536]{3,2,1,0:T(8,128)(2,1)} async-done(((bf16[32,1,48,1536]{3,2,1,0:T(8,128)(2,1)}), bf16[32,1,48,1536]{3,2,1,0:T(8,128)(2,1)}, u32[]{:S(2)}, u32[]{:S(2)}) %all-to-all-start.1) | async-done | bytes 4718624 | tf_op jit(solution)/shard_map/all_to_all | solution.py:304
  209.4 4.3 %fusion.21 = f32[256,1536]{1,0:T(8,128)S(1)} fusion(bf16[1536,1536]{1,0:T(8,128)(2,1)} %bitcast.24, f32[256,1536]{1,0:T(8,128)} %select_reduce_fusion), kind=kOutput, calls=%fused_computation.39 | convolution fusion | flops 1208352768 | bytes 7864320 | tf_op jit(solution)/shard_map/dot_general | solution.py:311
  213.8 4.7 %fusion.6 = bf16[256,1536]{1,0:T(8,128)(2,1)} fusion(f32[256,1536]{1,0:T(8,128)S(1)} %copy-done.2, f32[256,1536]{1,0:T(8,128)S(1)} %fusion.21, bf16[1536,1536]{1,0:T(8,128)(2,1)} %bitcast.24, f32[256,1536]{1,0:T(8,128)S(1)} %copy-done.4), kind=kOutput, calls=%fused_computation.17 | convolution fusion | flops 1210712064 | bytes 10223616 | tf_op jit(solution)/shard_map/dot_general | solution.py:311
  (63 shorter events, 8.3 us)
Async XLA Ops:
  0.6 135.1 %copy-start = (bf16[1,768,1536]{2,1,0:T(8,128)(2,1)S(1)}, bf16[1,768,1536]{2,1,0:T(8,128)(2,1)}, u32[]{:S(2)}) copy-start(bf16[1,768,1536]{2,1,0:T(8,128)(2,1)} %param.21) | copy-start | bytes 7077892
  0.6 37.0 %collective-permute-start = (s32[2,16]{1,0:T(2,128)}, s32[2,16]{1,0:T(2,128)S(1)}, u32[]{:S(2)}, u32[]{:S(2)}) collective-permute-start(s32[2,16]{1,0:T(2,128)} %param.25), channel_id=1, source_target_pairs={{0,4},{4,0},{8,12},{12,8},{16,20},{20,16},{24,28},{28,24},{32,36},... | collective-permute-start | bytes 392 | tf_op jit(solution)/shard_map/ppermute | solution.py:248
  0.7 39.7 %collective-permute-start.2 = (bf16[32,128,256]{2,1,0:T(8,128)(2,1)}, bf16[32,128,256]{2,1,0:T(8,128)(2,1)}, u32[]{:S(2)}, u32[]{:S(2)}) collective-permute-start(bf16[32,128,256]{2,1,0:T(8,128)(2,1)} %k_own.1), channel_id=1, source_target_pairs={{0,4},{4,0},{8,12},{12,8},{16,20},{20,16},{24,28},{28,24},{32,36},... | collective-permute-start | bytes 6291464 | tf_op jit(solution)/shard_map/ppermute | solution.py:248
  1.2 39.2 %collective-permute-start.3 = (bf16[32,128,256]{2,1,0:T(8,128)(2,1)}, bf16[32,128,256]{2,1,0:T(8,128)(2,1)}, u32[]{:S(2)}, u32[]{:S(2)}) collective-permute-start(bf16[32,128,256]{2,1,0:T(8,128)(2,1)} %v_own.1), channel_id=1, source_target_pairs={{0,4},{4,0},{8,12},{12,8},{16,20},{20,16},{24,28},{28,24},{32,36},... | collective-permute-start | bytes 6291464 | tf_op jit(solution)/shard_map/ppermute | solution.py:248
  12.9 1.3 copy-start.3
  14.2 11.4 %copy-start.5 = (bf16[256,256]{1,0:T(8,128)(2,1)}, bf16[256,256]{1,0:T(8,128)(2,1)S(1)}, u32[]{:S(2)}) copy-start(bf16[256,256]{1,0:T(8,128)(2,1)S(1)} %slice.77) | copy-start | bytes 393220
  15.4 0.7 copy-start.6
  16.8 21.4 %collective-permute-start.1 = (bf16[256,512]{1,0:T(8,128)(2,1)}, bf16[256,512]{1,0:T(8,128)(2,1)}, u32[]{:S(2)}, u32[]{:S(2)}) collective-permute-start(bf16[256,512]{1,0:T(8,128)(2,1)} %pad_maximum_fusion.1), channel_id=1, source_target_pairs={{0,1},{2,3},{4,5},{6,7},{8,9},{10,11},{12,13},{14,15},{16,17},{18,... | collective-permute-start | bytes 786440 | tf_op jit(solution)/shard_map/ppermute | solution.py:237
  25.6 3.1 %copy-start.9 = (s32[256,4]{0,1:T(4,128)S(1)}, s32[256,4]{0,1:T(4,128)}, u32[]{:S(2)}) copy-start(s32[256,4]{0,1:T(4,128)} %param.22) | copy-start | bytes 12292
  31.5 6.1 %copy-start.11 = (s32[2,16]{1,0:T(2,128)S(1)}, s32[2,16]{1,0:T(2,128)}, u32[]{:S(2)}) copy-start(s32[2,16]{1,0:T(2,128)} %param.25) | copy-start | bytes 388
  40.5 10.2 %copy-start.7 = (bf16[256,1536]{1,0:T(8,128)(2,1)S(1)}, bf16[256,1536]{1,0:T(8,128)(2,1)}, u32[]{:S(2)}) copy-start(bf16[256,1536]{1,0:T(8,128)(2,1)} %param.14) | copy-start | bytes 2359300
  50.7 4.2 %copy-start.10 = (f32[1536]{0:T(1024)S(1)}, f32[1536]{0:T(1024)}, u32[]{:S(2)}) copy-start(f32[1536]{0:T(1024)} %param.18) | copy-start | bytes 18436
  50.7 77.5 %slice-start = ((s8[4718592]{0:T(1024)(128)(4,1)}), s8[4194304]{0:T(1024)(128)(4,1)S(1)}, s32[]{:S(2)}) async-start(s8[4718592]{0:T(1024)(128)(4,1)} %bitcast.57), calls=%async_computation.2 | async-start | bytes 8388608
  54.9 1.5 copy-start.1
  55.0 73.3 %slice-start.1 = ((s8[4718592]{0:T(1024)(128)(4,1)}), s8[524288]{0:T(1024)(128)(4,1)S(1)}, s32[]{:S(2)}) async-start(s8[4718592]{0:T(1024)(128)(4,1)} %bitcast.57), calls=%async_computation.3 | async-start | bytes 1048576
  141.3 5.9 %copy-start.8 = (f32[1536,32]{0,1:T(8,128)S(1)}, f32[1536,32]{0,1:T(8,128)}, u32[]{:S(2)}) copy-start(f32[1536,32]{0,1:T(8,128)} %param.19) | copy-start | bytes 589828
  141.3 68.2 %all-to-all-start.1 = ((bf16[32,1,48,1536]{3,2,1,0:T(8,128)(2,1)}), bf16[32,1,48,1536]{3,2,1,0:T(8,128)(2,1)}, u32[]{:S(2)}, u32[]{:S(2)}) async-start(bf16[32,1,48,1536]{3,2,1,0:T(8,128)(2,1)} %convert_bitcast_fusion), calls=%async_computation.1 | async-start | bytes 9437184 | tf_op jit(solution)/shard_map/all_to_all | solution.py:304
  209.4 4.3 %copy-start.2 = (f32[256,1536]{1,0:T(8,128)S(1)}, f32[256,1536]{1,0:T(8,128)}, u32[]{:S(2)}) copy-start(f32[256,1536]{1,0:T(8,128)} %copy-done.1) | copy-start | bytes 4718596
  209.4 4.4 %copy-start.4 = (f32[256,1536]{1,0:T(8,128)S(1)}, f32[256,1536]{1,0:T(8,128)}, u32[]{:S(2)}) copy-start(f32[256,1536]{1,0:T(8,128)} %select_reduce_fusion) | copy-start | bytes 4718596

commit v5 on v4

--- a/solution.py
+++ b/solution.py
@@ -42,6 +42,18 @@
     return jnp.concatenate(
         [first_half * cosine - second * sines, second * cosine + first_half * sines], axis=-1
     )
+
+
+def rotate_flat(values, cosine, sines):
+    half_dim = cosine.shape[1]
+    heads = values.shape[1] // (2 * half_dim)
+    cos_full = jnp.tile(jnp.concatenate([cosine, cosine], axis=1), (1, heads))
+    sin_signed = jnp.tile(jnp.concatenate([-sines, sines], axis=1), (1, heads))
+    parts = []
+    for h in range(heads):
+        base = 2 * half_dim * h
+        parts += [values[:, base + half_dim : base + 2 * half_dim], values[:, base : base + half_dim]]
+    return values * cos_full + jnp.concatenate(parts, axis=1) * sin_signed
 
 
 def attention_kernel(
@@ -99,18 +111,24 @@
         qg = jnp.concatenate(
             [q_ref[:, g * HEAD_SIZE : (g + 1) * HEAD_SIZE] for g in heads], axis=0
         )
-        kn = kn_ref[:, c * HEAD_SIZE : (c + 1) * HEAD_SIZE]
-        vn = vn_ref[:, c * HEAD_SIZE : (c + 1) * HEAD_SIZE]
-        s = lax.dot_general(qg, kn, contract, preferred_element_type=jnp.float32)
+        key_cols = slice(c * HEAD_SIZE, (c + 1) * HEAD_SIZE)
+        value_cols = slice((KEY_VALUE_HEADS + c) * HEAD_SIZE, (KEY_VALUE_HEADS + c + 1) * HEAD_SIZE)
+        s = lax.dot_general(qg, kn_ref[:, key_cols], contract, preferred_element_type=jnp.float32)
         s = s * scaling
         t = lax.broadcasted_iota(jnp.int32, s.shape, 0) % tokens
         key_pos = lax.broadcasted_iota(jnp.int32, s.shape, 1)
-        s = jnp.where(key_pos <= t + half * tokens, s, -jnp.inf)
+        s = jnp.where(key_pos <= t, s, -jnp.inf)
         m = jnp.max(s, axis=1, keepdims=True)
         p = jnp.exp(s - m)
         l_sc[...] = jnp.broadcast_to(jnp.sum(p, axis=1, keepdims=True), l_sc.shape)
         m_sc[...] = jnp.broadcast_to(m, m_sc.shape)
-        acc_sc[...] = jnp.dot(p.astype(jnp.bfloat16), vn, preferred_element_type=jnp.float32)
+        acc_sc[...] = jnp.dot(
+            p.astype(jnp.bfloat16), kn_ref[:, value_cols], preferred_element_type=jnp.float32
+        )
+
+        @pl.when(half == 1)
+        def _():
+            absorb(qg, vn_ref[:, key_cols], vn_ref[:, value_cols])
 
         def wait_page(j, carry):
             for copy in page_copies(c, j, k_own, v_own):
@@ -212,38 +230,29 @@
 
     normed = rms_scale(tokens.astype(jnp.float32), norm1_gain).astype(jnp.bfloat16)
     projected_rows = jnp.dot(normed, query_key_value_weight, preferred_element_type=jnp.float32)
-    queries = apply_rotary(
-        projected_rows[:, : QUERY_HEADS * HEAD_SIZE].reshape(
-            tokens_per_device, QUERY_HEADS, HEAD_SIZE
-        ),
-        token_positions,
+    half_dim = HEAD_SIZE // 2
+    frequency = jnp.exp(
+        -jnp.log(jnp.float32(THETA))
+        * jnp.arange(half_dim, dtype=jnp.float32)
+        * 2.0
+        / HEAD_SIZE
+    )
+    angles = token_positions.astype(jnp.float32)[:, None] * frequency[None, :]
+    rotated = rotate_flat(
+        projected_rows[:, : (QUERY_HEADS + KEY_VALUE_HEADS) * HEAD_SIZE],
+        jnp.cos(angles),
+        jnp.sin(angles),
     ).astype(jnp.bfloat16)
-    fresh_keys = apply_rotary(
-        projected_rows[
-            :, QUERY_HEADS * HEAD_SIZE : (QUERY_HEADS + KEY_VALUE_HEADS) * HEAD_SIZE
-        ].reshape(tokens_per_device, KEY_VALUE_HEADS, HEAD_SIZE),
-        token_positions,
-    ).astype(jnp.bfloat16)
+    queries = rotated[:, : QUERY_HEADS * HEAD_SIZE]
     fresh_values = projected_rows[:, (QUERY_HEADS + KEY_VALUE_HEADS) * HEAD_SIZE :].astype(
         jnp.bfloat16
     )
-    appended = jnp.concatenate(
-        [fresh_keys.reshape(tokens_per_device, kv_width), fresh_values], axis=1
-    )
+    appended = jnp.concatenate([rotated[:, QUERY_HEADS * HEAD_SIZE :], fresh_values], axis=1)
 
     forward_pairs = [
         (h, h + 1) for h in range(count_of_heads) if h % share != share - 1
     ]
     earlier = lax.ppermute(appended, "head", forward_pairs)
-    is_second = half == 1
-    span_rows = jnp.where(
-        is_second,
-        jnp.concatenate([earlier, appended], axis=0),
-        jnp.concatenate([appended, earlier], axis=0),
-    )
-    new_keys = span_rows[:, :kv_width]
-    new_values = span_rows[:, kv_width:]
-
     pairs = [(source, source ^ 1) for source in range(req_count)]
     k_got, v_got, table_got = lax.ppermute(
         (key_page_store, value_page_store, page_table), "req", pairs
@@ -254,8 +263,7 @@
         [cached_pages[old_id], half.astype(jnp.int32), moved_in.astype(jnp.int32)]
     ).astype(jnp.int32)
     attention = attend(
-        meta, page_ids, queries.reshape(tokens_per_device, QUERY_HEADS * HEAD_SIZE),
-        new_keys, new_values, key_page_store, value_page_store, k_got, v_got,
+        meta, page_ids, queries, appended, earlier, key_page_store, value_page_store, k_got, v_got,
     )
 
     residual = tokens.astype(jnp.float32) + jnp.dot(
@@ -306,10 +314,8 @@
 
     token_hits = slot_ids[:, :, None] == slot_iota[None, None, :]
     combine = jnp.sum(jnp.where(token_hits, route_gates[:, :, None], 0.0), axis=1)
-    combine_hi = combine.astype(jnp.bfloat16)
-    combine_lo = (combine - combine_hi.astype(jnp.float32)).astype(jnp.bfloat16)
-    expert_sum = jnp.dot(combine_hi, flat_results, preferred_element_type=jnp.float32) + jnp.dot(
-        combine_lo, flat_results, preferred_element_type=jnp.float32
+    expert_sum = jnp.dot(
+        combine.astype(jnp.bfloat16), flat_results, preferred_element_type=jnp.float32
     )
     mixed_out = (residual + expert_sum).astype(jnp.bfloat16)
     return (mixed_out, appended)

time: 219 us -> 222 us (1.014)
  the two profiles are of different devices: /device:TPU:32 before, /device:TPU:56 now
where the time goes in v5:
time: 222 us; the launch traced here: 217 us
  blocking collectives  73.8 us (33%)
  waiting for transfers between devices  58.9 us (27%)
  matrix products  31.2 us (14%)
  local copies, waits for them, and re-layouts  22.9 us (10%)
  other arithmetic  10.5 us (5%)
  starting transfers between devices  7.82 us (4%)
  Pallas kernels  6.48 us (3%)
  between operations  5.8 us (3%)
    all_to_all x1, blocking collectives, on_device(): lax.all_to_all(dispatch, 'req', split_axis=0, concat_axis=0, tiled=True)  73.8 us
    all_to_all x1, waiting for transfers between devices, on_device(): lax.all_to_all(result, 'req', split_axis=0, concat_axis=0, tiled=True)  58.9 us
    dot_general x1, matrix products, on_device(): jnp.einsum('nekd,edf->nekf', lax.all_to_all(dispatch, 'req', split_axis=0...  7.52 us
    pallas_call x1, Pallas kernels, attend(): pl.pallas_call(functools.partial(attention_kernel, group=group, tokens=to...  6.48 us
    all_to_all x1, starting transfers between devices, on_device(): lax.all_to_all(result, 'req', split_axis=0, concat_axis=0, tiled=True)  5.85 us
    dot_general x1, matrix products, on_device(): jnp.einsum('nekf,efd->nekd', hidden, w_down, preferred_element_type=jnp.f...  5.48 us
    dot_general x1, matrix products, on_device(): jnp.dot(combine.astype(jnp.bfloat16), flat_results, preferred_element_typ...  5.1 us
    dot_general x1, matrix products, on_device(): jnp.dot(normed, query_key_value_weight, preferred_element_type=jnp.float32)  4.62 us
  transfers between devices with their start and end apart: 5, of which 1 were waited for; matrix products, arithmetic and copies ran while one was open for 19% of the time, Pallas kernels for 0%

profile of v5, /device:TPU:56, one launch (start us, length us, event | category | flops | bytes accessed | tf_op | source)
XLA Modules:
  0.0 217.3 jit_solution(7092356813571532930)
XLA Ops:
  1.3 1.3 dynamic_slice.13
  4.8 1.3 dynamic_slice.14
  7.1 1.4 tile.8
  8.5 2.7 %copy.45 = f32[256,1792]{1,0:T(8,128)} copy(f32[256,1792]{0,1:T(8,128)} %bitcast.48) | data formatting | bytes 3670016 | tf_op jit(solution)/shard_map/tile | solution.py:50
  11.5 1.4 tile.20
  13.0 2.8 %copy.46 = f32[256,1792]{1,0:T(8,128)} copy(f32[256,1792]{0,1:T(8,128)} %bitcast.49) | data formatting | bytes 3670016 | tf_op jit(solution)/shard_map/tile | solution.py:51
  15.7 4.6 %fusion.17 = f32[256,2048]{1,0:T(8,128)S(1)} fusion(bf16[1536,2048]{1,0:T(8,128)(2,1)} %param.16, bf16[256,1536]{1,0:T(8,128)(2,1)S(1)} %copy-done.5, f32[1536]{0:T(1024)S(1)} %copy-done.12, f32[256]{0:T(256)S(1)} %add_rsqrt_fusion.1), kind=kOutput, calls=%fused_computation.32 | convolution fusion | flops 1612185600 | bytes 9182208 | tf_op jit(solution)/shard_map/dot_general | solution.py:232
  21.3 1.9 fusion.28
  23.3 4.4 %concatenate.13 = f32[256,1792]{1,0:T(8,128)} concatenate(f32[256,64]{1,0:T(8,128)S(1)} %get-tuple-element.29, f32[256,64]{1,0:T(8,128)S(1)} %get-tuple-element.28, f32[256,64]{1,0:T(8,128)S(1)} %get-tuple-element.27, f32[256,64]{1,0:T(8,128)S(1)} %get-tuple-element.26, f32[256,64]{1,0:T(8,128)S(1)} %get-tuple-element.25, f32[256,64]{1,0:T(8,128)S(1)} %get-tuple-element.24, ...), dimensions={1} | concatenate | bytes 3670016 | tf_op jit(solution)/shard_map/concatenate | solution.py:56
  27.7 3.5 %fusion.11 = bf16[256,1792]{1,0:T(8,128)(2,1)S(1)} fusion(f32[256,1792]{1,0:T(8,128)} %copy.45, f32[256,2048]{1,0:T(8,128)} %copy-done.1, f32[256,1792]{1,0:T(8,128)} %concatenate.13, f32[256,1792]{1,0:T(8,128)} %copy.46), kind=kLoop, calls=%fused_computation.24 | loop fusion | flops 1835008 | bytes 8257536 | tf_op jit(solution)/shard_map/convert_element_type | solution.py:245
  31.3 1.3 collective-permute-start.1
  38.8 1.3 pad_add_fusion.meta_ref
  40.2 2.6 %fusion = pred[1536,256]{1,0:T(8,128)(4,1)} fusion(s32[256,4]{0,1:T(4,128)S(1)} %multiply_add_fusion), kind=kLoop, calls=%fused_computation.4 | loop fusion | flops 2752512 | bytes 397312 | tf_op jit(solution)/shard_map/reduce_or | solution.py:297
  43.7 1.2 fusion.25.page_ref
  44.9 6.5 %shard_map.149 = bf16[256,1536]{1,0:T(8,128)(2,1)} custom-call(s32[3]{0:T(128)} %pad_add_fusion.meta_ref, s32[16]{0:T(128)} %fusion.25.page_ref, bf16[256,1536]{1,0:T(8,128)(2,1)} %slice.194.q_ref, bf16[256,512]{1,0:T(8,128)(2,1)} %copy-done.4, bf16[256,512]{1,0:T(8,128)(2,1)} %collective-permute-done.1.vn_ref, bf16[32,128,256]{2,1,0:T(8,128)(2,1)} %k_own.1, ...), custom_call_target="tpu_custom_call" | custom-call | tf_op jit(solution)/shard_map/pallas_call | solution.py:173
  51.5 4.2 %multiply_reduce_fusion = (f32[256]{0:T(256)S(1)}, f32[256,1536]{1,0:T(8,128)S(1)}) fusion(bf16[256,1536]{1,0:T(8,128)(2,1)} %shard_map.149, bf16[1536,1536]{1,0:T(8,128)(2,1)} %param.17, bf16[256,1536]{1,0:T(8,128)(2,1)S(1)} %copy-done.6), kind=kOutput, calls=%fused_computation.29 | convolution fusion | flops 1209532160 | bytes 7865344 | tf_op jit(solution)/shard_map/dot_general | solution.py:269
  55.7 1.5 convolution_convert_fusion
  57.2 73.8 %all_to_all.10 = bf16[32,1,48,1536]{3,2,1,0:T(8,128)(2,1)S(1)} all-to-all(bf16[32,1,48,1536]{3,2,1,0:T(8,128)(2,1)S(1)} %bitcast.47), channel_id=1, replica_groups=mesh['req'=32,'head'=4] {'req'}, dimensions={0} | all-to-all | bytes 9437184 | tf_op jit(solution)/shard_map/all_to_all | solution.py:304
  131.0 7.5 %convolution_bitcast_fusion = f32[32,1,48,1536]{3,2,0,1:T(8,128)S(1)} fusion(bf16[1,1536,1536]{2,1,0:T(8,128)(2,1)S(1)} %bitcast.51, bf16[32,1,48,1536]{3,2,1,0:T(8,128)(2,1)S(1)} %all_to_all.10), kind=kOutput, calls=%fused_computation.5 | convolution fusion | flops 7247757312 | bytes 18874368 | tf_op jit(solution)/shard_map/nekd,edf->nekf/dot_general | solution.py:302
  138.5 5.5 %convert_bitcast_fusion = bf16[32,1,48,1536]{3,2,1,0:T(8,128)(2,1)} fusion(f32[32,1,48,1536]{3,2,0,1:T(8,128)S(1)} %convolution_bitcast_fusion, bf16[1,768,1536]{2,1,0:T(8,128)(2,1)S(1)} %copy-done), kind=kOutput, calls=%fused_computation.11 | convolution fusion | flops 3629776896 | bytes 16515072 | tf_op jit(solution)/shard_map/nekf,efd->nekd/dot_general | solution.py:309
  144.0 5.8 %all-to-all-start.1 = ((bf16[32,1,48,1536]{3,2,1,0:T(8,128)(2,1)}), bf16[32,1,48,1536]{3,2,1,0:T(8,128)(2,1)}, u32[]{:S(2)}, u32[]{:S(2)}) async-start(bf16[32,1,48,1536]{3,2,1,0:T(8,128)(2,1)} %convert_bitcast_fusion), calls=%async_computation.1 | async-start | bytes 9437184 | tf_op jit(solution)/shard_map/all_to_all | solution.py:312
  149.9 2.2 %fusion.27 = f32[256,32]{0,1:T(8,128)S(1)} fusion(f32[1536,32]{0,1:T(8,128)S(1)} %copy-done.8, f32[256,1536]{1,0:T(8,128)} %copy-done.2, f32[1536]{0:T(1024)S(1)} %copy-done.10, f32[256]{0:T(256)S(1)} %add_rsqrt_fusion), kind=kOutput, calls=%fused_computation.60 | convolution fusion | flops 152174592 | bytes 1809408 | tf_op jit(solution)/shard_map/dot_general | solution.py:273
  153.4 58.9 %all-to-all-done.1 = bf16[32,1,48,1536]{3,2,1,0:T(8,128)(2,1)} async-done(((bf16[32,1,48,1536]{3,2,1,0:T(8,128)(2,1)}), bf16[32,1,48,1536]{3,2,1,0:T(8,128)(2,1)}, u32[]{:S(2)}, u32[]{:S(2)}) %all-to-all-start.1) | async-done | bytes 4718624 | tf_op jit(solution)/shard_map/all_to_all | solution.py:312
  212.2 5.1 %fusion.5 = bf16[256,1536]{1,0:T(8,128)(2,1)} fusion(f32[256,1536]{1,0:T(8,128)} %copy-done.2, bf16[1536,1536]{1,0:T(8,128)(2,1)} %bitcast.24, bf16[256,1536]{1,0:T(8,128)(2,1)S(1)} %select_reduce_fusion), kind=kOutput, calls=%fused_computation.16 | convolution fusion | flops 1208745984 | bytes 7864320 | tf_op jit(solution)/shard_map/dot_general | solution.py:317
  (61 shorter events, 8.6 us)
Async XLA Ops:
  0.6 137.9 %copy-start = (bf16[1,768,1536]{2,1,0:T(8,128)(2,1)S(1)}, bf16[1,768,1536]{2,1,0:T(8,128)(2,1)}, u32[]{:S(2)}) copy-start(bf16[1,768,1536]{2,1,0:T(8,128)(2,1)} %param.21) | copy-start | bytes 7077892
  0.6 43.1 %collective-permute-start = (s32[2,16]{1,0:T(2,128)}, s32[2,16]{1,0:T(2,128)}, u32[]{:S(2)}, u32[]{:S(2)}) collective-permute-start(s32[2,16]{1,0:T(2,128)} %param.25), channel_id=1, source_target_pairs={{0,4},{4,0},{8,12},{12,8},{16,20},{20,16},{24,28},{28,24},{32,36},... | collective-permute-start | bytes 392 | tf_op jit(solution)/shard_map/ppermute | solution.py:257
  0.7 44.2 %collective-permute-start.2 = (bf16[32,128,256]{2,1,0:T(8,128)(2,1)}, bf16[32,128,256]{2,1,0:T(8,128)(2,1)}, u32[]{:S(2)}, u32[]{:S(2)}) collective-permute-start(bf16[32,128,256]{2,1,0:T(8,128)(2,1)} %k_own.1), channel_id=1, source_target_pairs={{0,4},{4,0},{8,12},{12,8},{16,20},{20,16},{24,28},{28,24},{32,36},... | collective-permute-start | bytes 6291464 | tf_op jit(solution)/shard_map/ppermute | solution.py:257
  1.2 43.7 %collective-permute-start.3 = (bf16[32,128,256]{2,1,0:T(8,128)(2,1)}, bf16[32,128,256]{2,1,0:T(8,128)(2,1)}, u32[]{:S(2)}, u32[]{:S(2)}) collective-permute-start(bf16[32,128,256]{2,1,0:T(8,128)(2,1)} %v_own.1), channel_id=1, source_target_pairs={{0,4},{4,0},{8,12},{12,8},{16,20},{20,16},{24,28},{28,24},{32,36},... | collective-permute-start | bytes 6291464 | tf_op jit(solution)/shard_map/ppermute | solution.py:257
  7.1 4.2 %copy-start.5 = (bf16[256,1536]{1,0:T(8,128)(2,1)S(1)}, bf16[256,1536]{1,0:T(8,128)(2,1)}, u32[]{:S(2)}) copy-start(bf16[256,1536]{1,0:T(8,128)(2,1)} %param.14) | copy-start | bytes 2359300
  11.5 4.2 %copy-start.12 = (f32[1536]{0:T(1024)S(1)}, f32[1536]{0:T(1024)}, u32[]{:S(2)}) copy-start(f32[1536]{0:T(1024)} %param.15) | copy-start | bytes 18436
  20.4 2.9 %copy-start.1 = (f32[256,2048]{1,0:T(8,128)}, f32[256,2048]{1,0:T(8,128)S(1)}, u32[]{:S(2)}) copy-start(f32[256,2048]{1,0:T(8,128)S(1)} %fusion.17) | copy-start | bytes 6291460
  27.7 3.6 %copy-start.7 = (bf16[256,256]{1,0:T(8,128)(2,1)S(1)}, bf16[256,256]{1,0:T(8,128)(2,1)}, u32[]{:S(2)}) copy-start(bf16[256,256]{1,0:T(8,128)(2,1)} %slice.217) | copy-start | bytes 393220
  27.7 7.0 %copy-start.9 = (s32[256,4]{0,1:T(4,128)S(1)}, s32[256,4]{0,1:T(4,128)}, u32[]{:S(2)}) copy-start(s32[256,4]{0,1:T(4,128)} %param.22) | copy-start | bytes 12292
  31.2 12.5 %copy-start.11 = (s32[2,16]{1,0:T(2,128)S(1)}, s32[2,16]{1,0:T(2,128)}, u32[]{:S(2)}) copy-start(s32[2,16]{1,0:T(2,128)} %param.25) | copy-start | bytes 388
  31.3 13.7 %copy-start.4 = (bf16[256,512]{1,0:T(8,128)(2,1)}, bf16[256,512]{1,0:T(8,128)(2,1)S(1)}, u32[]{:S(2)}) copy-start(bf16[256,512]{1,0:T(8,128)(2,1)S(1)} %pad_maximum_fusion.kn_ref) | copy-start | bytes 786436
  31.3 13.6 %collective-permute-start.1 = (bf16[256,512]{1,0:T(8,128)(2,1)S(1)}, bf16[256,512]{1,0:T(8,128)(2,1)}, u32[]{:S(2)}, u32[]{:S(2)}) collective-permute-start(bf16[256,512]{1,0:T(8,128)(2,1)S(1)} %pad_maximum_fusion.kn_ref), channel_id=1, source_target_pairs={{0,1},{2,3},{4,5},{6,7},{8,9},{10,11},{12,13},{14,15},{16,17},{18,... | collective-permute-start | bytes 786440 | tf_op jit(solution)/shard_map/ppermute | solution.py:255
  44.9 6.5 %copy-start.6 = (bf16[256,1536]{1,0:T(8,128)(2,1)S(1)}, bf16[256,1536]{1,0:T(8,128)(2,1)}, u32[]{:S(2)}) copy-start(bf16[256,1536]{1,0:T(8,128)(2,1)} %param.14) | copy-start | bytes 2359300
  51.4 4.3 %copy-start.3 = (pred[1536,256]{1,0:T(8,128)(4,1)S(1)}, pred[1536,256]{1,0:T(8,128)(4,1)}, u32[]{:S(2)}) copy-start(pred[1536,256]{1,0:T(8,128)(4,1)} %fusion) | copy-start | bytes 1179652
  51.4 4.3 %copy-start.10 = (f32[1536]{0:T(1024)S(1)}, f32[1536]{0:T(1024)}, u32[]{:S(2)}) copy-start(f32[1536]{0:T(1024)} %param.18) | copy-start | bytes 18436
  51.5 79.6 %slice-start = ((s8[4718592]{0:T(1024)(128)(4,1)}), s8[4194304]{0:T(1024)(128)(4,1)S(1)}, s32[]{:S(2)}) async-start(s8[4718592]{0:T(1024)(128)(4,1)} %bitcast.50), calls=%async_computation.2 | async-start | bytes 8388608
  55.7 1.5 copy-start.2
  55.7 75.3 %slice-start.1 = ((s8[4718592]{0:T(1024)(128)(4,1)}), s8[524288]{0:T(1024)(128)(4,1)S(1)}, s32[]{:S(2)}) async-start(s8[4718592]{0:T(1024)(128)(4,1)} %bitcast.50), calls=%async_computation.3 | async-start | bytes 1048576
  144.0 5.9 %copy-start.8 = (f32[1536,32]{0,1:T(8,128)S(1)}, f32[1536,32]{0,1:T(8,128)}, u32[]{:S(2)}) copy-start(f32[1536,32]{0,1:T(8,128)} %param.19) | copy-start | bytes 589828
  144.0 68.2 %all-to-all-start.1 = ((bf16[32,1,48,1536]{3,2,1,0:T(8,128)(2,1)}), bf16[32,1,48,1536]{3,2,1,0:T(8,128)(2,1)}, u32[]{:S(2)}, u32[]{:S(2)}) async-start(bf16[32,1,48,1536]{3,2,1,0:T(8,128)(2,1)} %convert_bitcast_fusion), calls=%async_computation.1 | async-start | bytes 9437184 | tf_op jit(solution)/shard_map/all_to_all | solution.py:312

commit v6 on v5

--- a/solution.py
+++ b/solution.py
@@ -44,16 +44,35 @@
     )
 
 
-def rotate_flat(values, cosine, sines):
-    half_dim = cosine.shape[1]
-    heads = values.shape[1] // (2 * half_dim)
-    cos_full = jnp.tile(jnp.concatenate([cosine, cosine], axis=1), (1, heads))
-    sin_signed = jnp.tile(jnp.concatenate([-sines, sines], axis=1), (1, heads))
-    parts = []
-    for h in range(heads):
-        base = 2 * half_dim * h
-        parts += [values[:, base + half_dim : base + 2 * half_dim], values[:, base : base + half_dim]]
-    return values * cos_full + jnp.concatenate(parts, axis=1) * sin_signed
+def rotary_kernel(proj_ref, cos_ref, sin_ref, q_ref, app_ref):
+    cosine = cos_ref[...]
+    sines = sin_ref[...]
+    for h in range(QUERY_HEADS + KEY_VALUE_HEADS):
+        x = proj_ref[:, h * HEAD_SIZE : (h + 1) * HEAD_SIZE]
+        swapped = pltpu.roll(x, HEAD_SIZE // 2, 1)
+        r = (x * cosine + swapped * sines).astype(jnp.bfloat16)
+        if h < QUERY_HEADS:
+            q_ref[:, h * HEAD_SIZE : (h + 1) * HEAD_SIZE] = r
+        else:
+            k = h - QUERY_HEADS
+            app_ref[:, k * HEAD_SIZE : (k + 1) * HEAD_SIZE] = r
+    base = (QUERY_HEADS + KEY_VALUE_HEADS) * HEAD_SIZE
+    width = KEY_VALUE_HEADS * HEAD_SIZE
+    app_ref[:, width : 2 * width] = proj_ref[:, base : base + width].astype(jnp.bfloat16)
+
+
+def rotate(projected_rows, cosine, sines):
+    tokens = projected_rows.shape[0]
+    vmem_spec = pl.BlockSpec(memory_space=pltpu.VMEM)
+    return pl.pallas_call(
+        rotary_kernel,
+        in_specs=[vmem_spec, vmem_spec, vmem_spec],
+        out_specs=(vmem_spec, vmem_spec),
+        out_shape=(
+            jax.ShapeDtypeStruct((tokens, QUERY_HEADS * HEAD_SIZE), jnp.bfloat16),
+            jax.ShapeDtypeStruct((tokens, 2 * KEY_VALUE_HEADS * HEAD_SIZE), jnp.bfloat16),
+        ),
+    )(projected_rows, cosine, sines)
 
 
 def attention_kernel(
@@ -238,16 +257,13 @@
         / HEAD_SIZE
     )
     angles = token_positions.astype(jnp.float32)[:, None] * frequency[None, :]
-    rotated = rotate_flat(
-        projected_rows[:, : (QUERY_HEADS + KEY_VALUE_HEADS) * HEAD_SIZE],
-        jnp.cos(angles),
-        jnp.sin(angles),
-    ).astype(jnp.bfloat16)
-    queries = rotated[:, : QUERY_HEADS * HEAD_SIZE]
-    fresh_values = projected_rows[:, (QUERY_HEADS + KEY_VALUE_HEADS) * HEAD_SIZE :].astype(
-        jnp.bfloat16
-    )
-    appended = jnp.concatenate([rotated[:, QUERY_HEADS * HEAD_SIZE :], fresh_values], axis=1)
+    cosine = jnp.cos(angles)
+    sines = jnp.sin(angles)
+    queries, appended = rotate(
+        projected_rows,
+        jnp.concatenate([cosine, cosine], axis=1),
+        jnp.concatenate([-sines, sines], axis=1),
+    )
 
     forward_pairs = [
         (h, h + 1) for h in range(count_of_heads) if h % share != share - 1

time: 222 us -> 203 us (0.914); the launches traced: 217 us -> 201 us
  local copies, waits for them, and re-layouts: 22.9 us -> 3.75 us
  Pallas kernels: 6.48 us -> 13.2 us
  blocking collectives: 73.8 us -> 69 us
  other arithmetic: 10.5 us -> 7.59 us
  waiting for transfers between devices: 58.9 us -> 61.7 us
    another operation x4 -> x0, local copies, waits for them, and re-layouts: 8.39 us -> none  [the longest x2 4.23 us: rotate_flat(): sin_signed = jnp.tile(jnp.concatenate([-sines, sines], axis=1), (1, heads))]
    all_to_all x1, blocking collectives: 73.8 us -> 69 us  [on_device(): lax.all_to_all(dispatch, 'req', split_axis=0, concat_axis=0, tiled=True)]
    concatenate x1 -> x0, local copies, waits for them, and re-layouts: 4.4 us -> none  [rotate_flat(): return values * cos_full + jnp.concatenate(parts, axis=1) * sin_signed]
    slice x5 -> x0, local copies, waits for them, and re-layouts: 3.81 us -> none  [the longest x1 1.93 us: rotate_flat(): values[:, base:base + half_dim]]
    pallas_call x1, Pallas kernels: 6.48 us -> 10.1 us  [attend(): pl.pallas_call(functools.partial(attention_kernel, group=group, tokens=to...]
    convert_element_type x1 -> x0, other arithmetic: 3.53 us -> none  [on_device(): rotated = rotate_flat(projected_rows[:, :(QUERY_HEADS + KEY_VALUE_HEADS)...]
    pallas_call x0 -> x1, Pallas kernels: none -> 3.12 us  [rotate(): pl.pallas_call(rotary_kernel, in_specs=[vmem_spec, vmem_spec, vmem_spec],...]
    ppermute x1, waiting for transfers between devices: 0.01 us -> 2.8 us  [on_device(): earlier = lax.ppermute(appended, 'head', forward_pairs)]
  transfers between devices with their start and end apart: 5 -> 5, of which waited for: 1 -> 2; matrix products, arithmetic and copies ran while one was open for 19% -> 10% of each run, Pallas kernels for 0% -> 2%
where the time goes in v6:
time: 203 us; the launch traced here: 201 us
  blocking collectives  69 us (34%)
  waiting for transfers between devices  61.7 us (30%)
  matrix products  32.8 us (16%)
  Pallas kernels  13.2 us (7%)
  starting transfers between devices  7.81 us (4%)
  other arithmetic  7.59 us (4%)
  between operations  5.35 us (3%)
  local copies, waits for them, and re-layouts  3.75 us (2%)
    all_to_all x1, blocking collectives, on_device(): lax.all_to_all(dispatch, 'req', split_axis=0, concat_axis=0, tiled=True)  69 us
    all_to_all x1, waiting for transfers between devices, on_device(): lax.all_to_all(result, 'req', split_axis=0, concat_axis=0, tiled=True)  58.9 us
    pallas_call x1, Pallas kernels, attend(): pl.pallas_call(functools.partial(attention_kernel, group=group, tokens=to...  10.1 us
    dot_general x1, matrix products, on_device(): jnp.einsum('nekd,edf->nekf', lax.all_to_all(dispatch, 'req', split_axis=0...  7.51 us
    dot_general x1, matrix products, on_device(): jnp.dot(normed, query_key_value_weight, preferred_element_type=jnp.float32)  6.23 us
    all_to_all x1, starting transfers between devices, on_device(): lax.all_to_all(result, 'req', split_axis=0, concat_axis=0, tiled=True)  5.85 us
    dot_general x1, matrix products, on_device(): jnp.einsum('nekf,efd->nekd', hidden, w_down, preferred_element_type=jnp.f...  5.47 us
    dot_general x1, matrix products, on_device(): jnp.dot(combine.astype(jnp.bfloat16), flat_results, preferred_element_typ...  5.1 us
  transfers between devices with their start and end apart: 5, of which 2 were waited for; matrix products, arithmetic and copies ran while one was open for 10% of the time, Pallas kernels for 2%

profile of v6, /device:TPU:56, one launch (start us, length us, event | category | flops | bytes accessed | tf_op | source)
XLA Modules:
  0.0 201.1 jit_solution(7770591426091517094)
XLA Ops:
  1.3 1.3 dynamic_slice.13
  4.5 1.3 dynamic_slice.14
  6.4 0.5 fusion.22
  7.0 0.9 pad_maximum_fusion
  7.8 1.4 fusion.10
  9.2 6.2 %fusion.15.proj_ref = f32[256,2048]{1,0:T(8,128)} fusion(bf16[1536,2048]{1,0:T(8,128)(2,1)} %param.16, bf16[256,1536]{1,0:T(8,128)(2,1)} %param.14, f32[1536]{0:T(1024)} %param.15, f32[256]{0:T(256)S(1)} %add_rsqrt_fusion.1), kind=kOutput, calls=%fused_computation.29 | convolution fusion | flops 1612185600 | bytes 9182208 | tf_op jit(solution)/shard_map/dot_general | solution.py:251
  15.5 3.1 %shard_map.149 = (bf16[256,1536]{1,0:T(8,128)(2,1)}, bf16[256,512]{1,0:T(8,128)(2,1)}) custom-call(f32[256,2048]{1,0:T(8,128)} %fusion.15.proj_ref, f32[256,128]{1,0:T(8,128)} %get-tuple-element.11.cos_ref, f32[256,128]{1,0:T(8,128)} %get-tuple-element.12.sin_ref), custom_call_target="tpu_custom_call" | custom-call | tf_op jit(solution)/shard_map/pallas_call | solution.py:67
  18.6 1.3 collective-permute-start.1
  22.1 0.5 fusion.14
  22.8 1.3 pad_add_fusion.meta_ref
  24.1 1.8 fusion
  26.5 2.8 %collective-permute-done.1.vn_ref = bf16[256,512]{1,0:T(8,128)(2,1)S(1)} collective-permute-done((bf16[256,512]{1,0:T(8,128)(2,1)}, bf16[256,512]{1,0:T(8,128)(2,1)S(1)}, u32[]{:S(2)}, u32[]{:S(2)}) %collective-permute-start.1) | collective-permute-done | bytes 262176 | tf_op jit(solution)/shard_map/ppermute | solution.py:271
  29.3 0.7 copy-done.3
  30.0 10.1 %shard_map.150 = bf16[256,1536]{1,0:T(8,128)(2,1)} custom-call(s32[3]{0:T(128)} %pad_add_fusion.meta_ref, s32[16]{0:T(128)} %fusion.23.page_ref, bf16[256,1536]{1,0:T(8,128)(2,1)} %get-tuple-element.4.q_ref, bf16[256,512]{1,0:T(8,128)(2,1)} %get-tuple-element.3.kn_ref, bf16[256,512]{1,0:T(8,128)(2,1)} %copy-done.3, bf16[32,128,256]{2,1,0:T(8,128)(2,1)} %k_own.1, ...), custom_call_target="tpu_custom_call" | custom-call | tf_op jit(solution)/shard_map/pallas_call | solution.py:192
  40.1 4.2 %multiply_reduce_fusion = (f32[256]{0:T(256)S(1)}, f32[256,1536]{1,0:T(8,128)S(1)}) fusion(bf16[256,1536]{1,0:T(8,128)(2,1)} %shard_map.150, bf16[1536,1536]{1,0:T(8,128)(2,1)} %param.17, bf16[256,1536]{1,0:T(8,128)(2,1)S(1)} %copy-done.2), kind=kOutput, calls=%fused_computation.26 | convolution fusion | flops 1209532160 | bytes 7865344 | tf_op jit(solution)/shard_map/dot_general | solution.py:285
  44.4 1.5 convolution_convert_fusion
  45.9 69.0 %all_to_all.10 = bf16[32,1,48,1536]{3,2,1,0:T(8,128)(2,1)S(1)} all-to-all(bf16[32,1,48,1536]{3,2,1,0:T(8,128)(2,1)S(1)} %bitcast.45), channel_id=1, replica_groups=mesh['req'=32,'head'=4] {'req'}, dimensions={0} | all-to-all | bytes 9437184 | tf_op jit(solution)/shard_map/all_to_all | solution.py:320
  114.9 7.5 %convolution_bitcast_fusion = f32[32,1,48,1536]{3,2,0,1:T(8,128)S(1)} fusion(bf16[1,1536,1536]{2,1,0:T(8,128)(2,1)S(1)} %bitcast.47, bf16[32,1,48,1536]{3,2,1,0:T(8,128)(2,1)S(1)} %all_to_all.10), kind=kOutput, calls=%fused_computation.5 | convolution fusion | flops 7247757312 | bytes 18874368 | tf_op jit(solution)/shard_map/nekd,edf->nekf/dot_general | solution.py:318
  122.4 5.5 %convert_bitcast_fusion = bf16[32,1,48,1536]{3,2,1,0:T(8,128)(2,1)} fusion(f32[32,1,48,1536]{3,2,0,1:T(8,128)S(1)} %convolution_bitcast_fusion, bf16[1,768,1536]{2,1,0:T(8,128)(2,1)S(1)} %copy-done), kind=kOutput, calls=%fused_computation.11 | convolution fusion | flops 3629776896 | bytes 16515072 | tf_op jit(solution)/shard_map/nekf,efd->nekd/dot_general | solution.py:325
  127.9 5.9 %all-to-all-start.1 = ((bf16[32,1,48,1536]{3,2,1,0:T(8,128)(2,1)}), bf16[32,1,48,1536]{3,2,1,0:T(8,128)(2,1)}, u32[]{:S(2)}, u32[]{:S(2)}) async-start(bf16[32,1,48,1536]{3,2,1,0:T(8,128)(2,1)} %convert_bitcast_fusion), calls=%async_computation.1 | async-start | bytes 9437184 | tf_op jit(solution)/shard_map/all_to_all | solution.py:328
  133.7 2.2 %fusion.25 = f32[256,32]{0,1:T(8,128)S(1)} fusion(f32[1536,32]{0,1:T(8,128)S(1)} %copy-done.4, f32[256,1536]{1,0:T(8,128)} %copy-done.1, f32[1536]{0:T(1024)S(1)} %copy-done.6, f32[256]{0:T(256)S(1)} %add_rsqrt_fusion), kind=kOutput, calls=%fused_computation.55 | convolution fusion | flops 152174592 | bytes 1809408 | tf_op jit(solution)/shard_map/dot_general | solution.py:289
  136.1 1.1 select_reduce_fusion
  137.2 58.9 %all-to-all-done.1 = bf16[32,1,48,1536]{3,2,1,0:T(8,128)(2,1)} async-done(((bf16[32,1,48,1536]{3,2,1,0:T(8,128)(2,1)}), bf16[32,1,48,1536]{3,2,1,0:T(8,128)(2,1)}, u32[]{:S(2)}, u32[]{:S(2)}) %all-to-all-start.1) | async-done | bytes 4718624 | tf_op jit(solution)/shard_map/all_to_all | solution.py:328
  196.0 5.1 %fusion.5 = bf16[256,1536]{1,0:T(8,128)(2,1)} fusion(f32[256,1536]{1,0:T(8,128)} %copy-done.1, bf16[1536,1536]{1,0:T(8,128)(2,1)} %bitcast.22, bf16[256,1536]{1,0:T(8,128)(2,1)S(1)} %select_reduce_fusion), kind=kOutput, calls=%fused_computation.16 | convolution fusion | flops 1208745984 | bytes 7864320 | tf_op jit(solution)/shard_map/dot_general | solution.py:333
  (40 shorter events, 1.8 us)
Async XLA Ops:
  0.6 121.7 %copy-start = (bf16[1,768,1536]{2,1,0:T(8,128)(2,1)S(1)}, bf16[1,768,1536]{2,1,0:T(8,128)(2,1)}, u32[]{:S(2)}) copy-start(bf16[1,768,1536]{2,1,0:T(8,128)(2,1)} %param.21) | copy-start | bytes 7077892
  0.6 25.3 %collective-permute-start = (s32[2,16]{1,0:T(2,128)}, s32[2,16]{1,0:T(2,128)S(1)}, u32[]{:S(2)}, u32[]{:S(2)}) collective-permute-start(s32[2,16]{1,0:T(2,128)} %param.25), channel_id=1, source_target_pairs={{0,4},{4,0},{8,12},{12,8},{16,20},{20,16},{24,28},{28,24},{32,36},... | collective-permute-start | bytes 392 | tf_op jit(solution)/shard_map/ppermute | solution.py:273
  0.7 28.5 %collective-permute-start.2 = (bf16[32,128,256]{2,1,0:T(8,128)(2,1)}, bf16[32,128,256]{2,1,0:T(8,128)(2,1)}, u32[]{:S(2)}, u32[]{:S(2)}) collective-permute-start(bf16[32,128,256]{2,1,0:T(8,128)(2,1)} %k_own.1), channel_id=1, source_target_pairs={{0,4},{4,0},{8,12},{12,8},{16,20},{20,16},{24,28},{28,24},{32,36},... | collective-permute-start | bytes 6291464 | tf_op jit(solution)/shard_map/ppermute | solution.py:273
  1.2 28.0 %collective-permute-start.3 = (bf16[32,128,256]{2,1,0:T(8,128)(2,1)}, bf16[32,128,256]{2,1,0:T(8,128)(2,1)}, u32[]{:S(2)}, u32[]{:S(2)}) collective-permute-start(bf16[32,128,256]{2,1,0:T(8,128)(2,1)} %v_own.1), channel_id=1, source_target_pairs={{0,4},{4,0},{8,12},{12,8},{16,20},{20,16},{24,28},{28,24},{32,36},... | collective-permute-start | bytes 6291464 | tf_op jit(solution)/shard_map/ppermute | solution.py:273
  9.2 12.6 %copy-start.5 = (s32[256,4]{0,1:T(4,128)S(1)}, s32[256,4]{0,1:T(4,128)}, u32[]{:S(2)}) copy-start(s32[256,4]{0,1:T(4,128)} %param.22) | copy-start | bytes 12292
  15.5 10.5 %copy-start.7 = (s32[2,16]{1,0:T(2,128)S(1)}, s32[2,16]{1,0:T(2,128)}, u32[]{:S(2)}) copy-start(s32[2,16]{1,0:T(2,128)} %param.25) | copy-start | bytes 388
  18.6 10.7 %collective-permute-start.1 = (bf16[256,512]{1,0:T(8,128)(2,1)}, bf16[256,512]{1,0:T(8,128)(2,1)S(1)}, u32[]{:S(2)}, u32[]{:S(2)}) collective-permute-start(bf16[256,512]{1,0:T(8,128)(2,1)} %get-tuple-element.3.kn_ref), channel_id=1, source_target_pairs={{0,1},{2,3},{4,5},{6,7},{8,9},{10,11},{12,13},{14,15},{16,17},{18,... | collective-permute-start | bytes 786440 | tf_op jit(solution)/shard_map/ppermute | solution.py:271
  29.3 0.7 copy-start.3
  30.0 10.1 %copy-start.2 = (bf16[256,1536]{1,0:T(8,128)(2,1)S(1)}, bf16[256,1536]{1,0:T(8,128)(2,1)}, u32[]{:S(2)}) copy-start(bf16[256,1536]{1,0:T(8,128)(2,1)} %param.14) | copy-start | bytes 2359300
  40.1 4.2 %copy-start.6 = (f32[1536]{0:T(1024)S(1)}, f32[1536]{0:T(1024)}, u32[]{:S(2)}) copy-start(f32[1536]{0:T(1024)} %param.18) | copy-start | bytes 18436
  40.1 74.7 %slice-start = ((s8[4718592]{0:T(1024)(128)(4,1)}), s8[4194304]{0:T(1024)(128)(4,1)S(1)}, s32[]{:S(2)}) async-start(s8[4718592]{0:T(1024)(128)(4,1)} %bitcast.46), calls=%async_computation.2 | async-start | bytes 8388608
  44.3 1.5 copy-start.1
  44.4 70.5 %slice-start.1 = ((s8[4718592]{0:T(1024)(128)(4,1)}), s8[524288]{0:T(1024)(128)(4,1)S(1)}, s32[]{:S(2)}) async-start(s8[4718592]{0:T(1024)(128)(4,1)} %bitcast.46), calls=%async_computation.3 | async-start | bytes 1048576
  127.9 5.9 %copy-start.4 = (f32[1536,32]{0,1:T(8,128)S(1)}, f32[1536,32]{0,1:T(8,128)}, u32[]{:S(2)}) copy-start(f32[1536,32]{0,1:T(8,128)} %param.19) | copy-start | bytes 589828
  127.9 68.2 %all-to-all-start.1 = ((bf16[32,1,48,1536]{3,2,1,0:T(8,128)(2,1)}), bf16[32,1,48,1536]{3,2,1,0:T(8,128)(2,1)}, u32[]{:S(2)}, u32[]{:S(2)}) async-start(bf16[32,1,48,1536]{3,2,1,0:T(8,128)(2,1)} %convert_bitcast_fusion), calls=%async_computation.1 | async-start | bytes 9437184 | tf_op jit(solution)/shard_map/all_to_all | solution.py:328

commit v7 on v6

--- a/solution.py
+++ b/solution.py
@@ -315,24 +315,35 @@
         jnp.bfloat16
     )
     dispatch = dispatch.reshape(req_count, exp_dev, capacity, MODEL_WIDTH)
+    cut = MODEL_WIDTH // 2
+    arrived = [
+        lax.all_to_all(dispatch[..., :cut], "req", split_axis=0, concat_axis=0, tiled=True),
+        lax.all_to_all(dispatch[..., cut:], "req", split_axis=0, concat_axis=0, tiled=True),
+    ]
     gate_up = jnp.einsum(
-        "nekd,edf->nekf",
-        lax.all_to_all(dispatch, "req", split_axis=0, concat_axis=0, tiled=True),
-        w_gate_up,
-        preferred_element_type=jnp.float32,
+        "nekd,edf->nekf", arrived[0], w_gate_up[:, :cut, :], preferred_element_type=jnp.float32
+    ) + jnp.einsum(
+        "nekd,edf->nekf", arrived[1], w_gate_up[:, cut:, :], preferred_element_type=jnp.float32
     )
     hidden = (jax.nn.relu(gate_up[..., :FE]) * gate_up[..., FE:]).astype(jnp.bfloat16)
-    result = jnp.einsum(
-        "nekf,efd->nekd", hidden, w_down, preferred_element_type=jnp.float32
-    ).astype(jnp.bfloat16)
-    results = lax.all_to_all(result, "req", split_axis=0, concat_axis=0, tiled=True)
-    flat_results = results.reshape(slot_total, MODEL_WIDTH)
-
     token_hits = slot_ids[:, :, None] == slot_iota[None, None, :]
     combine = jnp.sum(jnp.where(token_hits, route_gates[:, :, None], 0.0), axis=1)
-    expert_sum = jnp.dot(
-        combine.astype(jnp.bfloat16), flat_results, preferred_element_type=jnp.float32
-    )
+    combine = combine.astype(jnp.bfloat16)
+    sums = []
+    for part in range(2):
+        result = jnp.einsum(
+            "nekf,efd->nekd",
+            hidden,
+            w_down[:, :, part * cut : (part + 1) * cut],
+            preferred_element_type=jnp.float32,
+        ).astype(jnp.bfloat16)
+        results = lax.all_to_all(result, "req", split_axis=0, concat_axis=0, tiled=True)
+        sums.append(
+            jnp.dot(
+                combine, results.reshape(slot_total, cut), preferred_element_type=jnp.float32
+            )
+        )
+    expert_sum = jnp.concatenate(sums, axis=1)
     mixed_out = (residual + expert_sum).astype(jnp.bfloat16)
     return (mixed_out, appended)
 

time: 203 us -> 224 us (1.10)
  blocking collectives: 69 us -> 41 us
  starting transfers between devices: 7.81 us -> 21.1 us
  matrix products: 32.8 us -> 46 us
  waiting for transfers between devices: 61.7 us -> 73 us
  Pallas kernels: 13.2 us -> 18.8 us
  local copies, waits for them, and re-layouts: 3.75 us -> 6.87 us
    all_to_all x1, blocking collectives: 69 us -> 41 us  [on_device(): lax.all_to_all(dispatch[..., :cut], 'req', split_axis=0, concat_axis=0, t...]
    all_to_all x0 -> x1, waiting for transfers between devices: none -> 20.3 us  [on_device(): lax.all_to_all(dispatch[..., cut:], 'req', split_axis=0, concat_axis=0, t...]
    dot_general x3 -> x6, matrix products: 18.1 us -> 32.9 us  [the longest x1 9.85 us: on_device(): jnp.einsum('nekd,edf->nekf', arrived[0], w_gate_up[:, :cut, :], preferred...]
    all_to_all x1 -> x2, waiting for transfers between devices: 58.9 us -> 50.3 us  [on_device(): lax.all_to_all(result, 'req', split_axis=0, concat_axis=0, tiled=True)]
    all_to_all x1 -> x2, starting transfers between devices: 5.85 us -> 12.9 us  [on_device(): lax.all_to_all(result, 'req', split_axis=0, concat_axis=0, tiled=True)]
    all_to_all x0 -> x1, starting transfers between devices: none -> 6.18 us  [on_device(): lax.all_to_all(dispatch[..., cut:], 'req', split_axis=0, concat_axis=0, t...]
    pallas_call x1, Pallas kernels: 10.1 us -> 15.6 us  [attend(): pl.pallas_call(functools.partial(attention_kernel, group=group, tokens=to...]
  transfers between devices with their start and end apart: 5 -> 7, of which waited for: 2 -> 4; matrix products, arithmetic and copies ran while one was open for 10% -> 16% of each run, Pallas kernels for 2% -> 1%
where the time goes in v7:
time: 224 us; the launch traced here: 222 us
  waiting for transfers between devices  73 us (33%)
  matrix products  46 us (21%)
  blocking collectives  41 us (18%)
  starting transfers between devices  21.1 us (9%)
  Pallas kernels  18.8 us (8%)
  other arithmetic  9.38 us (4%)
  local copies, waits for them, and re-layouts  6.87 us (3%)
  between operations  5.37 us (2%)
    all_to_all x2, waiting for transfers between devices, on_device(): lax.all_to_all(result, 'req', split_axis=0, concat_axis=0, tiled=True)  50.3 us
    all_to_all x1, blocking collectives, on_device(): lax.all_to_all(dispatch[..., :cut], 'req', split_axis=0, concat_axis=0, t...  41 us
    all_to_all x1, waiting for transfers between devices, on_device(): lax.all_to_all(dispatch[..., cut:], 'req', split_axis=0, concat_axis=0, t...  20.3 us
    pallas_call x1, Pallas kernels, attend(): pl.pallas_call(functools.partial(attention_kernel, group=group, tokens=to...  15.6 us
    all_to_all x2, starting transfers between devices, on_device(): lax.all_to_all(result, 'req', split_axis=0, concat_axis=0, tiled=True)  12.9 us
    dot_general x1, matrix products, on_device(): jnp.einsum('nekd,edf->nekf', arrived[0], w_gate_up[:, :cut, :], preferred...  9.85 us
    dot_general x1, matrix products, on_device(): jnp.einsum('nekd,edf->nekf', arrived[1], w_gate_up[:, cut:, :], preferred...  9.28 us
    dot_general x2, matrix products, on_device(): jnp.einsum('nekf,efd->nekd', hidden, w_down[:, :, part * cut:(part + 1) *...  8.89 us
  transfers between devices with their start and end apart: 7, of which 4 were waited for; matrix products, arithmetic and copies ran while one was open for 16% of the time, Pallas kernels for 1%

profile of v7, /device:TPU:56, one launch (start us, length us, event | category | flops | bytes accessed | tf_op | source)
XLA Modules:
  0.0 221.6 jit_solution(9981663975170139854)
XLA Ops:
  7.7 1.4 fusion.11
  9.1 6.2 %fusion.21.proj_ref = f32[256,2048]{1,0:T(8,128)} fusion(bf16[1536,2048]{1,0:T(8,128)(2,1)} %param.16, bf16[256,1536]{1,0:T(8,128)(2,1)} %param.14, f32[1536]{0:T(1024)} %param.15, f32[256]{0:T(256)S(1)} %add_rsqrt_fusion.1), kind=kOutput, calls=%fused_computation.37 | convolution fusion | flops 1612185600 | bytes 9182208 | tf_op jit(solution)/shard_map/dot_general | solution.py:251
  15.3 3.1 %shard_map.149 = (bf16[256,1536]{1,0:T(8,128)(2,1)}, bf16[256,512]{1,0:T(8,128)(2,1)}) custom-call(f32[256,2048]{1,0:T(8,128)} %fusion.21.proj_ref, f32[256,128]{1,0:T(8,128)} %get-tuple-element.13.cos_ref, f32[256,128]{1,0:T(8,128)} %get-tuple-element.14.sin_ref), custom_call_target="tpu_custom_call" | custom-call | tf_op jit(solution)/shard_map/pallas_call | solution.py:67
  18.5 1.3 collective-permute-start.1
  24.1 1.8 fusion
  26.5 2.4 %collective-permute-done.1.vn_ref = bf16[256,512]{1,0:T(8,128)(2,1)S(1)} collective-permute-done((bf16[256,512]{1,0:T(8,128)(2,1)}, bf16[256,512]{1,0:T(8,128)(2,1)S(1)}, u32[]{:S(2)}, u32[]{:S(2)}) %collective-permute-start.1) | collective-permute-done | bytes 262176 | tf_op jit(solution)/shard_map/ppermute | solution.py:271
  29.6 15.6 %shard_map.150 = bf16[256,1536]{1,0:T(8,128)(2,1)} custom-call(s32[3]{0:T(128)} %pad_add_fusion.meta_ref, s32[16]{0:T(128)} %fusion.32.page_ref, bf16[256,1536]{1,0:T(8,128)(2,1)} %get-tuple-element.4.q_ref, bf16[256,512]{1,0:T(8,128)(2,1)} %get-tuple-element.3.kn_ref, bf16[256,512]{1,0:T(8,128)(2,1)} %copy-done.3, bf16[32,128,256]{2,1,0:T(8,128)(2,1)} %k_own.1, ...), custom_call_target="tpu_custom_call" | custom-call | tf_op jit(solution)/shard_map/pallas_call | solution.py:192
  45.2 4.1 %multiply_reduce_fusion = (f32[256]{0:T(256)S(1)}, f32[256,1536]{1,0:T(8,128)S(1)}) fusion(bf16[256,1536]{1,0:T(8,128)(2,1)} %shard_map.150, bf16[1536,1536]{1,0:T(8,128)(2,1)} %param.17, bf16[256,1536]{1,0:T(8,128)(2,1)S(1)} %copy-done.2), kind=kOutput, calls=%fused_computation.30 | convolution fusion | flops 1209532160 | bytes 7865344 | tf_op jit(solution)/shard_map/dot_general | solution.py:285
  49.3 1.5 convolution_convert_fusion
  50.8 1.7 fusion.34
  52.6 41.0 %all_to_all.20 = bf16[32,1,48,768]{3,2,1,0:T(8,128)(2,1)} all-to-all(bf16[32,1,48,768]{3,2,1,0:T(8,128)(2,1)S(1)} %get-tuple-element.7), channel_id=1, replica_groups=mesh['req'=32,'head'=4] {'req'}, dimensions={0} | all-to-all | bytes 4718592 | tf_op jit(solution)/shard_map/all_to_all | solution.py:320
  93.6 6.2 %all-to-all-start.1 = ((bf16[32,1,48,768]{3,2,1,0:T(8,128)(2,1)}), bf16[32,1,48,768]{3,2,1,0:T(8,128)(2,1)}, u32[]{:S(2)}, u32[]{:S(2)}) async-start(bf16[32,1,48,768]{3,2,1,0:T(8,128)(2,1)} %get-tuple-element.6), calls=%async_computation.1 | async-start | bytes 4718592 | tf_op jit(solution)/shard_map/all_to_all | solution.py:321
  99.8 9.8 %fusion.6 = f32[32,48,1536]{2,1,0:T(8,128)} fusion(bf16[32,1,48,768]{3,2,1,0:T(8,128)(2,1)} %all_to_all.20, bf16[1,1536,1536]{2,1,0:T(8,128)(2,1)} %param.20), kind=kOutput, calls=%fused_computation.17 | convolution fusion | flops 3623878656 | bytes 14155776 | tf_op jit(solution)/shard_map/nekd,edf->nekf/dot_general | solution.py:323
  109.6 20.3 %all-to-all-done.1 = bf16[32,1,48,768]{3,2,1,0:T(8,128)(2,1)} async-done(((bf16[32,1,48,768]{3,2,1,0:T(8,128)(2,1)}), bf16[32,1,48,768]{3,2,1,0:T(8,128)(2,1)}, u32[]{:S(2)}, u32[]{:S(2)}) %all-to-all-start.1) | async-done | bytes 2359328 | tf_op jit(solution)/shard_map/all_to_all | solution.py:321
  129.9 9.3 %add_bitcast_fusion = f32[32,1,48,1536]{3,2,0,1:T(8,128)S(1)} fusion(f32[32,48,1536]{2,1,0:T(8,128)} %fusion.6, bf16[32,1,48,768]{3,2,1,0:T(8,128)(2,1)} %all-to-all-done.1, bf16[1,1536,1536]{2,1,0:T(8,128)(2,1)} %param.20), kind=kOutput, calls=%fused_computation | convolution fusion | flops 3626237952 | bytes 23592960 | tf_op jit(solution)/shard_map/nekd,edf->nekf/dot_general | solution.py:325
  140.0 1.4 copy-done.1
  141.4 3.5 %convert_bitcast_fusion.1 = bf16[32,1,48,768]{3,2,1,0:T(8,128)(2,1)} fusion(bf16[32,48,768]{2,1,0:T(8,128)(2,1)S(1)} %fusion.3, bf16[1,768,1536]{2,1,0:T(8,128)(2,1)S(1)} %copy-done.7), kind=kOutput, calls=%fused_computation.21 | convolution fusion | flops 1813118976 | bytes 5898240 | tf_op jit(solution)/shard_map/nekf,efd->nekd/dot_general | solution.py:334
  144.9 6.4 %all-to-all-start.2 = ((bf16[32,1,48,768]{3,2,1,0:T(8,128)(2,1)}), bf16[32,1,48,768]{3,2,1,0:T(8,128)(2,1)}, u32[]{:S(2)}, u32[]{:S(2)}) async-start(bf16[32,1,48,768]{3,2,1,0:T(8,128)(2,1)} %convert_bitcast_fusion.1), calls=%async_computation.2 | async-start | bytes 4718592 | tf_op jit(solution)/shard_map/all_to_all | solution.py:340
  151.4 5.4 %convert_bitcast_fusion = bf16[32,1,48,768]{3,2,1,0:T(8,128)(2,1)} fusion(bf16[32,48,768]{2,1,0:T(8,128)(2,1)} %copy-done.1, bf16[1,768,1536]{2,1,0:T(8,128)(2,1)} %param.21), kind=kOutput, calls=%fused_computation.20 | convolution fusion | flops 1813118976 | bytes 5898240 | tf_op jit(solution)/shard_map/nekf,efd->nekd/dot_general | solution.py:334
  156.8 24.7 %all-to-all-done.2 = bf16[32,1,48,768]{3,2,1,0:T(8,128)(2,1)} async-done(((bf16[32,1,48,768]{3,2,1,0:T(8,128)(2,1)}), bf16[32,1,48,768]{3,2,1,0:T(8,128)(2,1)}, u32[]{:S(2)}, u32[]{:S(2)}) %all-to-all-start.2) | async-done | bytes 2359328 | tf_op jit(solution)/shard_map/all_to_all | solution.py:340
  181.5 6.4 %all-to-all-start.3 = ((bf16[32,1,48,768]{3,2,1,0:T(8,128)(2,1)}), bf16[32,1,48,768]{3,2,1,0:T(8,128)(2,1)}, u32[]{:S(2)}, u32[]{:S(2)}) async-start(bf16[32,1,48,768]{3,2,1,0:T(8,128)(2,1)} %convert_bitcast_fusion), calls=%async_computation.3 | async-start | bytes 4718592 | tf_op jit(solution)/shard_map/all_to_all | solution.py:340
  190.0 2.4 %fusion.36 = f32[256,768]{1,0:T(8,128)S(1)} fusion(bf16[256,1536]{1,0:T(8,128)(2,1)S(1)} %select_reduce_fusion, bf16[1536,768]{1,0:T(8,128)(2,1)} %bitcast.26), kind=kOutput, calls=%fused_computation.68 | convolution fusion | flops 603979776 | bytes 3932160 | tf_op jit(solution)/shard_map/dot_general | solution.py:342
  192.4 25.6 %all-to-all-done.3 = bf16[32,1,48,768]{3,2,1,0:T(8,128)(2,1)} async-done(((bf16[32,1,48,768]{3,2,1,0:T(8,128)(2,1)}), bf16[32,1,48,768]{3,2,1,0:T(8,128)(2,1)}, u32[]{:S(2)}, u32[]{:S(2)}) %all-to-all-start.3) | async-done | bytes 2359328 | tf_op jit(solution)/shard_map/all_to_all | solution.py:340
  218.1 2.4 %fusion.35 = f32[256,768]{1,0:T(8,128)S(1)} fusion(bf16[256,1536]{1,0:T(8,128)(2,1)S(1)} %select_reduce_fusion, bf16[1536,768]{1,0:T(8,128)(2,1)} %bitcast.33), kind=kOutput, calls=%fused_computation.67 | convolution fusion | flops 603979776 | bytes 3932160 | tf_op jit(solution)/shard_map/dot_general | solution.py:342
  (45 shorter events, 12.1 us)
Async XLA Ops:
  0.6 187.3 %copy-start = (f32[1536,32]{0,1:T(8,128)S(1)}, f32[1536,32]{0,1:T(8,128)}, u32[]{:S(2)}) copy-start(f32[1536,32]{0,1:T(8,128)} %param.19) | copy-start | bytes 589828
  0.6 28.2 %collective-permute-start.2 = (bf16[32,128,256]{2,1,0:T(8,128)(2,1)}, bf16[32,128,256]{2,1,0:T(8,128)(2,1)}, u32[]{:S(2)}, u32[]{:S(2)}) collective-permute-start(bf16[32,128,256]{2,1,0:T(8,128)(2,1)} %k_own.1), channel_id=1, source_target_pairs={{0,4},{4,0},{8,12},{12,8},{16,20},{20,16},{24,28},{28,24},{32,36},... | collective-permute-start | bytes 6291464 | tf_op jit(solution)/shard_map/ppermute | solution.py:273
  0.7 28.1 %collective-permute-start.3 = (bf16[32,128,256]{2,1,0:T(8,128)(2,1)}, bf16[32,128,256]{2,1,0:T(8,128)(2,1)}, u32[]{:S(2)}, u32[]{:S(2)}) collective-permute-start(bf16[32,128,256]{2,1,0:T(8,128)(2,1)} %v_own.1), channel_id=1, source_target_pairs={{0,4},{4,0},{8,12},{12,8},{16,20},{20,16},{24,28},{28,24},{32,36},... | collective-permute-start | bytes 6291464 | tf_op jit(solution)/shard_map/ppermute | solution.py:273
  15.3 4.4 %copy-start.6 = (s32[2,16]{1,0:T(2,128)S(1)}, s32[2,16]{1,0:T(2,128)}, u32[]{:S(2)}) copy-start(s32[2,16]{1,0:T(2,128)} %param.25) | copy-start | bytes 388
  15.3 6.5 %copy-start.4 = (s32[256,4]{0,1:T(4,128)S(1)}, s32[256,4]{0,1:T(4,128)}, u32[]{:S(2)}) copy-start(s32[256,4]{0,1:T(4,128)} %param.22) | copy-start | bytes 12292
  18.5 10.4 %collective-permute-start.1 = (bf16[256,512]{1,0:T(8,128)(2,1)}, bf16[256,512]{1,0:T(8,128)(2,1)S(1)}, u32[]{:S(2)}, u32[]{:S(2)}) collective-permute-start(bf16[256,512]{1,0:T(8,128)(2,1)} %get-tuple-element.3.kn_ref), channel_id=1, source_target_pairs={{0,1},{2,3},{4,5},{6,7},{8,9},{10,11},{12,13},{14,15},{16,17},{18,... | collective-permute-start | bytes 786440 | tf_op jit(solution)/shard_map/ppermute | solution.py:271
  19.8 6.2 %collective-permute-start = (s32[2,16]{1,0:T(2,128)S(1)}, s32[2,16]{1,0:T(2,128)S(1)}, u32[]{:S(2)}, u32[]{:S(2)}) collective-permute-start(s32[2,16]{1,0:T(2,128)S(1)} %copy-done.6), channel_id=1, source_target_pairs={{0,4},{4,0},{8,12},{12,8},{16,20},{20,16},{24,28},{28,24},{32,36},... | collective-permute-start | bytes 392 | tf_op jit(solution)/shard_map/ppermute | solution.py:273
  28.9 0.7 copy-start.3
  29.6 15.7 %copy-start.2 = (bf16[256,1536]{1,0:T(8,128)(2,1)S(1)}, bf16[256,1536]{1,0:T(8,128)(2,1)}, u32[]{:S(2)}) copy-start(bf16[256,1536]{1,0:T(8,128)(2,1)} %param.14) | copy-start | bytes 2359300
  45.2 4.1 %copy-start.5 = (f32[1536]{0:T(1024)S(1)}, f32[1536]{0:T(1024)}, u32[]{:S(2)}) copy-start(f32[1536]{0:T(1024)} %param.18) | copy-start | bytes 18436
  93.6 36.3 %all-to-all-start.1 = ((bf16[32,1,48,768]{3,2,1,0:T(8,128)(2,1)}), bf16[32,1,48,768]{3,2,1,0:T(8,128)(2,1)}, u32[]{:S(2)}, u32[]{:S(2)}) async-start(bf16[32,1,48,768]{3,2,1,0:T(8,128)(2,1)} %get-tuple-element.6), calls=%async_computation.1 | async-start | bytes 4718592 | tf_op jit(solution)/shard_map/all_to_all | solution.py:321
  139.2 2.2 %copy-start.7 = (bf16[1,768,1536]{2,1,0:T(8,128)(2,1)S(1)}, bf16[1,768,1536]{2,1,0:T(8,128)(2,1)}, u32[]{:S(2)}) copy-start(bf16[1,768,1536]{2,1,0:T(8,128)(2,1)} %param.21) | copy-start | bytes 7077892
  140.0 1.4 copy-start.1
  144.9 36.6 %all-to-all-start.2 = ((bf16[32,1,48,768]{3,2,1,0:T(8,128)(2,1)}), bf16[32,1,48,768]{3,2,1,0:T(8,128)(2,1)}, u32[]{:S(2)}, u32[]{:S(2)}) async-start(bf16[32,1,48,768]{3,2,1,0:T(8,128)(2,1)} %convert_bitcast_fusion.1), calls=%async_computation.2 | async-start | bytes 4718592 | tf_op jit(solution)/shard_map/all_to_all | solution.py:340
  181.5 36.6 %all-to-all-start.3 = ((bf16[32,1,48,768]{3,2,1,0:T(8,128)(2,1)}), bf16[32,1,48,768]{3,2,1,0:T(8,128)(2,1)}, u32[]{:S(2)}, u32[]{:S(2)}) async-start(bf16[32,1,48,768]{3,2,1,0:T(8,128)(2,1)} %convert_bitcast_fusion), calls=%async_computation.3 | async-start | bytes 4718592 | tf_op jit(solution)/shard_map/all_to_all | solution.py:340

commit v8 on v6

--- a/solution.py
+++ b/solution.py
@@ -157,15 +157,24 @@
         lax.fori_loop(0, count, wait_page, 0)
 
         def visit(i, carry):
-            first = pl.multiple_of(i * (2 * PAGE_CHUNK), 2 * PAGE_CHUNK)
+            first = pl.multiple_of(i * (4 * PAGE_CHUNK), 4 * PAGE_CHUNK)
+            absorb(
+                qg,
+                k_buf[c, pl.ds(first, 4 * PAGE_CHUNK), :],
+                v_buf[c, pl.ds(first, 4 * PAGE_CHUNK), :],
+            )
+            return carry
+
+        lax.fori_loop(0, count // 4, visit, 0)
+
+        @pl.when(count % 4 >= 2)
+        def _():
+            first = pl.multiple_of((count // 4) * (4 * PAGE_CHUNK), 4 * PAGE_CHUNK)
             absorb(
                 qg,
                 k_buf[c, pl.ds(first, 2 * PAGE_CHUNK), :],
                 v_buf[c, pl.ds(first, 2 * PAGE_CHUNK), :],
             )
-            return carry
-
-        lax.fori_loop(0, count // 2, visit, 0)
 
         @pl.when(count % 2 == 1)
         def _():

time: 203 us -> 201 us (level)
  Pallas kernels: 13.2 us -> 9.6 us
  blocking collectives: 69 us -> 72.2 us
    pallas_call x1, Pallas kernels: 10.1 us -> 6.48 us  [attend(): pl.pallas_call(functools.partial(attention_kernel, group=group, tokens=to...]
    all_to_all x1, blocking collectives: 69 us -> 72.2 us  [on_device(): lax.all_to_all(dispatch, 'req', split_axis=0, concat_axis=0, tiled=True)]
where the time goes in v8:
time: 201 us
  blocking collectives  72.2 us (36%)
  waiting for transfers between devices  61.7 us (31%)
  matrix products  32.8 us (16%)
  Pallas kernels  9.6 us (5%)
  starting transfers between devices  7.81 us (4%)
  other arithmetic  7.59 us (4%)
  between operations  5.35 us (3%)
  local copies, waits for them, and re-layouts  3.75 us (2%)
    all_to_all x1, blocking collectives, on_device(): lax.all_to_all(dispatch, 'req', split_axis=0, concat_axis=0, tiled=True)  72.2 us
    all_to_all x1, waiting for transfers between devices, on_device(): lax.all_to_all(result, 'req', split_axis=0, concat_axis=0, tiled=True)  58.9 us
    dot_general x1, matrix products, on_device(): jnp.einsum('nekd,edf->nekf', lax.all_to_all(dispatch, 'req', split_axis=0...  7.51 us
    pallas_call x1, Pallas kernels, attend(): pl.pallas_call(functools.partial(attention_kernel, group=group, tokens=to...  6.48 us
    dot_general x1, matrix products, on_device(): jnp.dot(normed, query_key_value_weight, preferred_element_type=jnp.float32)  6.23 us
    all_to_all x1, starting transfers between devices, on_device(): lax.all_to_all(result, 'req', split_axis=0, concat_axis=0, tiled=True)  5.85 us
    dot_general x1, matrix products, on_device(): jnp.einsum('nekf,efd->nekd', hidden, w_down, preferred_element_type=jnp.f...  5.47 us
    dot_general x1, matrix products, on_device(): jnp.dot(combine.astype(jnp.bfloat16), flat_results, preferred_element_typ...  5.1 us
  transfers between devices with their start and end apart: 5, of which 2 were waited for; matrix products, arithmetic and copies ran while one was open for 10% of the time, Pallas kernels for 2%

profile of v8, /device:TPU:56, one launch (start us, length us, event | category | flops | bytes accessed | tf_op | source)
XLA Modules:
  0.0 200.8 jit_solution(2438742365208446524)
XLA Ops:
  1.3 1.3 dynamic_slice.13
  4.5 1.3 dynamic_slice.14
  6.4 0.5 fusion.22
  7.0 0.9 pad_maximum_fusion
  7.8 1.4 fusion.10
  9.2 6.2 %fusion.15.proj_ref = f32[256,2048]{1,0:T(8,128)} fusion(bf16[1536,2048]{1,0:T(8,128)(2,1)} %param.16, bf16[256,1536]{1,0:T(8,128)(2,1)} %param.14, f32[1536]{0:T(1024)} %param.15, f32[256]{0:T(256)S(1)} %add_rsqrt_fusion.1), kind=kOutput, calls=%fused_computation.29 | convolution fusion | flops 1612185600 | bytes 9182208 | tf_op jit(solution)/shard_map/dot_general | solution.py:260
  15.5 3.1 %shard_map.149 = (bf16[256,1536]{1,0:T(8,128)(2,1)}, bf16[256,512]{1,0:T(8,128)(2,1)}) custom-call(f32[256,2048]{1,0:T(8,128)} %fusion.15.proj_ref, f32[256,128]{1,0:T(8,128)} %get-tuple-element.11.cos_ref, f32[256,128]{1,0:T(8,128)} %get-tuple-element.12.sin_ref), custom_call_target="tpu_custom_call" | custom-call | tf_op jit(solution)/shard_map/pallas_call | solution.py:67
  18.6 1.3 collective-permute-start.1
  22.1 0.5 fusion.14
  22.8 1.3 pad_add_fusion.meta_ref
  24.1 1.8 fusion
  26.5 2.8 %collective-permute-done.1.vn_ref = bf16[256,512]{1,0:T(8,128)(2,1)S(1)} collective-permute-done((bf16[256,512]{1,0:T(8,128)(2,1)}, bf16[256,512]{1,0:T(8,128)(2,1)S(1)}, u32[]{:S(2)}, u32[]{:S(2)}) %collective-permute-start.1) | collective-permute-done | bytes 262176 | tf_op jit(solution)/shard_map/ppermute | solution.py:280
  29.3 0.7 copy-done.3
  30.0 6.5 %shard_map.150 = bf16[256,1536]{1,0:T(8,128)(2,1)} custom-call(s32[3]{0:T(128)} %pad_add_fusion.meta_ref, s32[16]{0:T(128)} %fusion.23.page_ref, bf16[256,1536]{1,0:T(8,128)(2,1)} %get-tuple-element.4.q_ref, bf16[256,512]{1,0:T(8,128)(2,1)} %get-tuple-element.3.kn_ref, bf16[256,512]{1,0:T(8,128)(2,1)} %copy-done.3, bf16[32,128,256]{2,1,0:T(8,128)(2,1)} %k_own.1, ...), custom_call_target="tpu_custom_call" | custom-call | tf_op jit(solution)/shard_map/pallas_call | solution.py:201
  36.5 4.2 %multiply_reduce_fusion = (f32[256]{0:T(256)S(1)}, f32[256,1536]{1,0:T(8,128)S(1)}) fusion(bf16[256,1536]{1,0:T(8,128)(2,1)} %shard_map.150, bf16[1536,1536]{1,0:T(8,128)(2,1)} %param.17, bf16[256,1536]{1,0:T(8,128)(2,1)S(1)} %copy-done.2), kind=kOutput, calls=%fused_computation.26 | convolution fusion | flops 1209532160 | bytes 7865344 | tf_op jit(solution)/shard_map/dot_general | solution.py:294
  40.7 1.5 convolution_convert_fusion
  42.2 72.2 %all_to_all.10 = bf16[32,1,48,1536]{3,2,1,0:T(8,128)(2,1)S(1)} all-to-all(bf16[32,1,48,1536]{3,2,1,0:T(8,128)(2,1)S(1)} %bitcast.45), channel_id=1, replica_groups=mesh['req'=32,'head'=4] {'req'}, dimensions={0} | all-to-all | bytes 9437184 | tf_op jit(solution)/shard_map/all_to_all | solution.py:329
  114.4 7.5 %convolution_bitcast_fusion = f32[32,1,48,1536]{3,2,0,1:T(8,128)S(1)} fusion(bf16[1,1536,1536]{2,1,0:T(8,128)(2,1)S(1)} %bitcast.47, bf16[32,1,48,1536]{3,2,1,0:T(8,128)(2,1)S(1)} %all_to_all.10), kind=kOutput, calls=%fused_computation.5 | convolution fusion | flops 7247757312 | bytes 18874368 | tf_op jit(solution)/shard_map/nekd,edf->nekf/dot_general | solution.py:327
  122.0 5.5 %convert_bitcast_fusion = bf16[32,1,48,1536]{3,2,1,0:T(8,128)(2,1)} fusion(f32[32,1,48,1536]{3,2,0,1:T(8,128)S(1)} %convolution_bitcast_fusion, bf16[1,768,1536]{2,1,0:T(8,128)(2,1)S(1)} %copy-done), kind=kOutput, calls=%fused_computation.11 | convolution fusion | flops 3629776896 | bytes 16515072 | tf_op jit(solution)/shard_map/nekf,efd->nekd/dot_general | solution.py:334
  127.4 5.9 %all-to-all-start.1 = ((bf16[32,1,48,1536]{3,2,1,0:T(8,128)(2,1)}), bf16[32,1,48,1536]{3,2,1,0:T(8,128)(2,1)}, u32[]{:S(2)}, u32[]{:S(2)}) async-start(bf16[32,1,48,1536]{3,2,1,0:T(8,128)(2,1)} %convert_bitcast_fusion), calls=%async_computation.1 | async-start | bytes 9437184 | tf_op jit(solution)/shard_map/all_to_all | solution.py:337
  133.3 2.3 %fusion.25 = f32[256,32]{0,1:T(8,128)S(1)} fusion(f32[1536,32]{0,1:T(8,128)S(1)} %copy-done.4, f32[256,1536]{1,0:T(8,128)} %copy-done.1, f32[1536]{0:T(1024)S(1)} %copy-done.6, f32[256]{0:T(256)S(1)} %add_rsqrt_fusion), kind=kOutput, calls=%fused_computation.55 | convolution fusion | flops 152174592 | bytes 1809408 | tf_op jit(solution)/shard_map/dot_general | solution.py:298
  135.7 1.1 select_reduce_fusion
  136.8 58.9 %all-to-all-done.1 = bf16[32,1,48,1536]{3,2,1,0:T(8,128)(2,1)} async-done(((bf16[32,1,48,1536]{3,2,1,0:T(8,128)(2,1)}), bf16[32,1,48,1536]{3,2,1,0:T(8,128)(2,1)}, u32[]{:S(2)}, u32[]{:S(2)}) %all-to-all-start.1) | async-done | bytes 4718624 | tf_op jit(solution)/shard_map/all_to_all | solution.py:337
  195.7 5.1 %fusion.5 = bf16[256,1536]{1,0:T(8,128)(2,1)} fusion(f32[256,1536]{1,0:T(8,128)} %copy-done.1, bf16[1536,1536]{1,0:T(8,128)(2,1)} %bitcast.22, bf16[256,1536]{1,0:T(8,128)(2,1)S(1)} %select_reduce_fusion), kind=kOutput, calls=%fused_computation.16 | convolution fusion | flops 1208745984 | bytes 7864320 | tf_op jit(solution)/shard_map/dot_general | solution.py:342
  (40 shorter events, 1.8 us)
Async XLA Ops:
  0.6 121.3 %copy-start = (bf16[1,768,1536]{2,1,0:T(8,128)(2,1)S(1)}, bf16[1,768,1536]{2,1,0:T(8,128)(2,1)}, u32[]{:S(2)}) copy-start(bf16[1,768,1536]{2,1,0:T(8,128)(2,1)} %param.21) | copy-start | bytes 7077892
  0.6 25.3 %collective-permute-start = (s32[2,16]{1,0:T(2,128)}, s32[2,16]{1,0:T(2,128)S(1)}, u32[]{:S(2)}, u32[]{:S(2)}) collective-permute-start(s32[2,16]{1,0:T(2,128)} %param.25), channel_id=1, source_target_pairs={{0,4},{4,0},{8,12},{12,8},{16,20},{20,16},{24,28},{28,24},{32,36},... | collective-permute-start | bytes 392 | tf_op jit(solution)/shard_map/ppermute | solution.py:282
  0.7 28.5 %collective-permute-start.2 = (bf16[32,128,256]{2,1,0:T(8,128)(2,1)}, bf16[32,128,256]{2,1,0:T(8,128)(2,1)}, u32[]{:S(2)}, u32[]{:S(2)}) collective-permute-start(bf16[32,128,256]{2,1,0:T(8,128)(2,1)} %k_own.1), channel_id=1, source_target_pairs={{0,4},{4,0},{8,12},{12,8},{16,20},{20,16},{24,28},{28,24},{32,36},... | collective-permute-start | bytes 6291464 | tf_op jit(solution)/shard_map/ppermute | solution.py:282
  1.2 28.0 %collective-permute-start.3 = (bf16[32,128,256]{2,1,0:T(8,128)(2,1)}, bf16[32,128,256]{2,1,0:T(8,128)(2,1)}, u32[]{:S(2)}, u32[]{:S(2)}) collective-permute-start(bf16[32,128,256]{2,1,0:T(8,128)(2,1)} %v_own.1), channel_id=1, source_target_pairs={{0,4},{4,0},{8,12},{12,8},{16,20},{20,16},{24,28},{28,24},{32,36},... | collective-permute-start | bytes 6291464 | tf_op jit(solution)/shard_map/ppermute | solution.py:282
  9.2 12.6 %copy-start.5 = (s32[256,4]{0,1:T(4,128)S(1)}, s32[256,4]{0,1:T(4,128)}, u32[]{:S(2)}) copy-start(s32[256,4]{0,1:T(4,128)} %param.22) | copy-start | bytes 12292
  15.5 10.5 %copy-start.7 = (s32[2,16]{1,0:T(2,128)S(1)}, s32[2,16]{1,0:T(2,128)}, u32[]{:S(2)}) copy-start(s32[2,16]{1,0:T(2,128)} %param.25) | copy-start | bytes 388
  18.6 10.7 %collective-permute-start.1 = (bf16[256,512]{1,0:T(8,128)(2,1)}, bf16[256,512]{1,0:T(8,128)(2,1)S(1)}, u32[]{:S(2)}, u32[]{:S(2)}) collective-permute-start(bf16[256,512]{1,0:T(8,128)(2,1)} %get-tuple-element.3.kn_ref), channel_id=1, source_target_pairs={{0,1},{2,3},{4,5},{6,7},{8,9},{10,11},{12,13},{14,15},{16,17},{18,... | collective-permute-start | bytes 786440 | tf_op jit(solution)/shard_map/ppermute | solution.py:280
  29.3 0.7 copy-start.3
  30.0 6.5 %copy-start.2 = (bf16[256,1536]{1,0:T(8,128)(2,1)S(1)}, bf16[256,1536]{1,0:T(8,128)(2,1)}, u32[]{:S(2)}) copy-start(bf16[256,1536]{1,0:T(8,128)(2,1)} %param.14) | copy-start | bytes 2359300
  36.5 4.2 %copy-start.6 = (f32[1536]{0:T(1024)S(1)}, f32[1536]{0:T(1024)}, u32[]{:S(2)}) copy-start(f32[1536]{0:T(1024)} %param.18) | copy-start | bytes 18436
  36.5 77.9 %slice-start = ((s8[4718592]{0:T(1024)(128)(4,1)}), s8[4194304]{0:T(1024)(128)(4,1)S(1)}, s32[]{:S(2)}) async-start(s8[4718592]{0:T(1024)(128)(4,1)} %bitcast.46), calls=%async_computation.2 | async-start | bytes 8388608
  40.7 1.5 copy-start.1
  40.7 73.7 %slice-start.1 = ((s8[4718592]{0:T(1024)(128)(4,1)}), s8[524288]{0:T(1024)(128)(4,1)S(1)}, s32[]{:S(2)}) async-start(s8[4718592]{0:T(1024)(128)(4,1)} %bitcast.46), calls=%async_computation.3 | async-start | bytes 1048576
  127.4 5.9 %copy-start.4 = (f32[1536,32]{0,1:T(8,128)S(1)}, f32[1536,32]{0,1:T(8,128)}, u32[]{:S(2)}) copy-start(f32[1536,32]{0,1:T(8,128)} %param.19) | copy-start | bytes 589828
  127.4 68.2 %all-to-all-start.1 = ((bf16[32,1,48,1536]{3,2,1,0:T(8,128)(2,1)}), bf16[32,1,48,1536]{3,2,1,0:T(8,128)(2,1)}, u32[]{:S(2)}, u32[]{:S(2)}) async-start(bf16[32,1,48,1536]{3,2,1,0:T(8,128)(2,1)} %convert_bitcast_fusion), calls=%async_computation.1 | async-start | bytes 9437184 | tf_op jit(solution)/shard_map/all_to_all | solution.py:337

commit v9 on v8

--- a/solution.py
+++ b/solution.py
@@ -112,12 +112,12 @@
         start_all(k_own, v_own)
 
     def absorb(qg, k, v):
-        s = lax.dot_general(qg, k, contract, preferred_element_type=jnp.float32) * scaling
+        s = lax.dot_general(qg, k, contract, preferred_element_type=jnp.float32)
         m_prev = m_sc[...]
-        m_next = jnp.maximum(m_prev, jnp.max(s, axis=1, keepdims=True))
+        m_next = jnp.maximum(m_prev, jnp.max(s, axis=1, keepdims=True) * scaling)
         repeat = s.shape[1] // lanes
         wide = m_next if repeat == 1 else jnp.concatenate([m_next] * repeat, axis=1)
-        p = jnp.exp(s - wide)
+        p = jnp.exp(s * scaling - wide)
         alpha = jnp.exp(m_prev - m_next)
         l_sc[...] = alpha * l_sc[...] + jnp.sum(p, axis=1, keepdims=True)
         acc_sc[...] = acc_sc[...] * alpha + jnp.dot(
@@ -133,12 +133,11 @@
         key_cols = slice(c * HEAD_SIZE, (c + 1) * HEAD_SIZE)
         value_cols = slice((KEY_VALUE_HEADS + c) * HEAD_SIZE, (KEY_VALUE_HEADS + c + 1) * HEAD_SIZE)
         s = lax.dot_general(qg, kn_ref[:, key_cols], contract, preferred_element_type=jnp.float32)
-        s = s * scaling
         t = lax.broadcasted_iota(jnp.int32, s.shape, 0) % tokens
         key_pos = lax.broadcasted_iota(jnp.int32, s.shape, 1)
         s = jnp.where(key_pos <= t, s, -jnp.inf)
-        m = jnp.max(s, axis=1, keepdims=True)
-        p = jnp.exp(s - m)
+        m = jnp.max(s, axis=1, keepdims=True) * scaling
+        p = jnp.exp(s * scaling - m)
         l_sc[...] = jnp.broadcast_to(jnp.sum(p, axis=1, keepdims=True), l_sc.shape)
         m_sc[...] = jnp.broadcast_to(m, m_sc.shape)
         acc_sc[...] = jnp.dot(

time: 201 us -> 203 us (level)
  Pallas kernels: 9.6 us -> 12.9 us
  blocking collectives: 72.2 us -> 69.8 us
    pallas_call x1, Pallas kernels: 6.48 us -> 9.76 us  [attend(): pl.pallas_call(functools.partial(attention_kernel, group=group, tokens=to...]
    all_to_all x1, blocking collectives: 72.2 us -> 69.8 us  [on_device(): lax.all_to_all(dispatch, 'req', split_axis=0, concat_axis=0, tiled=True)]
where the time goes in v9:
time: 203 us; the launch traced here: 202 us
  blocking collectives  69.8 us (34%)
  waiting for transfers between devices  61.7 us (30%)
  matrix products  32.8 us (16%)
  Pallas kernels  12.9 us (6%)
  starting transfers between devices  7.81 us (4%)
  other arithmetic  7.59 us (4%)
  between operations  5.35 us (3%)
  local copies, waits for them, and re-layouts  3.75 us (2%)
    all_to_all x1, blocking collectives, on_device(): lax.all_to_all(dispatch, 'req', split_axis=0, concat_axis=0, tiled=True)  69.8 us
    all_to_all x1, waiting for transfers between devices, on_device(): lax.all_to_all(result, 'req', split_axis=0, concat_axis=0, tiled=True)  58.9 us
    pallas_call x1, Pallas kernels, attend(): pl.pallas_call(functools.partial(attention_kernel, group=group, tokens=to...  9.76 us
    dot_general x1, matrix products, on_device(): jnp.einsum('nekd,edf->nekf', lax.all_to_all(dispatch, 'req', split_axis=0...  7.51 us
    dot_general x1, matrix products, on_device(): jnp.dot(normed, query_key_value_weight, preferred_element_type=jnp.float32)  6.23 us
    all_to_all x1, starting transfers between devices, on_device(): lax.all_to_all(result, 'req', split_axis=0, concat_axis=0, tiled=True)  5.85 us
    dot_general x1, matrix products, on_device(): jnp.einsum('nekf,efd->nekd', hidden, w_down, preferred_element_type=jnp.f...  5.47 us
    dot_general x1, matrix products, on_device(): jnp.dot(combine.astype(jnp.bfloat16), flat_results, preferred_element_typ...  5.1 us
  transfers between devices with their start and end apart: 5, of which 2 were waited for; matrix products, arithmetic and copies ran while one was open for 10% of the time, Pallas kernels for 2%

profile of v9, /device:TPU:56, one launch (start us, length us, event | category | flops | bytes accessed | tf_op | source)
XLA Modules:
  0.0 201.6 jit_solution(2297128602629934090)
XLA Ops:
  1.3 1.3 dynamic_slice.13
  4.5 1.3 dynamic_slice.14
  6.4 0.5 fusion.22
  7.0 0.9 pad_maximum_fusion
  7.8 1.4 fusion.10
  9.2 6.2 %fusion.15.proj_ref = f32[256,2048]{1,0:T(8,128)} fusion(bf16[1536,2048]{1,0:T(8,128)(2,1)} %param.16, bf16[256,1536]{1,0:T(8,128)(2,1)} %param.14, f32[1536]{0:T(1024)} %param.15, f32[256]{0:T(256)S(1)} %add_rsqrt_fusion.1), kind=kOutput, calls=%fused_computation.29 | convolution fusion | flops 1612185600 | bytes 9182208 | tf_op jit(solution)/shard_map/dot_general | solution.py:259
  15.5 3.1 %shard_map.149 = (bf16[256,1536]{1,0:T(8,128)(2,1)}, bf16[256,512]{1,0:T(8,128)(2,1)}) custom-call(f32[256,2048]{1,0:T(8,128)} %fusion.15.proj_ref, f32[256,128]{1,0:T(8,128)} %get-tuple-element.11.cos_ref, f32[256,128]{1,0:T(8,128)} %get-tuple-element.12.sin_ref), custom_call_target="tpu_custom_call" | custom-call | tf_op jit(solution)/shard_map/pallas_call | solution.py:67
  18.6 1.3 collective-permute-start.1
  22.1 0.5 fusion.14
  22.8 1.3 pad_add_fusion.meta_ref
  24.1 1.8 fusion
  26.5 2.8 %collective-permute-done.1.vn_ref = bf16[256,512]{1,0:T(8,128)(2,1)S(1)} collective-permute-done((bf16[256,512]{1,0:T(8,128)(2,1)}, bf16[256,512]{1,0:T(8,128)(2,1)S(1)}, u32[]{:S(2)}, u32[]{:S(2)}) %collective-permute-start.1) | collective-permute-done | bytes 262176 | tf_op jit(solution)/shard_map/ppermute | solution.py:279
  29.3 0.7 copy-done.3
  30.0 9.8 %shard_map.150 = bf16[256,1536]{1,0:T(8,128)(2,1)} custom-call(s32[3]{0:T(128)} %pad_add_fusion.meta_ref, s32[16]{0:T(128)} %fusion.23.page_ref, bf16[256,1536]{1,0:T(8,128)(2,1)} %get-tuple-element.4.q_ref, bf16[256,512]{1,0:T(8,128)(2,1)} %get-tuple-element.3.kn_ref, bf16[256,512]{1,0:T(8,128)(2,1)} %copy-done.3, bf16[32,128,256]{2,1,0:T(8,128)(2,1)} %k_own.1, ...), custom_call_target="tpu_custom_call" | custom-call | tf_op jit(solution)/shard_map/pallas_call | solution.py:200
  39.8 4.2 %multiply_reduce_fusion = (f32[256]{0:T(256)S(1)}, f32[256,1536]{1,0:T(8,128)S(1)}) fusion(bf16[256,1536]{1,0:T(8,128)(2,1)} %shard_map.150, bf16[1536,1536]{1,0:T(8,128)(2,1)} %param.17, bf16[256,1536]{1,0:T(8,128)(2,1)S(1)} %copy-done.2), kind=kOutput, calls=%fused_computation.26 | convolution fusion | flops 1209532160 | bytes 7865344 | tf_op jit(solution)/shard_map/dot_general | solution.py:293
  44.0 1.5 convolution_convert_fusion
  45.5 69.8 %all_to_all.10 = bf16[32,1,48,1536]{3,2,1,0:T(8,128)(2,1)S(1)} all-to-all(bf16[32,1,48,1536]{3,2,1,0:T(8,128)(2,1)S(1)} %bitcast.45), channel_id=1, replica_groups=mesh['req'=32,'head'=4] {'req'}, dimensions={0} | all-to-all | bytes 9437184 | tf_op jit(solution)/shard_map/all_to_all | solution.py:328
  115.3 7.5 %convolution_bitcast_fusion = f32[32,1,48,1536]{3,2,0,1:T(8,128)S(1)} fusion(bf16[1,1536,1536]{2,1,0:T(8,128)(2,1)S(1)} %bitcast.47, bf16[32,1,48,1536]{3,2,1,0:T(8,128)(2,1)S(1)} %all_to_all.10), kind=kOutput, calls=%fused_computation.5 | convolution fusion | flops 7247757312 | bytes 18874368 | tf_op jit(solution)/shard_map/nekd,edf->nekf/dot_general | solution.py:326
  122.8 5.5 %convert_bitcast_fusion = bf16[32,1,48,1536]{3,2,1,0:T(8,128)(2,1)} fusion(f32[32,1,48,1536]{3,2,0,1:T(8,128)S(1)} %convolution_bitcast_fusion, bf16[1,768,1536]{2,1,0:T(8,128)(2,1)S(1)} %copy-done), kind=kOutput, calls=%fused_computation.11 | convolution fusion | flops 3629776896 | bytes 16515072 | tf_op jit(solution)/shard_map/nekf,efd->nekd/dot_general | solution.py:333
  128.3 5.9 %all-to-all-start.1 = ((bf16[32,1,48,1536]{3,2,1,0:T(8,128)(2,1)}), bf16[32,1,48,1536]{3,2,1,0:T(8,128)(2,1)}, u32[]{:S(2)}, u32[]{:S(2)}) async-start(bf16[32,1,48,1536]{3,2,1,0:T(8,128)(2,1)} %convert_bitcast_fusion), calls=%async_computation.1 | async-start | bytes 9437184 | tf_op jit(solution)/shard_map/all_to_all | solution.py:336
  134.2 2.3 %fusion.25 = f32[256,32]{0,1:T(8,128)S(1)} fusion(f32[1536,32]{0,1:T(8,128)S(1)} %copy-done.4, f32[256,1536]{1,0:T(8,128)} %copy-done.1, f32[1536]{0:T(1024)S(1)} %copy-done.6, f32[256]{0:T(256)S(1)} %add_rsqrt_fusion), kind=kOutput, calls=%fused_computation.55 | convolution fusion | flops 152174592 | bytes 1809408 | tf_op jit(solution)/shard_map/dot_general | solution.py:297
  136.5 1.1 select_reduce_fusion
  137.6 58.9 %all-to-all-done.1 = bf16[32,1,48,1536]{3,2,1,0:T(8,128)(2,1)} async-done(((bf16[32,1,48,1536]{3,2,1,0:T(8,128)(2,1)}), bf16[32,1,48,1536]{3,2,1,0:T(8,128)(2,1)}, u32[]{:S(2)}, u32[]{:S(2)}) %all-to-all-start.1) | async-done | bytes 4718624 | tf_op jit(solution)/shard_map/all_to_all | solution.py:336
  196.5 5.1 %fusion.5 = bf16[256,1536]{1,0:T(8,128)(2,1)} fusion(f32[256,1536]{1,0:T(8,128)} %copy-done.1, bf16[1536,1536]{1,0:T(8,128)(2,1)} %bitcast.22, bf16[256,1536]{1,0:T(8,128)(2,1)S(1)} %select_reduce_fusion), kind=kOutput, calls=%fused_computation.16 | convolution fusion | flops 1208745984 | bytes 7864320 | tf_op jit(solution)/shard_map/dot_general | solution.py:341
  (40 shorter events, 1.8 us)
Async XLA Ops:
  0.6 122.2 %copy-start = (bf16[1,768,1536]{2,1,0:T(8,128)(2,1)S(1)}, bf16[1,768,1536]{2,1,0:T(8,128)(2,1)}, u32[]{:S(2)}) copy-start(bf16[1,768,1536]{2,1,0:T(8,128)(2,1)} %param.21) | copy-start | bytes 7077892
  0.6 25.3 %collective-permute-start = (s32[2,16]{1,0:T(2,128)}, s32[2,16]{1,0:T(2,128)S(1)}, u32[]{:S(2)}, u32[]{:S(2)}) collective-permute-start(s32[2,16]{1,0:T(2,128)} %param.25), channel_id=1, source_target_pairs={{0,4},{4,0},{8,12},{12,8},{16,20},{20,16},{24,28},{28,24},{32,36},... | collective-permute-start | bytes 392 | tf_op jit(solution)/shard_map/ppermute | solution.py:281
  0.7 28.5 %collective-permute-start.2 = (bf16[32,128,256]{2,1,0:T(8,128)(2,1)}, bf16[32,128,256]{2,1,0:T(8,128)(2,1)}, u32[]{:S(2)}, u32[]{:S(2)}) collective-permute-start(bf16[32,128,256]{2,1,0:T(8,128)(2,1)} %k_own.1), channel_id=1, source_target_pairs={{0,4},{4,0},{8,12},{12,8},{16,20},{20,16},{24,28},{28,24},{32,36},... | collective-permute-start | bytes 6291464 | tf_op jit(solution)/shard_map/ppermute | solution.py:281
  1.2 28.0 %collective-permute-start.3 = (bf16[32,128,256]{2,1,0:T(8,128)(2,1)}, bf16[32,128,256]{2,1,0:T(8,128)(2,1)}, u32[]{:S(2)}, u32[]{:S(2)}) collective-permute-start(bf16[32,128,256]{2,1,0:T(8,128)(2,1)} %v_own.1), channel_id=1, source_target_pairs={{0,4},{4,0},{8,12},{12,8},{16,20},{20,16},{24,28},{28,24},{32,36},... | collective-permute-start | bytes 6291464 | tf_op jit(solution)/shard_map/ppermute | solution.py:281
  9.2 12.6 %copy-start.5 = (s32[256,4]{0,1:T(4,128)S(1)}, s32[256,4]{0,1:T(4,128)}, u32[]{:S(2)}) copy-start(s32[256,4]{0,1:T(4,128)} %param.22) | copy-start | bytes 12292
  15.5 10.5 %copy-start.7 = (s32[2,16]{1,0:T(2,128)S(1)}, s32[2,16]{1,0:T(2,128)}, u32[]{:S(2)}) copy-start(s32[2,16]{1,0:T(2,128)} %param.25) | copy-start | bytes 388
  18.6 10.7 %collective-permute-start.1 = (bf16[256,512]{1,0:T(8,128)(2,1)}, bf16[256,512]{1,0:T(8,128)(2,1)S(1)}, u32[]{:S(2)}, u32[]{:S(2)}) collective-permute-start(bf16[256,512]{1,0:T(8,128)(2,1)} %get-tuple-element.3.kn_ref), channel_id=1, source_target_pairs={{0,1},{2,3},{4,5},{6,7},{8,9},{10,11},{12,13},{14,15},{16,17},{18,... | collective-permute-start | bytes 786440 | tf_op jit(solution)/shard_map/ppermute | solution.py:279
  29.3 0.7 copy-start.3
  30.0 9.8 %copy-start.2 = (bf16[256,1536]{1,0:T(8,128)(2,1)S(1)}, bf16[256,1536]{1,0:T(8,128)(2,1)}, u32[]{:S(2)}) copy-start(bf16[256,1536]{1,0:T(8,128)(2,1)} %param.14) | copy-start | bytes 2359300
  39.8 4.2 %copy-start.6 = (f32[1536]{0:T(1024)S(1)}, f32[1536]{0:T(1024)}, u32[]{:S(2)}) copy-start(f32[1536]{0:T(1024)} %param.18) | copy-start | bytes 18436
  39.8 75.5 %slice-start = ((s8[4718592]{0:T(1024)(128)(4,1)}), s8[4194304]{0:T(1024)(128)(4,1)S(1)}, s32[]{:S(2)}) async-start(s8[4718592]{0:T(1024)(128)(4,1)} %bitcast.46), calls=%async_computation.2 | async-start | bytes 8388608
  44.0 1.5 copy-start.1
  44.0 71.3 %slice-start.1 = ((s8[4718592]{0:T(1024)(128)(4,1)}), s8[524288]{0:T(1024)(128)(4,1)S(1)}, s32[]{:S(2)}) async-start(s8[4718592]{0:T(1024)(128)(4,1)} %bitcast.46), calls=%async_computation.3 | async-start | bytes 1048576
  128.3 5.9 %copy-start.4 = (f32[1536,32]{0,1:T(8,128)S(1)}, f32[1536,32]{0,1:T(8,128)}, u32[]{:S(2)}) copy-start(f32[1536,32]{0,1:T(8,128)} %param.19) | copy-start | bytes 589828
  128.3 68.2 %all-to-all-start.1 = ((bf16[32,1,48,1536]{3,2,1,0:T(8,128)(2,1)}), bf16[32,1,48,1536]{3,2,1,0:T(8,128)(2,1)}, u32[]{:S(2)}, u32[]{:S(2)}) async-start(bf16[32,1,48,1536]{3,2,1,0:T(8,128)(2,1)} %convert_bitcast_fusion), calls=%async_computation.1 | async-start | bytes 9437184 | tf_op jit(solution)/shard_map/all_to_all | solution.py:336

commit v10 on v9

--- a/solution.py
+++ b/solution.py
@@ -251,9 +251,11 @@
 
     request = (req_index * count_of_heads + head_index) // share
     half = head_index % share
-    old_id = anchor[request]
+    request_ids = jnp.arange(anchor.shape[0], dtype=jnp.int32)
+    old_id = jnp.sum(jnp.where(request_ids == request, anchor, 0))
+    base_pages = jnp.sum(jnp.where(request_ids == old_id, cached_pages, 0))
     place = half * tokens_per_device + jnp.arange(tokens_per_device, dtype=jnp.int32)
-    token_positions = cached_pages[old_id] * page_size + place
+    token_positions = base_pages * page_size + place
 
     normed = rms_scale(tokens.astype(jnp.float32), norm1_gain).astype(jnp.bfloat16)
     projected_rows = jnp.dot(normed, query_key_value_weight, preferred_element_type=jnp.float32)
@@ -282,9 +284,10 @@
         (key_page_store, value_page_store, page_table), "req", pairs
     )
     moved_in = old_id // req_dev != req_index
-    page_ids = jnp.where(moved_in, table_got[old_id % req_dev], page_table[old_id % req_dev])
+    row_pick = (jnp.arange(req_dev, dtype=jnp.int32) == old_id % req_dev)[:, None]
+    page_ids = jnp.sum(jnp.where(row_pick, jnp.where(moved_in, table_got, page_table), 0), axis=0)
     meta = jnp.stack(
-        [cached_pages[old_id], half.astype(jnp.int32), moved_in.astype(jnp.int32)]
+        [base_pages, half.astype(jnp.int32), moved_in.astype(jnp.int32)]
     ).astype(jnp.int32)
     attention = attend(
         meta, page_ids, queries, appended, earlier, key_page_store, value_page_store, k_got, v_got,

time: 203 us -> 202 us (level)
  other arithmetic: 7.59 us -> 10.9 us
  local copies, waits for them, and re-layouts: 3.75 us -> 1.22 us
    reduce_sum x0 -> x3, other arithmetic: none -> 3.89 us  [the longest x1 1.93 us: on_device(): base_pages = jnp.sum(jnp.where(request_ids == old_id, cached_pages, 0))]
    dynamic_slice x2 -> x0, local copies, waits for them, and re-layouts: 2.55 us -> none  [the longest x1 1.28 us: on_device(): old_id = anchor[request]]
where the time goes in v10:
time: 202 us
  blocking collectives  71.6 us (35%)
  waiting for transfers between devices  61.2 us (30%)
  matrix products  32.8 us (16%)
  Pallas kernels  12.9 us (6%)
  other arithmetic  10.9 us (5%)
  starting transfers between devices  7.81 us (4%)
  between operations  3.85 us (2%)
    all_to_all x1, blocking collectives, on_device(): lax.all_to_all(dispatch, 'req', split_axis=0, concat_axis=0, tiled=True)  71.6 us
    all_to_all x1, waiting for transfers between devices, on_device(): lax.all_to_all(result, 'req', split_axis=0, concat_axis=0, tiled=True)  58.8 us
    pallas_call x1, Pallas kernels, attend(): pl.pallas_call(functools.partial(attention_kernel, group=group, tokens=to...  9.75 us
    dot_general x1, matrix products, on_device(): jnp.einsum('nekd,edf->nekf', lax.all_to_all(dispatch, 'req', split_axis=0...  7.51 us
    dot_general x1, matrix products, on_device(): jnp.dot(normed, query_key_value_weight, preferred_element_type=jnp.float32)  6.24 us
    all_to_all x1, starting transfers between devices, on_device(): lax.all_to_all(result, 'req', split_axis=0, concat_axis=0, tiled=True)  5.85 us
    dot_general x1, matrix products, on_device(): jnp.einsum('nekf,efd->nekd', hidden, w_down, preferred_element_type=jnp.f...  5.48 us
    dot_general x1, matrix products, on_device(): jnp.dot(combine.astype(jnp.bfloat16), flat_results, preferred_element_typ...  5.1 us
  transfers between devices with their start and end apart: 5, of which 2 were waited for; matrix products, arithmetic and copies ran while one was open for 10% of the time, Pallas kernels for 2%

profile of v10, /device:TPU:56, one launch (start us, length us, event | category | flops | bytes accessed | tf_op | source)
XLA Modules:
  0.0 202.2 jit_solution(17554328175566551907)
XLA Ops:
  1.3 1.3 fusion.23
  2.6 1.9 fusion.24
  5.8 0.8 pad_maximum_fusion
  6.6 1.4 fusion.10
  8.0 6.2 %fusion.15.proj_ref = f32[256,2048]{1,0:T(8,128)} fusion(bf16[1536,2048]{1,0:T(8,128)(2,1)} %param.16, bf16[256,1536]{1,0:T(8,128)(2,1)} %param.14, f32[1536]{0:T(1024)} %param.15, f32[256]{0:T(256)S(1)} %add_rsqrt_fusion.1), kind=kOutput, calls=%fused_computation.29 | convolution fusion | flops 1612185600 | bytes 9182208 | tf_op jit(solution)/shard_map/dot_general | solution.py:261
  14.2 3.1 %shard_map.149 = (bf16[256,1536]{1,0:T(8,128)(2,1)}, bf16[256,512]{1,0:T(8,128)(2,1)}) custom-call(f32[256,2048]{1,0:T(8,128)} %fusion.15.proj_ref, f32[256,128]{1,0:T(8,128)} %get-tuple-element.11.cos_ref, f32[256,128]{1,0:T(8,128)} %get-tuple-element.12.sin_ref), custom_call_target="tpu_custom_call" | custom-call | tf_op jit(solution)/shard_map/pallas_call | solution.py:67
  17.4 1.3 collective-permute-start.1
  20.7 0.5 fusion.14
  21.4 1.8 fusion
  23.9 1.2 pad_add_fusion.meta_ref
  25.1 0.7 select_reduce_fusion.2.page_ref
  25.8 2.3 %collective-permute-done.1.vn_ref = bf16[256,512]{1,0:T(8,128)(2,1)S(1)} collective-permute-done((bf16[256,512]{1,0:T(8,128)(2,1)}, bf16[256,512]{1,0:T(8,128)(2,1)S(1)}, u32[]{:S(2)}, u32[]{:S(2)}) %collective-permute-start.1) | collective-permute-done | bytes 262176 | tf_op jit(solution)/shard_map/ppermute | solution.py:281
  28.1 0.7 copy-done.3
  28.8 9.8 %shard_map.150 = bf16[256,1536]{1,0:T(8,128)(2,1)} custom-call(s32[3]{0:T(128)} %pad_add_fusion.meta_ref, s32[16]{0:T(128)} %select_reduce_fusion.2.page_ref, bf16[256,1536]{1,0:T(8,128)(2,1)} %get-tuple-element.4.q_ref, bf16[256,512]{1,0:T(8,128)(2,1)} %get-tuple-element.3.kn_ref, bf16[256,512]{1,0:T(8,128)(2,1)} %copy-done.3, bf16[32,128,256]{2,1,0:T(8,128)(2,1)} %k_own.1, ...), custom_call_target="tpu_custom_call" | custom-call | tf_op jit(solution)/shard_map/pallas_call | solution.py:200
  38.6 4.2 %multiply_reduce_fusion = (f32[256]{0:T(256)S(1)}, f32[256,1536]{1,0:T(8,128)S(1)}) fusion(bf16[256,1536]{1,0:T(8,128)(2,1)} %shard_map.150, bf16[1536,1536]{1,0:T(8,128)(2,1)} %param.17, bf16[256,1536]{1,0:T(8,128)(2,1)S(1)} %copy-done.2), kind=kOutput, calls=%fused_computation.26 | convolution fusion | flops 1209532160 | bytes 7865344 | tf_op jit(solution)/shard_map/dot_general | solution.py:296
  42.8 1.5 convolution_convert_fusion
  44.3 71.6 %all_to_all.10 = bf16[32,1,48,1536]{3,2,1,0:T(8,128)(2,1)S(1)} all-to-all(bf16[32,1,48,1536]{3,2,1,0:T(8,128)(2,1)S(1)} %bitcast.42), channel_id=1, replica_groups=mesh['req'=32,'head'=4] {'req'}, dimensions={0} | all-to-all | bytes 9437184 | tf_op jit(solution)/shard_map/all_to_all | solution.py:331
  116.0 7.5 %convolution_bitcast_fusion = f32[32,1,48,1536]{3,2,0,1:T(8,128)S(1)} fusion(bf16[1,1536,1536]{2,1,0:T(8,128)(2,1)S(1)} %bitcast.44, bf16[32,1,48,1536]{3,2,1,0:T(8,128)(2,1)S(1)} %all_to_all.10), kind=kOutput, calls=%fused_computation.5 | convolution fusion | flops 7247757312 | bytes 18874368 | tf_op jit(solution)/shard_map/nekd,edf->nekf/dot_general | solution.py:329
  123.5 5.5 %convert_bitcast_fusion = bf16[32,1,48,1536]{3,2,1,0:T(8,128)(2,1)} fusion(f32[32,1,48,1536]{3,2,0,1:T(8,128)S(1)} %convolution_bitcast_fusion, bf16[1,768,1536]{2,1,0:T(8,128)(2,1)S(1)} %copy-done), kind=kOutput, calls=%fused_computation.11 | convolution fusion | flops 3629776896 | bytes 16515072 | tf_op jit(solution)/shard_map/nekf,efd->nekd/dot_general | solution.py:336
  129.0 5.9 %all-to-all-start.1 = ((bf16[32,1,48,1536]{3,2,1,0:T(8,128)(2,1)}), bf16[32,1,48,1536]{3,2,1,0:T(8,128)(2,1)}, u32[]{:S(2)}, u32[]{:S(2)}) async-start(bf16[32,1,48,1536]{3,2,1,0:T(8,128)(2,1)} %convert_bitcast_fusion), calls=%async_computation.1 | async-start | bytes 9437184 | tf_op jit(solution)/shard_map/all_to_all | solution.py:339
  134.8 2.3 %fusion.26 = f32[256,32]{0,1:T(8,128)S(1)} fusion(f32[1536,32]{0,1:T(8,128)S(1)} %copy-done.4, f32[256,1536]{1,0:T(8,128)} %copy-done.1, f32[1536]{0:T(1024)S(1)} %copy-done.6, f32[256]{0:T(256)S(1)} %add_rsqrt_fusion), kind=kOutput, calls=%fused_computation.59 | convolution fusion | flops 152174592 | bytes 1809408 | tf_op jit(solution)/shard_map/dot_general | solution.py:300
  137.2 1.1 select_reduce_fusion
  138.3 58.8 %all-to-all-done.1 = bf16[32,1,48,1536]{3,2,1,0:T(8,128)(2,1)} async-done(((bf16[32,1,48,1536]{3,2,1,0:T(8,128)(2,1)}), bf16[32,1,48,1536]{3,2,1,0:T(8,128)(2,1)}, u32[]{:S(2)}, u32[]{:S(2)}) %all-to-all-start.1) | async-done | bytes 4718624 | tf_op jit(solution)/shard_map/all_to_all | solution.py:339
  197.1 5.1 %fusion.5 = bf16[256,1536]{1,0:T(8,128)(2,1)} fusion(f32[256,1536]{1,0:T(8,128)} %copy-done.1, bf16[1536,1536]{1,0:T(8,128)(2,1)} %bitcast.20, bf16[256,1536]{1,0:T(8,128)(2,1)S(1)} %select_reduce_fusion), kind=kOutput, calls=%fused_computation.16 | convolution fusion | flops 1208745984 | bytes 7864320 | tf_op jit(solution)/shard_map/dot_general | solution.py:344
  (41 shorter events, 1.8 us)
Async XLA Ops:
  0.6 122.8 %copy-start = (bf16[1,768,1536]{2,1,0:T(8,128)(2,1)S(1)}, bf16[1,768,1536]{2,1,0:T(8,128)(2,1)}, u32[]{:S(2)}) copy-start(bf16[1,768,1536]{2,1,0:T(8,128)(2,1)} %param.21) | copy-start | bytes 7077892
  0.6 24.4 %collective-permute-start = (s32[2,16]{1,0:T(2,128)}, s32[2,16]{1,0:T(2,128)S(1)}, u32[]{:S(2)}, u32[]{:S(2)}) collective-permute-start(s32[2,16]{1,0:T(2,128)} %param.25), channel_id=1, source_target_pairs={{0,4},{4,0},{8,12},{12,8},{16,20},{20,16},{24,28},{28,24},{32,36},... | collective-permute-start | bytes 392 | tf_op jit(solution)/shard_map/ppermute | solution.py:283
  0.7 27.3 %collective-permute-start.2 = (bf16[32,128,256]{2,1,0:T(8,128)(2,1)}, bf16[32,128,256]{2,1,0:T(8,128)(2,1)}, u32[]{:S(2)}, u32[]{:S(2)}) collective-permute-start(bf16[32,128,256]{2,1,0:T(8,128)(2,1)} %k_own.1), channel_id=1, source_target_pairs={{0,4},{4,0},{8,12},{12,8},{16,20},{20,16},{24,28},{28,24},{32,36},... | collective-permute-start | bytes 6291464 | tf_op jit(solution)/shard_map/ppermute | solution.py:283
  1.2 26.8 %collective-permute-start.3 = (bf16[32,128,256]{2,1,0:T(8,128)(2,1)}, bf16[32,128,256]{2,1,0:T(8,128)(2,1)}, u32[]{:S(2)}, u32[]{:S(2)}) collective-permute-start(bf16[32,128,256]{2,1,0:T(8,128)(2,1)} %v_own.1), channel_id=1, source_target_pairs={{0,4},{4,0},{8,12},{12,8},{16,20},{20,16},{24,28},{28,24},{32,36},... | collective-permute-start | bytes 6291464 | tf_op jit(solution)/shard_map/ppermute | solution.py:283
  8.0 12.4 %copy-start.5 = (s32[256,4]{0,1:T(4,128)S(1)}, s32[256,4]{0,1:T(4,128)}, u32[]{:S(2)}) copy-start(s32[256,4]{0,1:T(4,128)} %param.22) | copy-start | bytes 12292
  14.2 10.9 %copy-start.7 = (s32[2,16]{1,0:T(2,128)S(1)}, s32[2,16]{1,0:T(2,128)}, u32[]{:S(2)}) copy-start(s32[2,16]{1,0:T(2,128)} %param.25) | copy-start | bytes 388
  17.4 10.7 %collective-permute-start.1 = (bf16[256,512]{1,0:T(8,128)(2,1)}, bf16[256,512]{1,0:T(8,128)(2,1)S(1)}, u32[]{:S(2)}, u32[]{:S(2)}) collective-permute-start(bf16[256,512]{1,0:T(8,128)(2,1)} %get-tuple-element.3.kn_ref), channel_id=1, source_target_pairs={{0,1},{2,3},{4,5},{6,7},{8,9},{10,11},{12,13},{14,15},{16,17},{18,... | collective-permute-start | bytes 786440 | tf_op jit(solution)/shard_map/ppermute | solution.py:281
  28.1 0.7 copy-start.3
  28.8 9.8 %copy-start.2 = (bf16[256,1536]{1,0:T(8,128)(2,1)S(1)}, bf16[256,1536]{1,0:T(8,128)(2,1)}, u32[]{:S(2)}) copy-start(bf16[256,1536]{1,0:T(8,128)(2,1)} %param.14) | copy-start | bytes 2359300
  38.6 4.2 %copy-start.6 = (f32[1536]{0:T(1024)S(1)}, f32[1536]{0:T(1024)}, u32[]{:S(2)}) copy-start(f32[1536]{0:T(1024)} %param.18) | copy-start | bytes 18436
  38.6 77.4 %slice-start = ((s8[4718592]{0:T(1024)(128)(4,1)}), s8[4194304]{0:T(1024)(128)(4,1)S(1)}, s32[]{:S(2)}) async-start(s8[4718592]{0:T(1024)(128)(4,1)} %bitcast.43), calls=%async_computation.2 | async-start | bytes 8388608
  42.8 1.5 copy-start.1
  42.8 73.1 %slice-start.1 = ((s8[4718592]{0:T(1024)(128)(4,1)}), s8[524288]{0:T(1024)(128)(4,1)S(1)}, s32[]{:S(2)}) async-start(s8[4718592]{0:T(1024)(128)(4,1)} %bitcast.43), calls=%async_computation.3 | async-start | bytes 1048576
  129.0 5.9 %copy-start.4 = (f32[1536,32]{0,1:T(8,128)S(1)}, f32[1536,32]{0,1:T(8,128)}, u32[]{:S(2)}) copy-start(f32[1536,32]{0,1:T(8,128)} %param.19) | copy-start | bytes 589828
  129.0 68.2 %all-to-all-start.1 = ((bf16[32,1,48,1536]{3,2,1,0:T(8,128)(2,1)}), bf16[32,1,48,1536]{3,2,1,0:T(8,128)(2,1)}, u32[]{:S(2)}, u32[]{:S(2)}) async-start(bf16[32,1,48,1536]{3,2,1,0:T(8,128)(2,1)} %convert_bitcast_fusion), calls=%async_computation.1 | async-start | bytes 9437184 | tf_op jit(solution)/shard_map/all_to_all | solution.py:339

commit v11 on v8

--- a/solution.py
+++ b/solution.py
@@ -307,15 +307,16 @@
     slot_total = expert_total * capacity
     flat_ids = routes.reshape(-1)
     route_rows = flat_ids.shape[0]
-    one_hot = (flat_ids[:, None] == jnp.arange(expert_total, dtype=jnp.int32)[None, :]).astype(
-        jnp.bfloat16
-    )
-    row_i = lax.broadcasted_iota(jnp.int32, (route_rows, route_rows), 0)
-    col_i = lax.broadcasted_iota(jnp.int32, (route_rows, route_rows), 1)
+    route_hits = routes[:, :, None] == jnp.arange(expert_total, dtype=jnp.int32)[None, None, :]
+    per_token = jnp.sum(route_hits.astype(jnp.int32), axis=1).astype(jnp.bfloat16)
+    row_i = lax.broadcasted_iota(jnp.int32, (tokens_per_device, tokens_per_device), 0)
+    col_i = lax.broadcasted_iota(jnp.int32, (tokens_per_device, tokens_per_device), 1)
     before = (col_i < row_i).astype(jnp.bfloat16)
-    earlier_counts = jnp.dot(before, one_hot, preferred_element_type=jnp.float32)
-    slot_ranks = jnp.sum(earlier_counts * one_hot.astype(jnp.float32), axis=1).astype(jnp.int32)
-    slot_ids = (flat_ids * capacity + slot_ranks).reshape(tokens_per_device, TOPK)
+    earlier_counts = jnp.dot(before, per_token, preferred_element_type=jnp.float32)
+    slot_ranks = jnp.sum(
+        jnp.where(route_hits, earlier_counts[:, None, :], 0.0), axis=2
+    ).astype(jnp.int32)
+    slot_ids = routes * capacity + slot_ranks
 
     slot_iota = jnp.arange(slot_total, dtype=jnp.int32)
     hits = slot_ids[None, :, :] == slot_iota[:, None, None]

time: 201 us -> 205 us (1.020)
  waiting for transfers between devices: 61.7 us -> 66.8 us
    ppermute x1, waiting for transfers between devices: 2.8 us -> 5.59 us  [on_device(): earlier = lax.ppermute(appended, 'head', forward_pairs)]
    all_to_all x1, waiting for transfers between devices: 58.9 us -> 61.2 us  [on_device(): lax.all_to_all(result, 'req', split_axis=0, concat_axis=0, tiled=True)]
  transfers between devices with their start and end apart: 5 -> 5, of which waited for: 2 -> 2; matrix products, arithmetic and copies ran while one was open for 10% -> 7% of each run, Pallas kernels for 2% -> 2%
where the time goes in v11:
time: 205 us; the launch traced here: 204 us
  blocking collectives  71.9 us (35%)
  waiting for transfers between devices  66.8 us (33%)
  matrix products  31 us (15%)
  Pallas kernels  11 us (5%)
  starting transfers between devices  7.67 us (4%)
  other arithmetic  7.61 us (4%)
  between operations  5.03 us (2%)
  local copies, waits for them, and re-layouts  3.35 us (2%)
    all_to_all x1, blocking collectives, on_device(): lax.all_to_all(dispatch, 'req', split_axis=0, concat_axis=0, tiled=True)  71.9 us
    all_to_all x1, waiting for transfers between devices, on_device(): lax.all_to_all(result, 'req', split_axis=0, concat_axis=0, tiled=True)  61.2 us
    pallas_call x1, Pallas kernels, attend(): pl.pallas_call(functools.partial(attention_kernel, group=group, tokens=to...  7.85 us
    dot_general x1, matrix products, on_device(): jnp.einsum('nekd,edf->nekf', lax.all_to_all(dispatch, 'req', split_axis=0...  7.52 us
    dot_general x1, matrix products, on_device(): jnp.dot(normed, query_key_value_weight, preferred_element_type=jnp.float32)  6.24 us
    all_to_all x1, starting transfers between devices, on_device(): lax.all_to_all(result, 'req', split_axis=0, concat_axis=0, tiled=True)  5.72 us
    ppermute x1, waiting for transfers between devices, on_device(): earlier = lax.ppermute(appended, 'head', forward_pairs)  5.59 us
    dot_general x1, matrix products, on_device(): jnp.einsum('nekf,efd->nekd', hidden, w_down, preferred_element_type=jnp.f...  5.55 us
  transfers between devices with their start and end apart: 5, of which 2 were waited for; matrix products, arithmetic and copies ran while one was open for 7% of the time, Pallas kernels for 2%

profile of v11, /device:TPU:56, one launch (start us, length us, event | category | flops | bytes accessed | tf_op | source)
XLA Modules:
  0.0 204.3 jit_solution(15064953994301813580)
XLA Ops:
  1.3 1.3 dynamic_slice.13
  4.4 1.3 dynamic_slice.14
  6.3 0.5 fusion.18
  6.9 0.8 pad_maximum_fusion
  7.7 1.4 fusion.9
  9.1 6.2 %fusion.12.proj_ref = f32[256,2048]{1,0:T(8,128)} fusion(bf16[1536,2048]{1,0:T(8,128)(2,1)} %param.16, bf16[256,1536]{1,0:T(8,128)(2,1)} %param.14, f32[1536]{0:T(1024)} %param.15, f32[256]{0:T(256)S(1)} %add_rsqrt_fusion.1), kind=kOutput, calls=%fused_computation.25 | convolution fusion | flops 1612185600 | bytes 9182208 | tf_op jit(solution)/shard_map/dot_general | solution.py:260
  15.3 3.1 %shard_map.149 = (bf16[256,1536]{1,0:T(8,128)(2,1)}, bf16[256,512]{1,0:T(8,128)(2,1)}) custom-call(f32[256,2048]{1,0:T(8,128)} %fusion.12.proj_ref, f32[256,128]{1,0:T(8,128)} %get-tuple-element.13.cos_ref, f32[256,128]{1,0:T(8,128)} %get-tuple-element.14.sin_ref), custom_call_target="tpu_custom_call" | custom-call | tf_op jit(solution)/shard_map/pallas_call | solution.py:67
  18.4 1.3 collective-permute-start.1
  21.7 1.2 pad_add_fusion.meta_ref
  23.0 0.6 fusion.20.page_ref
  23.5 5.6 %collective-permute-done.1.vn_ref = bf16[256,512]{1,0:T(8,128)(2,1)S(1)} collective-permute-done((bf16[256,512]{1,0:T(8,128)(2,1)}, bf16[256,512]{1,0:T(8,128)(2,1)S(1)}, u32[]{:S(2)}, u32[]{:S(2)}) %collective-permute-start.1) | collective-permute-done | bytes 262176 | tf_op jit(solution)/shard_map/ppermute | solution.py:280
  29.1 0.7 copy-done.3
  29.9 7.9 %shard_map.150 = bf16[256,1536]{1,0:T(8,128)(2,1)} custom-call(s32[3]{0:T(128)} %pad_add_fusion.meta_ref, s32[16]{0:T(128)} %fusion.20.page_ref, bf16[256,1536]{1,0:T(8,128)(2,1)} %get-tuple-element.4.q_ref, bf16[256,512]{1,0:T(8,128)(2,1)} %get-tuple-element.3.kn_ref, bf16[256,512]{1,0:T(8,128)(2,1)} %copy-done.3, bf16[32,128,256]{2,1,0:T(8,128)(2,1)} %k_own.1, ...), custom_call_target="tpu_custom_call" | custom-call | tf_op jit(solution)/shard_map/pallas_call | solution.py:201
  37.8 4.1 %multiply_reduce_fusion = (f32[256]{0:T(256)S(1)}, f32[256,1536]{1,0:T(8,128)S(1)}) fusion(bf16[256,1536]{1,0:T(8,128)(2,1)} %shard_map.150, bf16[1536,1536]{1,0:T(8,128)(2,1)} %param.17, bf16[256,1536]{1,0:T(8,128)(2,1)S(1)} %copy-done.2), kind=kOutput, calls=%fused_computation.24 | convolution fusion | flops 1209532160 | bytes 7865344 | tf_op jit(solution)/shard_map/dot_general | solution.py:294
  41.9 0.8 fusion.22
  42.8 1.8 fusion
  44.6 1.5 convolution_convert_fusion
  46.1 71.9 %all_to_all.10 = bf16[32,1,48,1536]{3,2,1,0:T(8,128)(2,1)S(1)} all-to-all(bf16[32,1,48,1536]{3,2,1,0:T(8,128)(2,1)S(1)} %bitcast.45), channel_id=1, replica_groups=mesh['req'=32,'head'=4] {'req'}, dimensions={0} | all-to-all | bytes 9437184 | tf_op jit(solution)/shard_map/all_to_all | solution.py:330
  118.0 7.5 %convolution_bitcast_fusion = f32[32,1,48,1536]{3,2,0,1:T(8,128)S(1)} fusion(bf16[1,1536,1536]{2,1,0:T(8,128)(2,1)S(1)} %bitcast.47, bf16[32,1,48,1536]{3,2,1,0:T(8,128)(2,1)S(1)} %all_to_all.10), kind=kOutput, calls=%fused_computation.5 | convolution fusion | flops 7247757312 | bytes 18874368 | tf_op jit(solution)/shard_map/nekd,edf->nekf/dot_general | solution.py:328
  125.6 5.5 %convert_bitcast_fusion = bf16[32,1,48,1536]{3,2,1,0:T(8,128)(2,1)} fusion(f32[32,1,48,1536]{3,2,0,1:T(8,128)S(1)} %convolution_bitcast_fusion, bf16[1,768,1536]{2,1,0:T(8,128)(2,1)S(1)} %copy-done), kind=kOutput, calls=%fused_computation.11 | convolution fusion | flops 3629776896 | bytes 16515072 | tf_op jit(solution)/shard_map/nekf,efd->nekd/dot_general | solution.py:335
  131.1 5.7 %all-to-all-start.1 = ((bf16[32,1,48,1536]{3,2,1,0:T(8,128)(2,1)}), bf16[32,1,48,1536]{3,2,1,0:T(8,128)(2,1)}, u32[]{:S(2)}, u32[]{:S(2)}) async-start(bf16[32,1,48,1536]{3,2,1,0:T(8,128)(2,1)} %convert_bitcast_fusion), calls=%async_computation.1 | async-start | bytes 9437184 | tf_op jit(solution)/shard_map/all_to_all | solution.py:338
  136.9 1.1 select_reduce_fusion
  138.0 61.2 %all-to-all-done.1 = bf16[32,1,48,1536]{3,2,1,0:T(8,128)(2,1)} async-done(((bf16[32,1,48,1536]{3,2,1,0:T(8,128)(2,1)}), bf16[32,1,48,1536]{3,2,1,0:T(8,128)(2,1)}, u32[]{:S(2)}, u32[]{:S(2)}) %all-to-all-start.1) | async-done | bytes 4718624 | tf_op jit(solution)/shard_map/all_to_all | solution.py:338
  199.2 5.1 %fusion.4 = bf16[256,1536]{1,0:T(8,128)(2,1)} fusion(f32[256,1536]{1,0:T(8,128)} %copy-done.1, bf16[1536,1536]{1,0:T(8,128)(2,1)} %bitcast.22, bf16[256,1536]{1,0:T(8,128)(2,1)S(1)} %select_reduce_fusion), kind=kOutput, calls=%fused_computation.14 | convolution fusion | flops 1208745984 | bytes 7864320 | tf_op jit(solution)/shard_map/dot_general | solution.py:343
  (36 shorter events, 1.0 us)
Async XLA Ops:
  0.6 124.9 %copy-start = (bf16[1,768,1536]{2,1,0:T(8,128)(2,1)S(1)}, bf16[1,768,1536]{2,1,0:T(8,128)(2,1)}, u32[]{:S(2)}) copy-start(bf16[1,768,1536]{2,1,0:T(8,128)(2,1)} %param.21) | copy-start | bytes 7077892
  0.6 22.3 %collective-permute-start = (s32[2,16]{1,0:T(2,128)}, s32[2,16]{1,0:T(2,128)S(1)}, u32[]{:S(2)}, u32[]{:S(2)}) collective-permute-start(s32[2,16]{1,0:T(2,128)} %param.25), channel_id=1, source_target_pairs={{0,4},{4,0},{8,12},{12,8},{16,20},{20,16},{24,28},{28,24},{32,36},... | collective-permute-start | bytes 392 | tf_op jit(solution)/shard_map/ppermute | solution.py:282
  0.7 28.4 %collective-permute-start.2 = (bf16[32,128,256]{2,1,0:T(8,128)(2,1)}, bf16[32,128,256]{2,1,0:T(8,128)(2,1)}, u32[]{:S(2)}, u32[]{:S(2)}) collective-permute-start(bf16[32,128,256]{2,1,0:T(8,128)(2,1)} %k_own.1), channel_id=1, source_target_pairs={{0,4},{4,0},{8,12},{12,8},{16,20},{20,16},{24,28},{28,24},{32,36},... | collective-permute-start | bytes 6291464 | tf_op jit(solution)/shard_map/ppermute | solution.py:282
  1.2 27.9 %collective-permute-start.3 = (bf16[32,128,256]{2,1,0:T(8,128)(2,1)}, bf16[32,128,256]{2,1,0:T(8,128)(2,1)}, u32[]{:S(2)}, u32[]{:S(2)}) collective-permute-start(bf16[32,128,256]{2,1,0:T(8,128)(2,1)} %v_own.1), channel_id=1, source_target_pairs={{0,4},{4,0},{8,12},{12,8},{16,20},{20,16},{24,28},{28,24},{32,36},... | collective-permute-start | bytes 6291464 | tf_op jit(solution)/shard_map/ppermute | solution.py:282
  9.1 10.7 %copy-start.5 = (s32[256,4]{0,1:T(4,128)S(1)}, s32[256,4]{0,1:T(4,128)}, u32[]{:S(2)}) copy-start(s32[256,4]{0,1:T(4,128)} %param.22) | copy-start | bytes 12292
  9.1 13.9 %copy-start.7 = (s32[2,16]{1,0:T(2,128)S(1)}, s32[2,16]{1,0:T(2,128)}, u32[]{:S(2)}) copy-start(s32[2,16]{1,0:T(2,128)} %param.25) | copy-start | bytes 388
  18.4 10.7 %collective-permute-start.1 = (bf16[256,512]{1,0:T(8,128)(2,1)}, bf16[256,512]{1,0:T(8,128)(2,1)S(1)}, u32[]{:S(2)}, u32[]{:S(2)}) collective-permute-start(bf16[256,512]{1,0:T(8,128)(2,1)} %get-tuple-element.3.kn_ref), channel_id=1, source_target_pairs={{0,1},{2,3},{4,5},{6,7},{8,9},{10,11},{12,13},{14,15},{16,17},{18,... | collective-permute-start | bytes 786440 | tf_op jit(solution)/shard_map/ppermute | solution.py:280
  29.1 0.7 copy-start.3
  29.9 7.9 %copy-start.2 = (bf16[256,1536]{1,0:T(8,128)(2,1)S(1)}, bf16[256,1536]{1,0:T(8,128)(2,1)}, u32[]{:S(2)}) copy-start(bf16[256,1536]{1,0:T(8,128)(2,1)} %param.14) | copy-start | bytes 2359300
  37.7 4.1 %copy-start.4 = (f32[1536,32]{0,1:T(8,128)S(1)}, f32[1536,32]{0,1:T(8,128)}, u32[]{:S(2)}) copy-start(f32[1536,32]{0,1:T(8,128)} %param.19) | copy-start | bytes 589828
  37.7 4.1 %copy-start.6 = (f32[1536]{0:T(1024)S(1)}, f32[1536]{0:T(1024)}, u32[]{:S(2)}) copy-start(f32[1536]{0:T(1024)} %param.18) | copy-start | bytes 18436
  41.8 4.3 %copy-start.1 = (f32[256,1536]{1,0:T(8,128)}, f32[256,1536]{1,0:T(8,128)S(1)}, u32[]{:S(2)}) copy-start(f32[256,1536]{1,0:T(8,128)S(1)} %get-tuple-element.12) | copy-start | bytes 4718596
  41.9 76.2 %slice-start = ((s8[4718592]{0:T(1024)(128)(4,1)}), s8[4194304]{0:T(1024)(128)(4,1)S(1)}, s32[]{:S(2)}) async-start(s8[4718592]{0:T(1024)(128)(4,1)} %bitcast.46), calls=%async_computation.2 | async-start | bytes 8388608
  44.6 73.4 %slice-start.1 = ((s8[4718592]{0:T(1024)(128)(4,1)}), s8[524288]{0:T(1024)(128)(4,1)S(1)}, s32[]{:S(2)}) async-start(s8[4718592]{0:T(1024)(128)(4,1)} %bitcast.46), calls=%async_computation.3 | async-start | bytes 1048576
  131.1 68.1 %all-to-all-start.1 = ((bf16[32,1,48,1536]{3,2,1,0:T(8,128)(2,1)}), bf16[32,1,48,1536]{3,2,1,0:T(8,128)(2,1)}, u32[]{:S(2)}, u32[]{:S(2)}) async-start(bf16[32,1,48,1536]{3,2,1,0:T(8,128)(2,1)} %convert_bitcast_fusion), calls=%async_computation.1 | async-start | bytes 9437184 | tf_op jit(solution)/shard_map/all_to_all | solution.py:338

commit v12 on v10

--- a/solution.py
+++ b/solution.py
@@ -309,15 +309,16 @@
     slot_total = expert_total * capacity
     flat_ids = routes.reshape(-1)
     route_rows = flat_ids.shape[0]
-    one_hot = (flat_ids[:, None] == jnp.arange(expert_total, dtype=jnp.int32)[None, :]).astype(
-        jnp.bfloat16
-    )
-    row_i = lax.broadcasted_iota(jnp.int32, (route_rows, route_rows), 0)
-    col_i = lax.broadcasted_iota(jnp.int32, (route_rows, route_rows), 1)
+    route_hits = routes[:, :, None] == jnp.arange(expert_total, dtype=jnp.int32)[None, None, :]
+    per_token = jnp.sum(route_hits.astype(jnp.int32), axis=1).astype(jnp.bfloat16)
+    row_i = lax.broadcasted_iota(jnp.int32, (tokens_per_device, tokens_per_device), 0)
+    col_i = lax.broadcasted_iota(jnp.int32, (tokens_per_device, tokens_per_device), 1)
     before = (col_i < row_i).astype(jnp.bfloat16)
-    earlier_counts = jnp.dot(before, one_hot, preferred_element_type=jnp.float32)
-    slot_ranks = jnp.sum(earlier_counts * one_hot.astype(jnp.float32), axis=1).astype(jnp.int32)
-    slot_ids = (flat_ids * capacity + slot_ranks).reshape(tokens_per_device, TOPK)
+    earlier_counts = jnp.dot(before, per_token, preferred_element_type=jnp.float32)
+    slot_ranks = jnp.sum(
+        jnp.where(route_hits, earlier_counts[:, None, :], 0.0), axis=2
+    ).astype(jnp.int32)
+    slot_ids = routes * capacity + slot_ranks
 
     slot_iota = jnp.arange(slot_total, dtype=jnp.int32)
     hits = slot_ids[None, :, :] == slot_iota[:, None, None]

time: 202 us -> 205 us (1.015)
  waiting for transfers between devices: 61.2 us -> 66.1 us
  Pallas kernels: 12.9 us -> 9.62 us
    pallas_call x1, Pallas kernels: 9.75 us -> 6.51 us  [attend(): pl.pallas_call(functools.partial(attention_kernel, group=group, tokens=to...]
    ppermute x1, waiting for transfers between devices: 2.32 us -> 4.92 us  [on_device(): earlier = lax.ppermute(appended, 'head', forward_pairs)]
    all_to_all x1, waiting for transfers between devices: 58.8 us -> 61.2 us  [on_device(): lax.all_to_all(result, 'req', split_axis=0, concat_axis=0, tiled=True)]
  transfers between devices with their start and end apart: 5 -> 5, of which waited for: 2 -> 2; matrix products, arithmetic and copies ran while one was open for 10% -> 8% of each run, Pallas kernels for 2% -> 2%
where the time goes in v12:
time: 205 us; the launch traced here: 203 us
  blocking collectives  73.5 us (36%)
  waiting for transfers between devices  66.1 us (32%)
  matrix products  31 us (15%)
  other arithmetic  10.9 us (5%)
  Pallas kernels  9.62 us (5%)
  starting transfers between devices  7.68 us (4%)
  between operations  3.88 us (2%)
    all_to_all x1, blocking collectives, on_device(): lax.all_to_all(dispatch, 'req', split_axis=0, concat_axis=0, tiled=True)  73.5 us
    all_to_all x1, waiting for transfers between devices, on_device(): lax.all_to_all(result, 'req', split_axis=0, concat_axis=0, tiled=True)  61.2 us
    dot_general x1, matrix products, on_device(): jnp.einsum('nekd,edf->nekf', lax.all_to_all(dispatch, 'req', split_axis=0...  7.51 us
    pallas_call x1, Pallas kernels, attend(): pl.pallas_call(functools.partial(attention_kernel, group=group, tokens=to...  6.51 us
    dot_general x1, matrix products, on_device(): jnp.dot(normed, query_key_value_weight, preferred_element_type=jnp.float32)  6.24 us
    all_to_all x1, starting transfers between devices, on_device(): lax.all_to_all(result, 'req', split_axis=0, concat_axis=0, tiled=True)  5.72 us
    dot_general x1, matrix products, on_device(): jnp.einsum('nekf,efd->nekd', hidden, w_down, preferred_element_type=jnp.f...  5.48 us
    dot_general x1, matrix products, on_device(): jnp.dot(combine.astype(jnp.bfloat16), flat_results, preferred_element_typ...  5.12 us
  transfers between devices with their start and end apart: 5, of which 2 were waited for; matrix products, arithmetic and copies ran while one was open for 8% of the time, Pallas kernels for 2%

profile of v12, /device:TPU:56, one launch (start us, length us, event | category | flops | bytes accessed | tf_op | source)
XLA Modules:
  0.0 203.5 jit_solution(2399954886977720189)
XLA Ops:
  1.3 1.3 fusion.20
  2.7 1.9 fusion.21
  5.2 0.5 fusion.18
  5.8 0.8 pad_maximum_fusion
  6.6 1.4 fusion.9
  8.0 6.2 %fusion.12.proj_ref = f32[256,2048]{1,0:T(8,128)} fusion(bf16[1536,2048]{1,0:T(8,128)(2,1)} %param.16, bf16[256,1536]{1,0:T(8,128)(2,1)} %param.14, f32[1536]{0:T(1024)} %param.15, f32[256]{0:T(256)S(1)} %add_rsqrt_fusion.1), kind=kOutput, calls=%fused_computation.25 | convolution fusion | flops 1612185600 | bytes 9182208 | tf_op jit(solution)/shard_map/dot_general | solution.py:261
  14.3 3.1 %shard_map.149 = (bf16[256,1536]{1,0:T(8,128)(2,1)}, bf16[256,512]{1,0:T(8,128)(2,1)}) custom-call(f32[256,2048]{1,0:T(8,128)} %fusion.12.proj_ref, f32[256,128]{1,0:T(8,128)} %get-tuple-element.13.cos_ref, f32[256,128]{1,0:T(8,128)} %get-tuple-element.14.sin_ref), custom_call_target="tpu_custom_call" | custom-call | tf_op jit(solution)/shard_map/pallas_call | solution.py:67
  17.4 1.3 collective-permute-start.1
  21.3 1.2 pad_add_fusion.meta_ref
  22.5 0.7 select_reduce_fusion.3.page_ref
  23.2 4.9 %collective-permute-done.1.vn_ref = bf16[256,512]{1,0:T(8,128)(2,1)S(1)} collective-permute-done((bf16[256,512]{1,0:T(8,128)(2,1)}, bf16[256,512]{1,0:T(8,128)(2,1)S(1)}, u32[]{:S(2)}, u32[]{:S(2)}) %collective-permute-start.1) | collective-permute-done | bytes 262176 | tf_op jit(solution)/shard_map/ppermute | solution.py:281
  28.1 0.7 copy-done.3
  28.8 6.5 %shard_map.150 = bf16[256,1536]{1,0:T(8,128)(2,1)} custom-call(s32[3]{0:T(128)} %pad_add_fusion.meta_ref, s32[16]{0:T(128)} %select_reduce_fusion.3.page_ref, bf16[256,1536]{1,0:T(8,128)(2,1)} %get-tuple-element.4.q_ref, bf16[256,512]{1,0:T(8,128)(2,1)} %get-tuple-element.3.kn_ref, bf16[256,512]{1,0:T(8,128)(2,1)} %copy-done.3, bf16[32,128,256]{2,1,0:T(8,128)(2,1)} %k_own.1, ...), custom_call_target="tpu_custom_call" | custom-call | tf_op jit(solution)/shard_map/pallas_call | solution.py:200
  35.3 4.1 %multiply_reduce_fusion = (f32[256]{0:T(256)S(1)}, f32[256,1536]{1,0:T(8,128)S(1)}) fusion(bf16[256,1536]{1,0:T(8,128)(2,1)} %shard_map.150, bf16[1536,1536]{1,0:T(8,128)(2,1)} %param.17, bf16[256,1536]{1,0:T(8,128)(2,1)S(1)} %copy-done.2), kind=kOutput, calls=%fused_computation.24 | convolution fusion | flops 1209532160 | bytes 7865344 | tf_op jit(solution)/shard_map/dot_general | solution.py:296
  39.5 0.8 fusion.23
  40.4 1.8 fusion
  42.2 1.5 convolution_convert_fusion
  43.7 73.5 %all_to_all.10 = bf16[32,1,48,1536]{3,2,1,0:T(8,128)(2,1)S(1)} all-to-all(bf16[32,1,48,1536]{3,2,1,0:T(8,128)(2,1)S(1)} %bitcast.42), channel_id=1, replica_groups=mesh['req'=32,'head'=4] {'req'}, dimensions={0} | all-to-all | bytes 9437184 | tf_op jit(solution)/shard_map/all_to_all | solution.py:332
  117.3 7.5 %convolution_bitcast_fusion = f32[32,1,48,1536]{3,2,0,1:T(8,128)S(1)} fusion(bf16[1,1536,1536]{2,1,0:T(8,128)(2,1)S(1)} %bitcast.44, bf16[32,1,48,1536]{3,2,1,0:T(8,128)(2,1)S(1)} %all_to_all.10), kind=kOutput, calls=%fused_computation.5 | convolution fusion | flops 7247757312 | bytes 18874368 | tf_op jit(solution)/shard_map/nekd,edf->nekf/dot_general | solution.py:330
  124.8 5.5 %convert_bitcast_fusion = bf16[32,1,48,1536]{3,2,1,0:T(8,128)(2,1)} fusion(f32[32,1,48,1536]{3,2,0,1:T(8,128)S(1)} %convolution_bitcast_fusion, bf16[1,768,1536]{2,1,0:T(8,128)(2,1)S(1)} %copy-done), kind=kOutput, calls=%fused_computation.11 | convolution fusion | flops 3629776896 | bytes 16515072 | tf_op jit(solution)/shard_map/nekf,efd->nekd/dot_general | solution.py:337
  130.3 5.7 %all-to-all-start.1 = ((bf16[32,1,48,1536]{3,2,1,0:T(8,128)(2,1)}), bf16[32,1,48,1536]{3,2,1,0:T(8,128)(2,1)}, u32[]{:S(2)}, u32[]{:S(2)}) async-start(bf16[32,1,48,1536]{3,2,1,0:T(8,128)(2,1)} %convert_bitcast_fusion), calls=%async_computation.1 | async-start | bytes 9437184 | tf_op jit(solution)/shard_map/all_to_all | solution.py:340
  136.1 1.1 select_reduce_fusion
  137.2 61.2 %all-to-all-done.1 = bf16[32,1,48,1536]{3,2,1,0:T(8,128)(2,1)} async-done(((bf16[32,1,48,1536]{3,2,1,0:T(8,128)(2,1)}), bf16[32,1,48,1536]{3,2,1,0:T(8,128)(2,1)}, u32[]{:S(2)}, u32[]{:S(2)}) %all-to-all-start.1) | async-done | bytes 4718624 | tf_op jit(solution)/shard_map/all_to_all | solution.py:340
  198.4 5.1 %fusion.4 = bf16[256,1536]{1,0:T(8,128)(2,1)} fusion(f32[256,1536]{1,0:T(8,128)} %copy-done.1, bf16[1536,1536]{1,0:T(8,128)(2,1)} %bitcast.20, bf16[256,1536]{1,0:T(8,128)(2,1)S(1)} %select_reduce_fusion), kind=kOutput, calls=%fused_computation.14 | convolution fusion | flops 1208745984 | bytes 7864320 | tf_op jit(solution)/shard_map/dot_general | solution.py:345
  (37 shorter events, 1.1 us)
Async XLA Ops:
  0.6 124.2 %copy-start = (bf16[1,768,1536]{2,1,0:T(8,128)(2,1)S(1)}, bf16[1,768,1536]{2,1,0:T(8,128)(2,1)}, u32[]{:S(2)}) copy-start(bf16[1,768,1536]{2,1,0:T(8,128)(2,1)} %param.21) | copy-start | bytes 7077892
  0.6 21.8 %collective-permute-start = (s32[2,16]{1,0:T(2,128)}, s32[2,16]{1,0:T(2,128)S(1)}, u32[]{:S(2)}, u32[]{:S(2)}) collective-permute-start(s32[2,16]{1,0:T(2,128)} %param.25), channel_id=1, source_target_pairs={{0,4},{4,0},{8,12},{12,8},{16,20},{20,16},{24,28},{28,24},{32,36},... | collective-permute-start | bytes 392 | tf_op jit(solution)/shard_map/ppermute | solution.py:283
  0.7 27.3 %collective-permute-start.2 = (bf16[32,128,256]{2,1,0:T(8,128)(2,1)}, bf16[32,128,256]{2,1,0:T(8,128)(2,1)}, u32[]{:S(2)}, u32[]{:S(2)}) collective-permute-start(bf16[32,128,256]{2,1,0:T(8,128)(2,1)} %k_own.1), channel_id=1, source_target_pairs={{0,4},{4,0},{8,12},{12,8},{16,20},{20,16},{24,28},{28,24},{32,36},... | collective-permute-start | bytes 6291464 | tf_op jit(solution)/shard_map/ppermute | solution.py:283
  1.2 26.8 %collective-permute-start.3 = (bf16[32,128,256]{2,1,0:T(8,128)(2,1)}, bf16[32,128,256]{2,1,0:T(8,128)(2,1)}, u32[]{:S(2)}, u32[]{:S(2)}) collective-permute-start(bf16[32,128,256]{2,1,0:T(8,128)(2,1)} %v_own.1), channel_id=1, source_target_pairs={{0,4},{4,0},{8,12},{12,8},{16,20},{20,16},{24,28},{28,24},{32,36},... | collective-permute-start | bytes 6291464 | tf_op jit(solution)/shard_map/ppermute | solution.py:283
  8.0 12.4 %copy-start.5 = (s32[256,4]{0,1:T(4,128)S(1)}, s32[256,4]{0,1:T(4,128)}, u32[]{:S(2)}) copy-start(s32[256,4]{0,1:T(4,128)} %param.22) | copy-start | bytes 12292
  8.0 14.5 %copy-start.7 = (s32[2,16]{1,0:T(2,128)S(1)}, s32[2,16]{1,0:T(2,128)}, u32[]{:S(2)}) copy-start(s32[2,16]{1,0:T(2,128)} %param.25) | copy-start | bytes 388
  17.4 10.7 %collective-permute-start.1 = (bf16[256,512]{1,0:T(8,128)(2,1)}, bf16[256,512]{1,0:T(8,128)(2,1)S(1)}, u32[]{:S(2)}, u32[]{:S(2)}) collective-permute-start(bf16[256,512]{1,0:T(8,128)(2,1)} %get-tuple-element.3.kn_ref), channel_id=1, source_target_pairs={{0,1},{2,3},{4,5},{6,7},{8,9},{10,11},{12,13},{14,15},{16,17},{18,... | collective-permute-start | bytes 786440 | tf_op jit(solution)/shard_map/ppermute | solution.py:281
  28.1 0.7 copy-start.3
  28.8 6.5 %copy-start.2 = (bf16[256,1536]{1,0:T(8,128)(2,1)S(1)}, bf16[256,1536]{1,0:T(8,128)(2,1)}, u32[]{:S(2)}) copy-start(bf16[256,1536]{1,0:T(8,128)(2,1)} %param.14) | copy-start | bytes 2359300
  35.3 4.1 %copy-start.4 = (f32[1536,32]{0,1:T(8,128)S(1)}, f32[1536,32]{0,1:T(8,128)}, u32[]{:S(2)}) copy-start(f32[1536,32]{0,1:T(8,128)} %param.19) | copy-start | bytes 589828
  35.3 4.1 %copy-start.6 = (f32[1536]{0:T(1024)S(1)}, f32[1536]{0:T(1024)}, u32[]{:S(2)}) copy-start(f32[1536]{0:T(1024)} %param.18) | copy-start | bytes 18436
  39.4 4.3 %copy-start.1 = (f32[256,1536]{1,0:T(8,128)}, f32[256,1536]{1,0:T(8,128)S(1)}, u32[]{:S(2)}) copy-start(f32[256,1536]{1,0:T(8,128)S(1)} %get-tuple-element.12) | copy-start | bytes 4718596
  39.5 77.8 %slice-start = ((s8[4718592]{0:T(1024)(128)(4,1)}), s8[4194304]{0:T(1024)(128)(4,1)S(1)}, s32[]{:S(2)}) async-start(s8[4718592]{0:T(1024)(128)(4,1)} %bitcast.43), calls=%async_computation.2 | async-start | bytes 8388608
  42.2 75.1 %slice-start.1 = ((s8[4718592]{0:T(1024)(128)(4,1)}), s8[524288]{0:T(1024)(128)(4,1)S(1)}, s32[]{:S(2)}) async-start(s8[4718592]{0:T(1024)(128)(4,1)} %bitcast.43), calls=%async_computation.3 | async-start | bytes 1048576
  130.3 68.1 %all-to-all-start.1 = ((bf16[32,1,48,1536]{3,2,1,0:T(8,128)(2,1)}), bf16[32,1,48,1536]{3,2,1,0:T(8,128)(2,1)}, u32[]{:S(2)}, u32[]{:S(2)}) async-start(bf16[32,1,48,1536]{3,2,1,0:T(8,128)(2,1)} %convert_bitcast_fusion), calls=%async_computation.1 | async-start | bytes 9437184 | tf_op jit(solution)/shard_map/all_to_all | solution.py:340
